TPU v7x, 128 devices: a whole 4x4x4 slice. The times are simulated.
128 devices in a mesh: heads: 8 (over y, core), seq: 16 (over z, x).
Axes of the slice: x: 4, y: 4, z: 4, core: 2. Of those that a mesh axis runs over, the one named last changes fastest.
Arguments:
- queries: bfloat16 [8192, 32768], P(('heads', 'seq')), may hold values from -84 to 84
- keys: bfloat16 [8192, 32768], P(('heads', 'seq')), may hold values from -6 to 6
- values: bfloat16 [8192, 32768], P(('heads', 'seq')), may hold values from -12 to 12
- feat_q: bfloat16 [64, 128, 64], P('heads'), may hold values from -3 to 3
- feat_k: bfloat16 [64, 128, 64], P('heads'), may hold values from -3 to 3
- mix: float32 [64], P('heads'), may hold values from -2 to 2
Outputs:
- attended: bfloat16 [32768, 8192], P('seq', 'heads')
All inputs are finite; a program needn't handle non-finite values.
Results may differ from a plain program's by a relative error of at most 0.0054.
Values may be sent and summed in bfloat16 or wider, within the bound.
No kernel may reach another device: no remote copies, remote signals or barrier semaphores. Data moves between devices by JAX's collectives and lax.ppermute only.
A program may use at most 128 MiB of HBM per device.

v0:
```python
import jax
import jax.numpy as jnp
from jax import lax
from jax.sharding import PartitionSpec as P

WIN = 64
BLOCK = 512


def passed_along(block, axis, distance):
    devices = range(lax.axis_size(axis))
    route = [(i - distance, i) for i in devices if i - distance in devices]
    return lax.ppermute(block, axis, route)


def entering(value, axis, join, neutral):
    place = lax.axis_index(axis)
    gathered = jax.tree.map(
        lambda a, kind: lax.all_gather(a.astype(kind), axis), value, (jnp.bfloat16, jnp.bfloat16)
    )
    state = jax.tree.map(lambda a, e: jnp.zeros_like(a) + jnp.asarray(e, a.dtype), value, neutral)

    def one(step, state):
        return join(
            state,
            jax.tree.map(
                lambda a, own: lax.dynamic_index_in_dim(a, step, 0, False).astype(own.dtype),
                gathered,
                value,
            ),
        )

    return lax.fori_loop(0, place, one, state)


def feature_map(rows, weight):
    logits = jnp.einsum("rhd,hdf->hrf", rows, weight, preferred_element_type=jnp.float32)
    halves = [jax.nn.softmax(logits, axis=-1), jax.nn.softmax(-logits, axis=-1)]
    return jnp.concatenate(halves, axis=-1).astype(jnp.bfloat16)


def add_states(earlier, later):
    return (earlier[0] + later[0], earlier[1] + later[1])


def token_major(features, group, head_dim):
    count = features.shape[-1]
    return features.reshape(group, head_dim, count).transpose(2, 0, 1)


def attend_blocks(
    queries, phi_queries, keys_ext, values_ext, phi_keys, state, normer, gate, earlier, block
):
    count = queries.shape[0] // block
    head_dim = queries.shape[2]
    query_ids = jnp.arange(block)[:, None]
    window_ids = jnp.arange(block + WIN)[None, :]
    linear_ids = jnp.arange(block)[None, :]

    def advance(carry, index):
        states, norms = carry
        start = index * block
        query_rows = lax.dynamic_slice_in_dim(queries, start, block, 0)
        phi_rows = lax.dynamic_slice_in_dim(phi_queries, start, block, 1)
        window_keys = lax.dynamic_slice_in_dim(keys_ext, start, block + WIN, 0)
        window_values = lax.dynamic_slice_in_dim(values_ext, start, block + WIN, 0)
        phi_block = lax.dynamic_slice_in_dim(phi_keys, start, block, 1)
        value_block = lax.dynamic_slice_in_dim(values_ext, start, block, 0)
        keep = (window_ids > query_ids) & (window_ids <= query_ids + WIN)
        keep = keep & jnp.logical_or(start + window_ids >= WIN, earlier)
        scores = jnp.einsum(
            "qhd,khd->hqk", query_rows, window_keys, preferred_element_type=jnp.float32
        )
        scores = scores / jnp.sqrt(jnp.float32(head_dim))
        scores = jnp.where(keep[None], scores, jnp.float32(-1e30))
        top = jnp.max(scores, axis=-1, keepdims=True)
        probs = jnp.exp(scores - top)
        total = jnp.sum(probs, axis=-1)
        rounded = probs.astype(jnp.bfloat16)
        window = jnp.einsum(
            "hqk,khd->qhd", rounded, window_values, preferred_element_type=jnp.float32
        )
        window = window / total.T[:, :, None]
        affinity = jnp.einsum(
            "hqf,hkf->hqk", phi_rows, phi_block, preferred_element_type=jnp.float32
        )
        affinity = jnp.where((linear_ids <= query_ids)[None], affinity, jnp.float32(0.0)).astype(
            jnp.bfloat16
        )
        inner_num = jnp.einsum(
            "hqk,khd->qhd", affinity, value_block, preferred_element_type=jnp.float32
        )
        inner_den = jnp.sum(affinity, axis=-1, dtype=jnp.float32)
        phi_wide = phi_rows.astype(jnp.float32)
        cross_num = jnp.einsum("hqf,hfd->qhd", phi_wide, states, precision=lax.Precision.HIGHEST)
        cross_den = jnp.einsum("hqf,hf->hq", phi_wide, norms, precision=lax.Precision.HIGHEST)
        linear = (cross_num + inner_num) / (cross_den + inner_den + 1.0).T[:, :, None]
        mixed = gate[None, :, None] * window + (1.0 - gate)[None, :, None] * linear
        mixed = mixed.astype(jnp.bfloat16).reshape(block, -1)
        states = states + jnp.einsum(
            "hkf,khd->hfd", phi_block, value_block, preferred_element_type=jnp.float32
        )
        norms = norms + jnp.sum(phi_block, axis=1, dtype=jnp.float32)
        return ((states, norms), mixed)

    steps = jnp.arange(count, dtype=jnp.int32)
    _, outputs = lax.scan(advance, (state, normer), steps)
    return outputs.reshape(count * block, -1)


def body(queries, keys, values, feat_q, feat_k, mix):
    shards = lax.axis_size("seq")
    place = lax.axis_index("seq")
    feature_rows = queries.shape[0]
    length = queries.shape[1] // shards
    group = feat_q.shape[0]
    head_dim = feat_q.shape[1]
    moved = (
        lax.all_to_all(
            queries.reshape(feature_rows, shards, length),
            "seq",
            split_axis=1,
            concat_axis=0,
            tiled=True,
        ),
        lax.all_to_all(
            keys.reshape(feature_rows, shards, length),
            "seq",
            split_axis=1,
            concat_axis=0,
            tiled=True,
        ),
        lax.all_to_all(
            values.reshape(feature_rows, shards, length),
            "seq",
            split_axis=1,
            concat_axis=0,
            tiled=True,
        ),
    )
    local_queries = token_major(moved[0], group, head_dim)
    local_keys = token_major(moved[1], group, head_dim)
    local_values = token_major(moved[2], group, head_dim)
    tails = jnp.stack([local_keys[length - WIN :], local_values[length - WIN :]])
    before = passed_along(tails, "seq", 1)
    keys_ext = jnp.concatenate([before[0], local_keys], axis=0)
    values_ext = jnp.concatenate([before[1], local_values], axis=0)
    earlier = place > 0
    keep = jnp.logical_or(jnp.arange(length + WIN) >= WIN, earlier).astype(jnp.bfloat16)
    phi_queries = feature_map(local_queries, feat_q)
    phi_keys = feature_map(keys_ext, feat_k) * keep[None, :, None]
    own_state = jnp.einsum(
        "hrf,rhd->hfd", phi_keys[:, WIN:], values_ext[WIN:], preferred_element_type=jnp.float32
    )
    own_norm = jnp.sum(phi_keys[:, WIN:], axis=1, dtype=jnp.float32)
    empty_state = jnp.zeros_like(own_state)
    empty_norm = jnp.zeros_like(own_norm)
    prior_state, prior_norm = entering(
        (own_state, own_norm), "seq", add_states, (empty_state, empty_norm)
    )
    halo_state = jnp.einsum(
        "hrf,rhd->hfd", phi_keys[:, :WIN], values_ext[:WIN], preferred_element_type=jnp.float32
    )
    halo_norm = jnp.sum(phi_keys[:, :WIN], axis=1, dtype=jnp.float32)
    gate = jax.nn.sigmoid(mix)
    return attend_blocks(
        local_queries,
        phi_queries,
        keys_ext,
        values_ext,
        phi_keys,
        prior_state - halo_state,
        prior_norm - halo_norm,
        gate,
        earlier,
        BLOCK,
    )


def solution(mesh):
    return jax.shard_map(
        body,
        mesh=mesh,
        in_specs=(
            P(("heads", "seq"), None),
            P(("heads", "seq"), None),
            P(("heads", "seq"), None),
            P("heads", None, None),
            P("heads", None, None),
            P("heads"),
        ),
        out_specs=P("seq", "heads"),
        check_vma=False,
    )
```

profile of v0, /device:TPU:116, one launch (start us, length us, event | category | flops | bytes accessed | tf_op | source)
XLA Modules:
  0.0 427.5 jit_solution(13444663231772661010)
XLA Ops:
  6.5 4.8 %copy.70 = bf16[8,16,8,2048]{3,2,0,1:T(8,128)(2,1)} copy(bf16[8,16,8,2048]{3,2,1,0:T(8,128)(2,1)} %bitcast.144) | data formatting | bytes 8388608 | tf_op jit(solution)/shard_map/reshape | solution.py:127
  11.4 6.9 %all-to-all-start = ((bf16[64,16,2048]{2,0,1:T(8,128)(2,1)}), bf16[64,16,2048]{2,0,1:T(8,128)(2,1)}, u32[]{:S(2)}, u32[]{:S(2)}) async-start(bf16[64,16,2048]{2,0,1:T(8,128)(2,1)} %bitcast.143), calls=%async_computation | async-start | bytes 8388608 | tf_op jit(solution)/shard_map/all_to_all | solution.py:126
  18.3 4.7 %copy.69 = bf16[8,16,8,2048]{3,2,0,1:T(8,128)(2,1)} copy(bf16[8,16,8,2048]{3,2,1,0:T(8,128)(2,1)} %bitcast.145) | data formatting | bytes 8388608 | tf_op jit(solution)/shard_map/reshape | solution.py:134
  23.0 52.6 %all-to-all-done = bf16[64,16,2048]{2,0,1:T(8,128)(2,1)} async-done(((bf16[64,16,2048]{2,0,1:T(8,128)(2,1)}), bf16[64,16,2048]{2,0,1:T(8,128)(2,1)}, u32[]{:S(2)}, u32[]{:S(2)}) %all-to-all-start) | async-done | bytes 4194336 | tf_op jit(solution)/shard_map/all_to_all | solution.py:126
  75.6 10.7 %all-to-all-start.1 = ((bf16[64,16,2048]{2,0,1:T(8,128)(2,1)}), bf16[64,16,2048]{2,0,1:T(8,128)(2,1)}, u32[]{:S(2)}, u32[]{:S(2)}) async-start(bf16[64,16,2048]{2,0,1:T(8,128)(2,1)} %bitcast.141), calls=%async_computation.1 | async-start | bytes 8388608 | tf_op jit(solution)/shard_map/all_to_all | solution.py:133
  86.3 6.4 %copy.42 = bf16[8,128,2048]{1,2,0:T(8,128)(2,1)} copy(bf16[8,128,2048]{2,1,0:T(8,128)(2,1)} %bitcast.4) | data formatting | bytes 8388608 | tf_op jit(solution)/shard_map/reshape | solution.py:48
  92.8 48.0 %all-to-all-done.1 = bf16[64,16,2048]{2,0,1:T(8,128)(2,1)} async-done(((bf16[64,16,2048]{2,0,1:T(8,128)(2,1)}), bf16[64,16,2048]{2,0,1:T(8,128)(2,1)}, u32[]{:S(2)}, u32[]{:S(2)}) %all-to-all-start.1) | async-done | bytes 4194336 | tf_op jit(solution)/shard_map/all_to_all | solution.py:133
  140.8 6.4 %copy.44 = bf16[8,128,2048]{1,2,0:T(8,128)(2,1)} copy(bf16[8,128,2048]{2,1,0:T(8,128)(2,1)} %bitcast.9) | data formatting | bytes 8388608 | tf_op jit(solution)/shard_map/reshape | solution.py:48
  148.3 4.6 %collective-permute-start = (bf16[2,64,8,128]{3,1,2,0:T(8,128)(2,1)S(1)}, bf16[2,64,8,128]{3,1,2,0:T(8,128)(2,1)S(1)}, u32[]{:S(2)}, u32[]{:S(2)}) collective-permute-start(bf16[2,64,8,128]{3,1,2,0:T(8,128)(2,1)S(1)} %pad_maximum_fusion.3), channel_id=1, source_target_pairs={{0,1},{1,2},{2,3},{3,4},{4,5},{5,6},{6,7},{7,8},{8,9},{9,10},{10,1... | collective-permute-start | bytes 786440 | tf_op jit(solution)/shard_map/ppermute | solution.py:13
  152.9 3.8 collective-permute-done
  156.8 5.8 %fusion.79 = (f32[8,2112]{1,0:T(8,128)S(1)}, f32[8,2112,64]{1,2,0:T(8,128)}) fusion(bf16[8,128,64]{1,2,0:T(8,128)(2,1)S(1)} %copy-done, bf16[2048,8,128]{2,0,1:T(8,128)(2,1)} %bitcast.136, bf16[64,8,128]{2,0,1:T(8,128)(2,1)S(1)} %get-tuple-element.279), kind=kOutput, calls=%fused_computation.112 | convolution fusion | flops 288718912 | bytes 8849408 | tf_op jit(solution)/shard_map/sub | solution.py:38
  162.6 5.8 %fusion.80 = (f32[8,2112]{1,0:T(8,128)S(1)}, f32[8,2112,64]{1,2,0:T(8,128)}) fusion(bf16[8,128,64]{1,2,0:T(8,128)(2,1)S(1)} %copy-done, bf16[2048,8,128]{2,0,1:T(8,128)(2,1)} %bitcast.137, bf16[64,8,128]{2,0,1:T(8,128)(2,1)S(1)} %get-tuple-element.279), kind=kOutput, calls=%fused_computation.113 | convolution fusion | flops 287637568 | bytes 8849408 | tf_op jit(solution)/shard_map/sub | solution.py:38
  168.4 2.8 divide_convert_fusion
  173.4 2.0 copy-done.2
  175.4 2.4 fusion.65
  177.9 4.8 %copy.68 = bf16[8,16,8,2048]{3,2,0,1:T(8,128)(2,1)} copy(bf16[8,16,8,2048]{3,2,1,0:T(8,128)(2,1)} %bitcast.146) | data formatting | bytes 8388608 | tf_op jit(solution)/shard_map/reshape | solution.py:120
  182.6 11.9 %all-to-all-start.2 = ((bf16[64,16,2048]{2,0,1:T(8,128)(2,1)}), bf16[64,16,2048]{2,0,1:T(8,128)(2,1)}, u32[]{:S(2)}, u32[]{:S(2)}) async-start(bf16[64,16,2048]{2,0,1:T(8,128)(2,1)} %bitcast.142), calls=%async_computation.2 | async-start | bytes 8388608 | tf_op jit(solution)/shard_map/all_to_all | solution.py:119
  194.6 53.3 %all-to-all-done.2 = bf16[64,16,2048]{2,0,1:T(8,128)(2,1)} async-done(((bf16[64,16,2048]{2,0,1:T(8,128)(2,1)}), bf16[64,16,2048]{2,0,1:T(8,128)(2,1)}, u32[]{:S(2)}, u32[]{:S(2)}) %all-to-all-start.2) | async-done | bytes 4194336 | tf_op jit(solution)/shard_map/all_to_all | solution.py:119
  247.9 6.6 %copy.47 = bf16[8,128,2048]{1,2,0:T(8,128)(2,1)} copy(bf16[8,128,2048]{2,1,0:T(8,128)(2,1)} %bitcast.18) | data formatting | bytes 8388608 | tf_op jit(solution)/shard_map/reshape | solution.py:48
  254.5 4.0 divide_convert_fusion.3
  258.5 5.6 %divide_convert_fusion.2 = bf16[8,2048,64]{1,2,0:T(8,128)(2,1)} fusion(bf16[8,128,64]{1,2,0:T(8,128)(2,1)} %param.13, bf16[8,128,2048]{1,2,0:T(8,128)(2,1)} %copy.47), kind=kOutput, calls=%fused_computation.80 | convolution fusion | flops 272662656 | bytes 6422528 | tf_op jit(solution)/shard_map/div | solution.py:38
  264.0 4.2 pad_maximum_fusion.2
  268.2 5.5 %slice_reduce_fusion = bf16[8,128]{1,0:T(8,128)(2,1)S(1)} fusion(bf16[8,2112,128]{1,2,0:T(8,128)(2,1)} %copy-done.2), kind=kLoop, calls=%fused_computation.88 | loop fusion | flops 2096128 | bytes 4196352 | tf_op jit(solution)/shard_map/reduce_sum | solution.py:155
  273.7 24.9 %all-gather.1 = bf16[128,128]{1,0:T(8,128)(2,1)S(1)} all-gather(bf16[8,128]{1,0:T(8,128)(2,1)S(1)} %slice_reduce_fusion), channel_id=3, replica_groups=mesh['heads'=8,'seq'=16] {'seq'}, dimensions={0}, use_global_device_ids=true | all-gather | bytes 34816 | tf_op jit(solution)/shard_map/all_gather | solution.py:19
  299.7 2.5 pad_maximum_fusion
  303.4 2.3 pad_maximum_fusion.1
  305.8 15.8 %while.28 = (s32[]{:T(128)}, f32[8,128,128]{2,1,0:T(8,128)S(1)}, f32[8,128]{1,0:T(8,128)S(1)}, s32[]{:T(128)}, bf16[16,8,128,128]{3,2,1,0:T(8,128)(2,1)}, /*inde...) while((s32[]{:T(128)}, f32[8,128,128]{2,1,0:T(8,128)S(1)}, f32[8,128]{1,0:T(8,128)S(1)}, ...), condition=%wide.region_6.0_spmd, body=%wide.region_5.0_spmd.sunk | while | flops 264197 | bytes 1321103 | solution.py:33
  322.8 97.0 %while.29 = (s32[]{:T(128)}, f32[8,128,128]{2,1,0:T(8,128)S(1)}, f32[8,128]{1,0:T(8,128)S(1)}, bf16[4,512,1024]{2,1,0:T(8,128)(2,1)}, s32[4]{0:T(128)S(1)}, /*in...) while((s32[]{:T(128)}, f32[8,128,128]{2,1,0:T(8,128)S(1)}, ...), condition=%wide.region_17.18_spmd.clone.clone, body=%wide.region_12.17_spmd.clone.clone.sunk | while | flops 3268147456 | bytes 82914816 | solution.py:107
  324.0 2.1 convert_reduce_fusion.5
  328.2 2.3 fusion.128
  332.4 3.6 convert_reduce_fusion.6
  336.9 3.3 fusion.131
  342.2 3.3 fusion.135
  348.2 2.1 convert_reduce_fusion.5
  352.5 2.3 fusion.128
  356.6 3.7 convert_reduce_fusion.6
  361.2 3.3 fusion.131
  366.4 3.3 fusion.135
  372.4 2.1 convert_reduce_fusion.5
  376.7 2.3 fusion.128
  380.9 3.7 convert_reduce_fusion.6
  385.4 3.3 fusion.131
  390.7 3.3 fusion.135
  396.7 2.1 convert_reduce_fusion.5
  400.9 2.3 fusion.128
  405.1 3.7 convert_reduce_fusion.6
  409.7 3.3 fusion.131
  414.9 3.3 fusion.135
  (124 shorter events, 58.7 us)
Async XLA Ops:
  6.5 150.3 %copy-start = (bf16[8,128,64]{1,2,0:T(8,128)(2,1)S(1)}, bf16[8,128,64]{1,2,0:T(8,128)(2,1)}, u32[]{:S(2)}) copy-start(bf16[8,128,64]{1,2,0:T(8,128)(2,1)} %param.14) | copy-start | bytes 393220
  11.4 64.3 %all-to-all-start = ((bf16[64,16,2048]{2,0,1:T(8,128)(2,1)}), bf16[64,16,2048]{2,0,1:T(8,128)(2,1)}, u32[]{:S(2)}, u32[]{:S(2)}) async-start(bf16[64,16,2048]{2,0,1:T(8,128)(2,1)} %bitcast.143), calls=%async_computation | async-start | bytes 8388608 | tf_op jit(solution)/shard_map/all_to_all | solution.py:126
  75.6 65.2 %all-to-all-start.1 = ((bf16[64,16,2048]{2,0,1:T(8,128)(2,1)}), bf16[64,16,2048]{2,0,1:T(8,128)(2,1)}, u32[]{:S(2)}, u32[]{:S(2)}) async-start(bf16[64,16,2048]{2,0,1:T(8,128)(2,1)} %bitcast.141), calls=%async_computation.1 | async-start | bytes 8388608 | tf_op jit(solution)/shard_map/all_to_all | solution.py:133
  86.3 219.4 %all-gather.4.cloned.1.call-start = ((), (), s32[]{:S(2)}) async-start(), calls=%async_computation.3 | async-start | bytes 4456448 | tf_op jit(solution)/shard_map/all_gather | solution.py:19
  148.3 8.5 %collective-permute-start = (bf16[2,64,8,128]{3,1,2,0:T(8,128)(2,1)S(1)}, bf16[2,64,8,128]{3,1,2,0:T(8,128)(2,1)S(1)}, u32[]{:S(2)}, u32[]{:S(2)}) collective-permute-start(bf16[2,64,8,128]{3,1,2,0:T(8,128)(2,1)S(1)} %pad_maximum_fusion.3), channel_id=1, source_target_pairs={{0,1},{1,2},{2,3},{3,4},{4,5},{5,6},{6,7},{7,8},{8,9},{9,10},{10,1... | collective-permute-start | bytes 786440 | tf_op jit(solution)/shard_map/ppermute | solution.py:13
  168.4 3.6 copy-start.7
  172.4 3.0 copy-start.5
  173.4 2.0 copy-start.2
  182.6 11.9 %copy-start.8 = (f32[8]{0:T(128)S(1)}, f32[8]{0:T(128)}, u32[]{:S(2)}) copy-start(f32[8]{0:T(128)} %param.15) | copy-start | bytes 100
  182.6 65.3 %all-to-all-start.2 = ((bf16[64,16,2048]{2,0,1:T(8,128)(2,1)}), bf16[64,16,2048]{2,0,1:T(8,128)(2,1)}, u32[]{:S(2)}, u32[]{:S(2)}) async-start(bf16[64,16,2048]{2,0,1:T(8,128)(2,1)} %bitcast.142), calls=%async_computation.2 | async-start | bytes 8388608 | tf_op jit(solution)/shard_map/all_to_all | solution.py:119
  268.2 31.5 %copy-start.4 = (bf16[8,128,2048]{1,2,0:T(8,128)(2,1)S(1)}, bf16[8,128,2048]{1,2,0:T(8,128)(2,1)}, u32[]{:S(2)}) copy-start(bf16[8,128,2048]{1,2,0:T(8,128)(2,1)} %copy.42) | copy-start | bytes 12582916
  299.7 3.8 copy-start.6
  323.9 6.6 %copy-start.3 = (bf16[2112,8,128]{2,0,1:T(8,128)(2,1)S(1)}, bf16[2112,8,128]{2,0,1:T(8,128)(2,1)}, u32[]{:S(2)}) copy-start(bf16[2112,8,128]{2,0,1:T(8,128)(2,1)} %get-tuple-element.472) | copy-start | bytes 12976132 | tf_op jit(solution)/shard_map/while
  348.2 6.6 %copy-start.3 = (bf16[2112,8,128]{2,0,1:T(8,128)(2,1)S(1)}, bf16[2112,8,128]{2,0,1:T(8,128)(2,1)}, u32[]{:S(2)}) copy-start(bf16[2112,8,128]{2,0,1:T(8,128)(2,1)} %get-tuple-element.472) | copy-start | bytes 12976132 | tf_op jit(solution)/shard_map/while
  372.4 6.6 %copy-start.3 = (bf16[2112,8,128]{2,0,1:T(8,128)(2,1)S(1)}, bf16[2112,8,128]{2,0,1:T(8,128)(2,1)}, u32[]{:S(2)}) copy-start(bf16[2112,8,128]{2,0,1:T(8,128)(2,1)} %get-tuple-element.472) | copy-start | bytes 12976132 | tf_op jit(solution)/shard_map/while
  396.6 6.6 %copy-start.3 = (bf16[2112,8,128]{2,0,1:T(8,128)(2,1)S(1)}, bf16[2112,8,128]{2,0,1:T(8,128)(2,1)}, u32[]{:S(2)}) copy-start(bf16[2112,8,128]{2,0,1:T(8,128)(2,1)} %get-tuple-element.472) | copy-start | bytes 12976132 | tf_op jit(solution)/shard_map/while
  419.7 0.9 copy-start.1
Sparse Core Ops, SparseCore 0:
  178.0 91.9 all-gather.3
where the time goes:
time: 432 us; the launch traced here: 427 us
  waiting for transfers between devices  158 us (37%)
  matrix products  92.5 us (21%)
  other arithmetic  52.7 us (12%)
  local copies, waits for them, and re-layouts  48.5 us (11%)
  starting transfers between devices  34.2 us (8%)
  blocking collectives  24.9 us (6%)
  between operations  13.6 us (3%)
    all_to_all x1, waiting for transfers between devices, body(): lax.all_to_all(queries.reshape(feature_rows, shards, length), 'seq', spli...  53.3 us
    all_to_all x1, waiting for transfers between devices, body(): lax.all_to_all(keys.reshape(feature_rows, shards, length), 'seq', split_a...  52.6 us
    all_to_all x1, waiting for transfers between devices, body(): lax.all_to_all(values.reshape(feature_rows, shards, length), 'seq', split...  48 us
    all_gather x1, blocking collectives, entering(): lax.all_gather(a.astype(kind), axis)  24.9 us
    reshape x3, local copies, waits for them, and re-layouts, token_major(): return features.reshape(group, head_dim, count).transpose(2, 0, 1)  19.5 us
    add x28, other arithmetic, add_states(): return (earlier[0] + later[0], earlier[1] + later[1])  15.1 us
    dot_general x4, matrix products, advance(): jnp.einsum('hqf,hkf->hqk', phi_rows, phi_block, preferred_element_type=jn...  14.6 us
    dot_general x4, matrix products, advance(): jnp.einsum('qhd,khd->hqk', query_rows, window_keys, preferred_element_typ...  13.1 us
  transfers between devices with their start and end apart: 5, of which 4 were waited for; matrix products, arithmetic and copies ran while one was open for 11% of the time, Pallas kernels for 0%

commit v1 on v0

v1 whole, which is shorter than its diff:
```python
import jax
import jax.numpy as jnp
from jax import lax
from jax.sharding import PartitionSpec as P

WIN = 64
BLOCK = 512
CHUNKS = 4


def passed_along(block, axis, distance):
    devices = range(lax.axis_size(axis))
    route = [(i - distance, i) for i in devices if i - distance in devices]
    return lax.ppermute(block, axis, route)


def exchange(rows, group, head_dim):
    moved = lax.all_to_all(rows, "seq", split_axis=1, concat_axis=0, tiled=True)
    return moved.reshape(group, head_dim, -1)


def feature_map(rows, weight):
    logits = jnp.einsum("hdt,hdf->htf", rows, weight, preferred_element_type=jnp.float32)
    halves = [jax.nn.softmax(logits, axis=-1), jax.nn.softmax(-logits, axis=-1)]
    return jnp.concatenate(halves, axis=-1).astype(jnp.bfloat16)


def window_chunk(q, k_cur, k_prev, v_cur, v_prev, first_masked):
    head_dim = q.shape[1]
    w = q.shape[3]
    scale = jnp.sqrt(jnp.float32(head_dim))
    s_cur = jnp.einsum("hdbt,hdbj->hbtj", q, k_cur, preferred_element_type=jnp.float32) / scale
    s_prev = jnp.einsum("hdbt,hdbj->hbtj", q, k_prev, preferred_element_type=jnp.float32) / scale
    ti = jnp.arange(w)[:, None]
    ji = jnp.arange(w)[None, :]
    keep_cur = ji <= ti
    keep_prev = ji > ti
    bi = jnp.arange(q.shape[2])[:, None, None]
    keep_prev = keep_prev[None] & jnp.logical_not((bi == 0) & first_masked)
    s_cur = jnp.where(keep_cur[None, None], s_cur, jnp.float32(-1e30))
    s_prev = jnp.where(keep_prev[None], s_prev, jnp.float32(-1e30))
    top = jnp.maximum(jnp.max(s_cur, axis=-1, keepdims=True), jnp.max(s_prev, axis=-1, keepdims=True))
    p_cur = jnp.exp(s_cur - top)
    p_prev = jnp.exp(s_prev - top)
    total = jnp.sum(p_cur, axis=-1) + jnp.sum(p_prev, axis=-1)
    out = jnp.einsum(
        "hbtj,hdbj->hbtd", p_cur.astype(jnp.bfloat16), v_cur, preferred_element_type=jnp.float32
    ) + jnp.einsum(
        "hbtj,hdbj->hbtd", p_prev.astype(jnp.bfloat16), v_prev, preferred_element_type=jnp.float32
    )
    return out / total[..., None]


def body(queries, keys, values, feat_q, feat_k, mix):
    shards = lax.axis_size("seq")
    place = lax.axis_index("seq")
    feature_rows = queries.shape[0]
    length = queries.shape[1] // shards
    group = feat_q.shape[0]
    head_dim = feat_q.shape[1]
    chunk = length // CHUNKS
    nb = chunk // WIN

    k = exchange(keys.reshape(feature_rows, shards, length), group, head_dim)
    v = exchange(values.reshape(feature_rows, shards, length), group, head_dim)
    qs = queries.reshape(feature_rows, shards, CHUNKS, chunk)
    q_parts = [exchange(qs[:, :, c, :], group, head_dim) for c in range(CHUNKS)]

    earlier = place > 0
    tails = jnp.stack([k[:, :, length - WIN :], v[:, :, length - WIN :]])
    before = passed_along(tails, "seq", 1)
    k_ext = jnp.concatenate([before[0], k], axis=2)
    v_ext = jnp.concatenate([before[1], v], axis=2)

    keep = jnp.logical_or(jnp.arange(length + WIN) >= WIN, earlier).astype(jnp.bfloat16)
    phi_k = feature_map(k_ext, feat_k) * keep[None, :, None]

    own_state = jnp.einsum(
        "htf,hdt->hfd", phi_k[:, WIN:], v, preferred_element_type=jnp.float32
    )
    own_norm = jnp.sum(phi_k[:, WIN:], axis=1, dtype=jnp.float32)
    gathered_state = lax.all_gather(own_state.astype(jnp.bfloat16), "seq")
    gathered_norm = lax.all_gather(own_norm.astype(jnp.bfloat16), "seq")
    below = (jnp.arange(shards) < place).astype(jnp.float32)
    prior_state = jnp.einsum(
        "s,shfd->hfd", below, gathered_state.astype(jnp.float32), precision=lax.Precision.HIGHEST
    )
    prior_norm = jnp.einsum(
        "s,shf->hf", below, gathered_norm.astype(jnp.float32), precision=lax.Precision.HIGHEST
    )

    halo_state = jnp.einsum(
        "htf,hdt->hfd", phi_k[:, :WIN], before[1], preferred_element_type=jnp.float32
    )
    halo_norm = jnp.sum(phi_k[:, :WIN], axis=1, dtype=jnp.float32)

    gate = jax.nn.sigmoid(mix)
    qi = jnp.arange(chunk)[:, None]
    ki = jnp.arange(chunk)[None, :]
    lin_keep = ki <= qi

    states = -halo_state
    norms = -halo_norm
    windows, nums, dens, phis = [], [], [], []
    for c in range(CHUNKS):
        start = c * chunk
        q = q_parts[c]
        phi_q = feature_map(q, feat_q)
        qb = q.reshape(group, head_dim, nb, WIN)
        k_cur = k[:, :, start : start + chunk].reshape(group, head_dim, nb, WIN)
        k_prev = k_ext[:, :, start : start + chunk].reshape(group, head_dim, nb, WIN)
        v_cur = v[:, :, start : start + chunk].reshape(group, head_dim, nb, WIN)
        v_prev = v_ext[:, :, start : start + chunk].reshape(group, head_dim, nb, WIN)
        first_masked = jnp.logical_and(c == 0, jnp.logical_not(earlier))
        win = window_chunk(qb, k_cur, k_prev, v_cur, v_prev, first_masked)
        windows.append(win.reshape(group, chunk, head_dim))

        phi_block = phi_k[:, start : start + chunk]
        value_block = v_ext[:, :, start : start + chunk]
        affinity = jnp.einsum("htf,hjf->htj", phi_q, phi_block, preferred_element_type=jnp.float32)
        affinity = jnp.where(lin_keep[None], affinity, jnp.float32(0.0)).astype(jnp.bfloat16)
        inner_num = jnp.einsum(
            "htj,hdj->htd", affinity, value_block, preferred_element_type=jnp.float32
        )
        inner_den = jnp.sum(affinity, axis=-1, dtype=jnp.float32)
        phi_wide = phi_q.astype(jnp.float32)
        cross_num = jnp.einsum("htf,hfd->htd", phi_wide, states, precision=lax.Precision.HIGHEST)
        cross_den = jnp.einsum("htf,hf->ht", phi_wide, norms, precision=lax.Precision.HIGHEST)
        nums.append(cross_num + inner_num)
        dens.append(cross_den + inner_den)
        phis.append(phi_q)
        if c + 1 < CHUNKS:
            states = states + jnp.einsum(
                "hjf,hdj->hfd", phi_block, value_block, preferred_element_type=jnp.float32
            )
            norms = norms + jnp.sum(phi_block, axis=1, dtype=jnp.float32)

    window = jnp.concatenate(windows, axis=1)
    num = jnp.concatenate(nums, axis=1)
    den = jnp.concatenate(dens, axis=1)
    phi_all = jnp.concatenate(phis, axis=1).astype(jnp.float32)
    prior_num = jnp.einsum("htf,hfd->htd", phi_all, prior_state, precision=lax.Precision.HIGHEST)
    prior_den = jnp.einsum("htf,hf->ht", phi_all, prior_norm, precision=lax.Precision.HIGHEST)
    linear = (num + prior_num) / (den + prior_den + 1.0)[..., None]
    mixed = gate[:, None, None] * window + (1.0 - gate)[:, None, None] * linear
    return mixed.astype(jnp.bfloat16).transpose(1, 0, 2).reshape(length, group * head_dim)


def solution(mesh):
    return jax.shard_map(
        body,
        mesh=mesh,
        in_specs=(
            P(("heads", "seq"), None),
            P(("heads", "seq"), None),
            P(("heads", "seq"), None),
            P("heads", None, None),
            P("heads", None, None),
            P("heads"),
        ),
        out_specs=P("seq", "heads"),
        check_vma=False,
    )
```

time: 432 us -> 479 us (1.11)
  waiting for transfers between devices: 158 us -> 59.7 us
  local copies, waits for them, and re-layouts: 48.5 us -> 139 us
  matrix products: 92.5 us -> 143 us
  starting transfers between devices: 34.2 us -> 55.7 us
  other arithmetic: 52.7 us -> 36.1 us
    all_to_all x3 -> x6, waiting for transfers between devices: 154 us -> 51.3 us  [exchange(): moved = lax.all_to_all(rows, 'seq', split_axis=1, concat_axis=0, tiled=True)]
    slice x0 -> x18, local copies, waits for them, and re-layouts: none -> 54.8 us  [the longest x1 16.2 us: body(): q_parts = [exchange(qs[:, :, c, :], group, head_dim) for c in range(CHUNKS)]]
    dot_general x30 -> x41, matrix products: 71.3 us -> 118 us  [the longest x4 22.7 us: window_chunk(): jnp.einsum('hdbt,hdbj->hbtj', q, k_cur, preferred_element_type=jnp.float32)]
    another operation x1 -> x9, local copies, waits for them, and re-layouts: 0.99 us -> 23 us  [the longest x8 22.1 us: body(): qb = q.reshape(group, head_dim, nb, WIN)]
    all_to_all x3 -> x6, starting transfers between devices: 29.5 us -> 50.8 us  [exchange(): moved = lax.all_to_all(rows, 'seq', split_axis=1, concat_axis=0, tiled=True)]
    unnamed x16 -> x217, local copies, waits for them, and re-layouts: 5.02 us -> 21 us
    reduce_sum x10 -> x4, other arithmetic: 23 us -> 8.5 us  [the longest x1 3.78 us: body(): own_norm = jnp.sum(phi_k[:, WIN:], axis=1, dtype=jnp.float32)]
    add x40 -> x10, other arithmetic: 15.2 us -> 1.93 us  [the longest x4 1.87 us: window_chunk(): total = jnp.sum(p_cur, axis=-1) + jnp.sum(p_prev, axis=-1)]
  transfers between devices with their start and end apart: 5 -> 8, of which waited for: 4 -> 7; matrix products, arithmetic and copies ran while one was open for 11% -> 34% of each run, Pallas kernels for 0% -> 0%
where the time goes in v1:
time: 479 us; the launch traced here: 472 us
  matrix products  143 us (30%)
  local copies, waits for them, and re-layouts  139 us (29%)
  waiting for transfers between devices  59.7 us (12%)
  starting transfers between devices  55.7 us (12%)
  other arithmetic  36.1 us (8%)
  blocking collectives  24 us (5%)
  between operations  14.7 us (3%)
    all_to_all x6, waiting for transfers between devices, exchange(): moved = lax.all_to_all(rows, 'seq', split_axis=1, concat_axis=0, tiled=True)  51.3 us
    all_to_all x6, starting transfers between devices, exchange(): moved = lax.all_to_all(rows, 'seq', split_axis=1, concat_axis=0, tiled=True)  50.8 us
    sub x10, matrix products, feature_map(): halves = [jax.nn.softmax(logits, axis=-1), jax.nn.softmax(-logits, axis=-1)]  24.4 us
    all_gather x1, blocking collectives, body(): gathered_norm = lax.all_gather(own_norm.astype(jnp.bfloat16), 'seq')  24 us
    dot_general x4, matrix products, window_chunk(): jnp.einsum('hdbt,hdbj->hbtj', q, k_cur, preferred_element_type=jnp.float32)  22.7 us
    another operation x8, local copies, waits for them, and re-layouts, body(): qb = q.reshape(group, head_dim, nb, WIN)  22.1 us
    unnamed x217, local copies, waits for them, and re-layouts  21 us
    slice x1, local copies, waits for them, and re-layouts, body(): q_parts = [exchange(qs[:, :, c, :], group, head_dim) for c in range(CHUNKS)]  16.2 us
  transfers between devices with their start and end apart: 8, of which 7 were waited for; matrix products, arithmetic and copies ran while one was open for 34% of the time, Pallas kernels for 0%

profile of v1, /device:TPU:116, one launch (start us, length us, event | category | flops | bytes accessed | tf_op | source)
XLA Modules:
  0.0 472.2 jit_solution(14864268384581718247)
XLA Ops:
  6.5 7.9 %reshape.219 = bf16[64,16,4,512]{3,2,1,0:T(4,128)(2,1)} reshape(bf16[64,32768]{1,0:T(8,128)(2,1)} %param.6) | data formatting | bytes 8388608 | tf_op jit(solution)/shard_map/reshape | solution.py:66
  14.4 16.2 %fusion.191 = (bf16[64,16,1,512]{3,2,1,0:T(2,128)(2,1)}, bf16[64,16,1,512]{3,2,1,0:T(2,128)(2,1)S(1)}, bf16[64,16,1,512]{3,2,1,0:T(2,128)(2,1)}, bf16[64,16,1,512]{3,2,1,0:T(2,128)(2,1)S(1)}) fusion(bf16[64,16,4,512]{3,2,1,0:T(4,128)(2,1)} %reshape.219), kind=kLoop, calls=%fused_computation.265 | loop fusion | bytes 8388608 | tf_op jit(solution)/shard_map/slice | solution.py:67
  32.7 6.9 %all-to-all-start.4 = ((bf16[64,16,512]{2,0,1:T(8,128)(2,1)}), bf16[64,16,512]{2,0,1:T(8,128)(2,1)S(1)}, u32[]{:S(2)}, u32[]{:S(2)}) async-start(bf16[64,16,512]{2,0,1:T(8,128)(2,1)} %bitcast.221), calls=%async_computation.4 | async-start | bytes 2097152 | tf_op jit(solution)/shard_map/all_to_all | solution.py:18
  41.7 11.3 %all-to-all-done.4 = bf16[64,16,512]{2,0,1:T(8,128)(2,1)S(1)} async-done(((bf16[64,16,512]{2,0,1:T(8,128)(2,1)}), bf16[64,16,512]{2,0,1:T(8,128)(2,1)S(1)}, u32[]{:S(2)}, u32[]{:S(2)}) %all-to-all-start.4) | async-done | bytes 1048608 | tf_op jit(solution)/shard_map/all_to_all | solution.py:18
  53.0 8.0 %all-to-all-start.5 = ((bf16[64,16,512]{2,0,1:T(8,128)(2,1)}), bf16[64,16,512]{2,0,1:T(8,128)(2,1)S(1)}, u32[]{:S(2)}, u32[]{:S(2)}) async-start(bf16[64,16,512]{2,0,1:T(8,128)(2,1)} %bitcast.219), calls=%async_computation.5 | async-start | bytes 2097152 | tf_op jit(solution)/shard_map/all_to_all | solution.py:18
  61.0 3.7 copy.306
  64.6 8.3 %all-to-all-done.5 = bf16[64,16,512]{2,0,1:T(8,128)(2,1)S(1)} async-done(((bf16[64,16,512]{2,0,1:T(8,128)(2,1)}), bf16[64,16,512]{2,0,1:T(8,128)(2,1)S(1)}, u32[]{:S(2)}, u32[]{:S(2)}) %all-to-all-start.5) | async-done | bytes 1048608 | tf_op jit(solution)/shard_map/all_to_all | solution.py:18
  73.0 7.9 %all-to-all-start.3 = ((bf16[64,16,512]{2,0,1:T(8,128)(2,1)}), bf16[64,16,512]{2,0,1:T(8,128)(2,1)S(1)}, u32[]{:S(2)}, u32[]{:S(2)}) async-start(bf16[64,16,512]{2,0,1:T(8,128)(2,1)} %bitcast.218), calls=%async_computation.3 | async-start | bytes 2097152 | tf_op jit(solution)/shard_map/all_to_all | solution.py:18
  80.9 3.7 copy.307
  84.6 8.4 %all-to-all-done.3 = bf16[64,16,512]{2,0,1:T(8,128)(2,1)S(1)} async-done(((bf16[64,16,512]{2,0,1:T(8,128)(2,1)}), bf16[64,16,512]{2,0,1:T(8,128)(2,1)S(1)}, u32[]{:S(2)}, u32[]{:S(2)}) %all-to-all-start.3) | async-done | bytes 1048608 | tf_op jit(solution)/shard_map/all_to_all | solution.py:18
  93.0 8.6 %all-to-all-start = ((bf16[64,16,512]{2,0,1:T(8,128)(2,1)}), bf16[64,16,512]{2,0,1:T(8,128)(2,1)}, u32[]{:S(2)}, u32[]{:S(2)}) async-start(bf16[64,16,512]{2,0,1:T(8,128)(2,1)} %bitcast.220), calls=%async_computation | async-start | bytes 2097152 | tf_op jit(solution)/shard_map/all_to_all | solution.py:18
  101.6 4.8 %copy.303 = bf16[8,16,8,2048]{3,2,0,1:T(8,128)(2,1)} copy(bf16[8,16,8,2048]{3,2,1,0:T(8,128)(2,1)} %bitcast.223) | data formatting | bytes 8388608 | tf_op jit(solution)/shard_map/reshape | solution.py:64
  106.3 6.9 %all-to-all-done = bf16[64,16,512]{2,0,1:T(8,128)(2,1)} async-done(((bf16[64,16,512]{2,0,1:T(8,128)(2,1)}), bf16[64,16,512]{2,0,1:T(8,128)(2,1)}, u32[]{:S(2)}, u32[]{:S(2)}) %all-to-all-start) | async-done | bytes 1048608 | tf_op jit(solution)/shard_map/all_to_all | solution.py:18
  113.3 9.2 %all-to-all-start.1 = ((bf16[64,16,2048]{2,0,1:T(8,128)(2,1)}), bf16[64,16,2048]{2,0,1:T(8,128)(2,1)}, u32[]{:S(2)}, u32[]{:S(2)}) async-start(bf16[64,16,2048]{2,0,1:T(8,128)(2,1)} %bitcast.210), calls=%async_computation.1 | async-start | bytes 8388608 | tf_op jit(solution)/shard_map/all_to_all | solution.py:18
  122.5 4.7 %copy.302 = bf16[8,16,8,2048]{3,2,0,1:T(8,128)(2,1)} copy(bf16[8,16,8,2048]{3,2,1,0:T(8,128)(2,1)} %bitcast.224) | data formatting | bytes 8388608 | tf_op jit(solution)/shard_map/reshape | solution.py:65
  132.0 3.0 copy.200
  142.1 3.0 copy.191
  145.1 3.9 reshape_reshape.12
  149.0 3.0 copy.176
  160.6 11.6 %all-to-all-done.1 = bf16[64,16,2048]{2,0,1:T(8,128)(2,1)} async-done(((bf16[64,16,2048]{2,0,1:T(8,128)(2,1)}), bf16[64,16,2048]{2,0,1:T(8,128)(2,1)}, u32[]{:S(2)}, u32[]{:S(2)}) %all-to-all-start.1) | async-done | bytes 4194336 | tf_op jit(solution)/shard_map/all_to_all | solution.py:18
  172.3 10.2 %all-to-all-start.2 = ((bf16[64,16,2048]{2,0,1:T(8,128)(2,1)}), bf16[64,16,2048]{2,0,1:T(8,128)(2,1)}, u32[]{:S(2)}, u32[]{:S(2)}) async-start(bf16[64,16,2048]{2,0,1:T(8,128)(2,1)} %bitcast.209), calls=%async_computation.2 | async-start | bytes 8388608 | tf_op jit(solution)/shard_map/all_to_all | solution.py:18
  194.2 6.4 %copy.177 = bf16[8,128,2048]{1,2,0:T(8,128)(2,1)} copy(bf16[8,128,2048]{2,1,0:T(8,128)(2,1)} %bitcast.5) | data formatting | bytes 8388608 | tf_op jit(solution)/shard_map/reshape | solution.py:19
  200.7 7.3 %fusion.190 = (bf16[8,128,512]{2,1,0:T(8,128)(2,1)S(1)}, bf16[8,128,512]{2,1,0:T(8,128)(2,1)}, bf16[8,128,512]{2,1,0:T(8,128)(2,1)}, bf16[8,128,512]{2,1,0:T(8,1...) fusion(bf16[8,128,2048]{2,1,0:T(8,128)(2,1)} %bitcast.5), kind=kLoop, calls=%fused_computation.264 | loop fusion | bytes 14680064 | tf_op jit(solution)/shard_map/slice | solution.py:110
  229.1 4.7 all-to-all-done.2
  237.6 4.5 collective-permute-start
  242.1 3.9 fusion.30
  250.5 17.3 %fusion.49 = (f32[8,8,64]{2,1,0:T(8,128)S(1)}, f32[8,8,64]{2,1,0:T(8,128)S(1)}, f32[8,8,64]{2,1,0:T(8,128)S(1)}, f32[8,8,64]{2,1,0:T(8,128)S(1)}, f32[8,8,64]{2,...) fusion(f32[8,8,64,64]{2,3,1,0:T(8,128)S(1)} %copy-done.13, ...), kind=kOutput, calls=%fused_computation.95 | convolution fusion | flops 74158080 | bytes 9609216 | tf_op jit(solution)/shard_map/hdbt,hdbj->hbtj/dot_general | solution.py:32
  272.1 5.8 %fusion.195 = (f32[8,2112]{1,0:T(8,128)S(1)}, f32[8,2112,64]{1,2,0:T(8,128)}) fusion(bf16[8,128,64]{1,2,0:T(8,128)(2,1)S(1)} %copy-done, bf16[8,128,2048]{1,2,0:T(8,128)(2,1)} %copy.177, bf16[8,128,64]{1,2,0:T(8,128)(2,1)S(1)} %get-tuple-element.52), kind=kOutput, calls=%fused_computation.267 | convolution fusion | flops 287637568 | bytes 8849408 | tf_op jit(solution)/shard_map/sub | solution.py:24
  277.9 5.8 %fusion.192 = (f32[8,2112]{1,0:T(8,128)S(1)}, f32[8,2112,64]{1,2,0:T(8,128)}) fusion(bf16[8,128,64]{1,2,0:T(8,128)(2,1)S(1)} %copy-done, bf16[8,128,2048]{1,2,0:T(8,128)(2,1)} %copy.177, bf16[8,128,64]{1,2,0:T(8,128)(2,1)S(1)} %get-tuple-element.52), kind=kOutput, calls=%fused_computation.266 | convolution fusion | flops 288718912 | bytes 8849408 | tf_op jit(solution)/shard_map/sub | solution.py:24
  283.7 4.6 divide_convert_fusion
  289.3 3.8 slice_reduce_fusion
  294.9 4.6 fusion.67
  299.5 3.2 multiply_bitcast_fusion
  305.8 6.7 %fusion.189 = (bf16[8,128,512]{2,1,0:T(8,128)(2,1)}, bf16[8,128,512]{2,1,0:T(8,128)(2,1)}, bf16[8,128,512]{2,1,0:T(8,128)(2,1)}, bf16[8,128,512]{2,1,0:T(8,128)(...) fusion(bf16[8,128,2048]{2,1,0:T(8,128)(2,1)} %bitcast.12, ...), kind=kLoop, calls=%fused_computation.263 | loop fusion | flops 2097152 | bytes 20054016 | tf_op jit(solution)/shard_map/slice | solution.py:112
  335.4 3.2 convolution_add_fusion.4
  338.6 24.0 %all-gather.1 = bf16[128,128]{1,0:T(8,128)(2,1)S(1)} all-gather(bf16[8,128]{1,0:T(8,128)(2,1)S(1)} %copy-done.99), channel_id=3, replica_groups=mesh['heads'=8,'seq'=16] {'seq'}, dimensions={0}, use_global_device_ids=true | all-gather | bytes 34816 | tf_op jit(solution)/shard_map/all_gather | solution.py:83
  363.4 4.0 convert_reduce_fusion.3
  368.6 4.0 convert_reduce_fusion.2
  373.7 3.9 convert_reduce_fusion.1
  378.7 4.0 convert_reduce_fusion
  393.0 3.4 fusion.185
  399.2 3.2 fusion.182
  405.0 3.2 fusion.179
  428.5 8.4 %all-gather.4.cloned.1.call-done = bf16[128,128,128]{2,1,0:T(8,128)(2,1)} async-done(((bf16[8,128,128]{2,1,0:T(8,128)(2,1)}), bf16[128,128,128]{2,1,0:T(8,128)(2,1)}) %all-gather.4.cloned.1.call-update) | async-done | bytes 4194320 | tf_op jit(solution)/shard_map/all_gather | solution.py:82
  436.9 4.8 %fusion.22 = f32[1,8,128,128]{3,0,2,1:T(1,128)S(1)} fusion(bf16[16,8,128,128]{3,2,1,0:T(8,128)(2,1)} %bitcast.222, s32[]{:T(128)S(6)} %axis_index.12), kind=kOutput, calls=%fused_computation.38 | convolution fusion | flops 4194320 | bytes 4718596 | tf_op jit(solution)/shard_map/s,shfd->hfd/dot_general | solution.py:85
  441.8 10.4 %fusion.27 = bf16[2048,8,128]{2,0,1:T(8,128)(2,1)} fusion(f32[8,2048]{1,0:T(8,128)S(1)} %fusion.135, f32[8,128,128]{2,1,0:T(8,128)S(1)} %bitcast.235, f32[8,512,128]{2,1,0:T(8,128)} %convolution_add_fusion, f32[8,512,128]{2,1,0:T(8,128)S(1)} %copy-done.44, f32[8,512,128]{2,1,0:T(8,128)S(1)} %copy-done.43, f32[8,512,128]{2,1,0:T(8,128)S(1)} %copy-done.42, ...), kind=kOutput, calls=%fused_computation.45 | convolution fusion | flops 3279945728 | bytes 25755712 | tf_op jit(solution)/shard_map/htf,hfd->htd/dot_general | solution.py:142
  452.1 6.6 %copy.235 = bf16[2048,8,128]{0,2,1:T(8,128)(2,1)} copy(bf16[2048,8,128]{2,0,1:T(8,128)(2,1)} %fusion.27) | data formatting | bytes 8388608 | tf_op jit(solution)/shard_map/transpose | solution.py:146
  458.7 6.4 %copy.236 = bf16[2048,1024]{1,0:T(8,128)(2,1)} copy(bf16[2048,1024]{0,1:T(8,128)(2,1)} %bitcast.211) | data formatting | bytes 8388608 | tf_op jit(solution)/shard_map/reshape | solution.py:146
  (309 shorter events, 138.0 us)
Async XLA Ops:
  6.5 265.6 %copy-start = (bf16[8,128,64]{1,2,0:T(8,128)(2,1)S(1)}, bf16[8,128,64]{1,2,0:T(8,128)(2,1)}, u32[]{:S(2)}) copy-start(bf16[8,128,64]{1,2,0:T(8,128)(2,1)} %param.10) | copy-start | bytes 393220
  32.7 20.3 %all-to-all-start.4 = ((bf16[64,16,512]{2,0,1:T(8,128)(2,1)}), bf16[64,16,512]{2,0,1:T(8,128)(2,1)S(1)}, u32[]{:S(2)}, u32[]{:S(2)}) async-start(bf16[64,16,512]{2,0,1:T(8,128)(2,1)} %bitcast.221), calls=%async_computation.4 | async-start | bytes 2097152 | tf_op jit(solution)/shard_map/all_to_all | solution.py:18
  53.0 20.0 %all-to-all-start.5 = ((bf16[64,16,512]{2,0,1:T(8,128)(2,1)}), bf16[64,16,512]{2,0,1:T(8,128)(2,1)S(1)}, u32[]{:S(2)}, u32[]{:S(2)}) async-start(bf16[64,16,512]{2,0,1:T(8,128)(2,1)} %bitcast.219), calls=%async_computation.5 | async-start | bytes 2097152 | tf_op jit(solution)/shard_map/all_to_all | solution.py:18
  73.0 20.0 %all-to-all-start.3 = ((bf16[64,16,512]{2,0,1:T(8,128)(2,1)}), bf16[64,16,512]{2,0,1:T(8,128)(2,1)S(1)}, u32[]{:S(2)}, u32[]{:S(2)}) async-start(bf16[64,16,512]{2,0,1:T(8,128)(2,1)} %bitcast.218), calls=%async_computation.3 | async-start | bytes 2097152 | tf_op jit(solution)/shard_map/all_to_all | solution.py:18
  93.0 20.3 %all-to-all-start = ((bf16[64,16,512]{2,0,1:T(8,128)(2,1)}), bf16[64,16,512]{2,0,1:T(8,128)(2,1)}, u32[]{:S(2)}, u32[]{:S(2)}) async-start(bf16[64,16,512]{2,0,1:T(8,128)(2,1)} %bitcast.220), calls=%async_computation | async-start | bytes 2097152 | tf_op jit(solution)/shard_map/all_to_all | solution.py:18
  113.3 59.0 %all-to-all-start.1 = ((bf16[64,16,2048]{2,0,1:T(8,128)(2,1)}), bf16[64,16,2048]{2,0,1:T(8,128)(2,1)}, u32[]{:S(2)}, u32[]{:S(2)}) async-start(bf16[64,16,2048]{2,0,1:T(8,128)(2,1)} %bitcast.210), calls=%async_computation.1 | async-start | bytes 8388608 | tf_op jit(solution)/shard_map/all_to_all | solution.py:18
  122.5 6.2 %copy-start.101 = (f32[8]{0:T(128)S(1)}, f32[8]{0:T(128)}, u32[]{:S(2)}) copy-start(f32[8]{0:T(128)} %param.11) | copy-start | bytes 100
  172.3 61.6 %all-to-all-start.2 = ((bf16[64,16,2048]{2,0,1:T(8,128)(2,1)}), bf16[64,16,2048]{2,0,1:T(8,128)(2,1)}, u32[]{:S(2)}, u32[]{:S(2)}) async-start(bf16[64,16,2048]{2,0,1:T(8,128)(2,1)} %bitcast.209), calls=%async_computation.2 | async-start | bytes 8388608 | tf_op jit(solution)/shard_map/all_to_all | solution.py:18
  182.5 254.4 %all-gather.4.cloned.1.call-start = ((), (), s32[]{:S(2)}) async-start(), calls=%async_computation.6 | async-start | bytes 4456448 | tf_op jit(solution)/shard_map/all_gather | solution.py:82
  227.0 15.1 %copy-start.7 = (bf16[8,128,8,64]{1,3,2,0:T(8,128)(2,1)S(1)}, bf16[8,128,8,64]{1,3,2,0:T(8,128)(2,1)}, u32[]{:S(2)}) copy-start(bf16[8,128,8,64]{1,3,2,0:T(8,128)(2,1)} %copy.191) | copy-start | bytes 3145732
  237.6 32.1 %collective-permute-start = (bf16[2,8,128,64]{2,3,1,0:T(8,128)(2,1)S(1)}, bf16[2,8,128,64]{2,3,1,0:T(8,128)(2,1)S(1)}, u32[]{:S(2)}, u32[]{:S(2)}) collective-permute-start(bf16[2,8,128,64]{2,3,1,0:T(8,128)(2,1)S(1)} %pad_maximum_fusion.18), channel_id=1, source_target_pairs={{0,1},{1,2},{2,3},{3,4},{4,5},{5,6},{6,7},{7,8},{8,9},{9,10},{10,1... | collective-permute-start | bytes 786440 | tf_op jit(solution)/shard_map/ppermute | solution.py:14
  242.1 4.0 copy-start.3
  246.1 4.0 copy-start.35
  246.2 4.3 copy-start.69
  247.6 20.2 %copy-start.10 = (f32[8,8,64,64]{2,3,1,0:T(8,128)}, f32[8,8,64,64]{2,3,1,0:T(8,128)S(1)}, u32[]{:S(2)}) copy-start(f32[8,8,64,64]{2,3,1,0:T(8,128)S(1)} %get-tuple-element.82) | copy-start | bytes 3145732
  247.6 20.1 %copy-start.79 = (f32[8,8,64]{2,1,0:T(8,128)}, f32[8,8,64]{2,1,0:T(8,128)S(1)}, u32[]{:S(2)}) copy-start(f32[8,8,64]{2,1,0:T(8,128)S(1)} %max.44) | copy-start | bytes 49156
  247.7 20.1 %copy-start.81 = (f32[8,8,64]{2,1,0:T(8,128)}, f32[8,8,64]{2,1,0:T(8,128)S(1)}, u32[]{:S(2)}) copy-start(f32[8,8,64]{2,1,0:T(8,128)S(1)} %max.43) | copy-start | bytes 49156
  247.7 20.1 %copy-start.77 = (f32[8,8,64]{2,1,0:T(8,128)}, f32[8,8,64]{2,1,0:T(8,128)S(1)}, u32[]{:S(2)}) copy-start(f32[8,8,64]{2,1,0:T(8,128)S(1)} %max.45) | copy-start | bytes 49156
  250.5 20.6 %copy-start.6 = (bf16[8,128,2048]{1,2,0:T(8,128)(2,1)S(1)}, bf16[8,128,2048]{1,2,0:T(8,128)(2,1)}, u32[]{:S(2)}) copy-start(bf16[8,128,2048]{1,2,0:T(8,128)(2,1)} %copy.177) | copy-start | bytes 12582916
  283.7 4.6 copy-start.87
  289.2 5.6 %copy-start.2 = (bf16[8,2112,128]{1,2,0:T(8,128)(2,1)}, bf16[8,2112,128]{1,2,0:T(8,128)(2,1)S(1)}, u32[]{:S(2)}) copy-start(bf16[8,2112,128]{1,2,0:T(8,128)(2,1)S(1)} %maximum_multiply_fusion.1) | copy-start | bytes 12976132
  294.9 4.6 copy-start.36
  325.2 38.1 %slice-start = ((s8[4456448]{0:T(1024)(128)(4,1)}), s8[262144]{0:T(1024)(128)(4,1)S(1)}, s32[]{:S(2)}) async-start(s8[4456448]{0:T(1024)(128)(4,1)} %bitcast.198), calls=%async_computation.7 | async-start | bytes 524288
  331.0 4.3 copy-start.18
  331.0 32.3 %slice-start.1 = ((s8[4456448]{0:T(1024)(128)(4,1)}), s8[4194304]{0:T(1024)(128)(4,1)S(1)}, s32[]{:S(2)}) async-start(s8[4456448]{0:T(1024)(128)(4,1)} %bitcast.198), calls=%async_computation.8 | async-start | bytes 8388608
  332.9 5.7 %copy-start.63 = (f32[8,128,128]{2,1,0:T(8,128)}, f32[8,128,128]{2,1,0:T(8,128)S(1)}, u32[]{:S(2)}) copy-start(f32[8,128,128]{2,1,0:T(8,128)S(1)} %convolution_add_fusion.6) | copy-start | bytes 1572868
  335.3 28.0 %copy-start.74 = (f32[8,128,128]{2,1,0:T(8,128)}, f32[8,128,128]{2,1,0:T(8,128)S(1)}, u32[]{:S(2)}) copy-start(f32[8,128,128]{2,1,0:T(8,128)S(1)} %convolution_add_fusion.5) | copy-start | bytes 1572868
  335.4 28.0 %copy-start.45 = (bf16[8,512,64]{1,2,0:T(8,128)(2,1)S(1)}, bf16[8,512,64]{1,2,0:T(8,128)(2,1)}, u32[]{:S(2)}) copy-start(bf16[8,512,64]{1,2,0:T(8,128)(2,1)} %get-tuple-element.93) | copy-start | bytes 1572868
  335.4 28.0 %copy-start.48 = (bf16[8,512,64]{1,2,0:T(8,128)(2,1)S(1)}, bf16[8,512,64]{1,2,0:T(8,128)(2,1)}, u32[]{:S(2)}) copy-start(bf16[8,512,64]{1,2,0:T(8,128)(2,1)} %get-tuple-element.94) | copy-start | bytes 1572868
  335.4 28.0 %copy-start.76 = (pred[512,512]{0,1:T(8,128)(4,1)S(1)}, pred[512,512]{0,1:T(8,128)(4,1)}, u32[]{:S(2)}) copy-start(pred[512,512]{0,1:T(8,128)(4,1)} %iota_compare_fusion) | copy-start | bytes 786436
  363.4 4.1 copy-start.88
  363.4 4.0 copy-start.89
  363.4 4.0 copy-start.90
  363.4 4.0 copy-start.91
  363.4 5.2 %copy-start.51 = (bf16[8,512,64]{1,2,0:T(8,128)(2,1)S(1)}, bf16[8,512,64]{1,2,0:T(8,128)(2,1)}, u32[]{:S(2)}) copy-start(bf16[8,512,64]{1,2,0:T(8,128)(2,1)} %get-tuple-element.91) | copy-start | bytes 1572868
  363.4 5.1 %copy-start.53 = (bf16[8,512,64]{1,2,0:T(8,128)(2,1)S(1)}, bf16[8,512,64]{1,2,0:T(8,128)(2,1)}, u32[]{:S(2)}) copy-start(bf16[8,512,64]{1,2,0:T(8,128)(2,1)} %get-tuple-element.92) | copy-start | bytes 1572868
  368.5 5.1 %copy-start.55 = (bf16[8,512,64]{1,2,0:T(8,128)(2,1)S(1)}, bf16[8,512,64]{1,2,0:T(8,128)(2,1)}, u32[]{:S(2)}) copy-start(bf16[8,512,64]{1,2,0:T(8,128)(2,1)} %get-tuple-element.89) | copy-start | bytes 1572868
  368.6 5.1 %copy-start.57 = (bf16[8,512,64]{1,2,0:T(8,128)(2,1)S(1)}, bf16[8,512,64]{1,2,0:T(8,128)(2,1)}, u32[]{:S(2)}) copy-start(bf16[8,512,64]{1,2,0:T(8,128)(2,1)} %get-tuple-element.90) | copy-start | bytes 1572868
  373.7 5.1 %copy-start.59 = (bf16[8,512,64]{1,2,0:T(8,128)(2,1)S(1)}, bf16[8,512,64]{1,2,0:T(8,128)(2,1)}, u32[]{:S(2)}) copy-start(bf16[8,512,64]{1,2,0:T(8,128)(2,1)} %get-tuple-element.87) | copy-start | bytes 1572868
  373.7 5.1 %copy-start.61 = (bf16[8,512,64]{1,2,0:T(8,128)(2,1)S(1)}, bf16[8,512,64]{1,2,0:T(8,128)(2,1)}, u32[]{:S(2)}) copy-start(bf16[8,512,64]{1,2,0:T(8,128)(2,1)} %get-tuple-element.88) | copy-start | bytes 1572868
  426.2 15.6 %copy-start.44 = (f32[8,512,128]{2,1,0:T(8,128)S(1)}, f32[8,512,128]{2,1,0:T(8,128)}, u32[]{:S(2)}) copy-start(f32[8,512,128]{2,1,0:T(8,128)} %convolution_add_fusion.1) | copy-start | bytes 6291460
  426.2 15.6 %copy-start.50 = (bf16[8,512,64]{1,2,0:T(8,128)(2,1)S(1)}, bf16[8,512,64]{1,2,0:T(8,128)(2,1)}, u32[]{:S(2)}) copy-start(bf16[8,512,64]{1,2,0:T(8,128)(2,1)} %get-tuple-element.94) | copy-start | bytes 1572868
  436.9 4.9 %copy-start.42 = (f32[8,512,128]{2,1,0:T(8,128)S(1)}, f32[8,512,128]{2,1,0:T(8,128)}, u32[]{:S(2)}) copy-start(f32[8,512,128]{2,1,0:T(8,128)} %convolution_add_fusion.3) | copy-start | bytes 6291460
  436.9 4.9 %copy-start.43 = (f32[8,512,128]{2,1,0:T(8,128)S(1)}, f32[8,512,128]{2,1,0:T(8,128)}, u32[]{:S(2)}) copy-start(f32[8,512,128]{2,1,0:T(8,128)} %convolution_add_fusion.2) | copy-start | bytes 6291460
  436.9 4.9 %copy-start.47 = (bf16[8,512,64]{1,2,0:T(8,128)(2,1)S(1)}, bf16[8,512,64]{1,2,0:T(8,128)(2,1)}, u32[]{:S(2)}) copy-start(bf16[8,512,64]{1,2,0:T(8,128)(2,1)} %get-tuple-element.93) | copy-start | bytes 1572868
  436.9 4.9 %copy-start.102 = (f32[8]{0:T(128)S(1)}, f32[8]{0:T(128)}, u32[]{:S(2)}) copy-start(f32[8]{0:T(128)} %get-tuple-element.27) | copy-start | bytes 100
  436.9 4.9 %copy-start.103 = (f32[8]{0:T(128)S(1)}, f32[8]{0:T(128)}, u32[]{:S(2)}) copy-start(f32[8]{0:T(128)} %get-tuple-element.28) | copy-start | bytes 100
  458.7 6.4 %copy-start.1 = (bf16[8,128,64]{1,2,0:T(8,128)(2,1)S(1)}, bf16[8,128,64]{1,2,0:T(8,128)(2,1)}, u32[]{:S(2)}) copy-start(bf16[8,128,64]{1,2,0:T(8,128)(2,1)} %param.10) | copy-start | bytes 393220
  (66 other events, 160.0 us)
Sparse Core Ops, SparseCore 0:
  383.4 53.3 all-gather.3

commit v2 on v1

v2 whole, which is shorter than its diff:
```python
import functools

import jax
import jax.numpy as jnp
from jax import lax
from jax.experimental import pallas as pl
from jax.experimental.pallas import tpu as pltpu
from jax.sharding import PartitionSpec as P

WIN = 64
QB = 128
INTERPRET = False


def passed_along(block, axis, distance):
    devices = range(lax.axis_size(axis))
    route = [(i - distance, i) for i in devices if i - distance in devices]
    return lax.ppermute(block, axis, route)


def exchange(rows, group, head_dim):
    moved = lax.all_to_all(rows, "seq", split_axis=1, concat_axis=0, tiled=True)
    return moved.reshape(group, head_dim, -1)


def feature_map(rows, weight):
    logits = jnp.einsum("hdt,hdf->htf", rows, weight, preferred_element_type=jnp.float32)
    halves = [jax.nn.softmax(logits, axis=-1), jax.nn.softmax(-logits, axis=-1)]
    return jnp.concatenate(halves, axis=-1).astype(jnp.bfloat16)


def _nt(a, b):
    return lax.dot_general(a, b, (((1,), (1,)), ((), ())), preferred_element_type=jnp.float32)


def attend_kernel(q_ref, k_ref, v_ref, pk_ref, fq_ref, st_ref, z_ref, g_ref, b_ref, o_ref):
    length = q_ref.shape[1]
    head_dim = q_ref.shape[2]
    feats = fq_ref.shape[2]
    half = feats // 2
    scale = jnp.sqrt(jnp.float32(head_dim))
    fq = fq_ref[0]
    g = g_ref[0]
    lane = lax.broadcasted_iota(jnp.int32, (QB, feats), 1)
    lo = lane < half
    tq = lax.broadcasted_iota(jnp.int32, (QB, 2 * QB), 0)
    wk = lax.broadcasted_iota(jnp.int32, (QB, 2 * QB), 1)
    win_keep = (wk > tq + WIN) & (wk <= tq + QB)
    lin_keep = wk <= tq + WIN
    neg = jnp.float32(-1e30)

    def step(i, carry):
        st, z = carry
        t0 = pl.multiple_of(i * QB, QB)
        q = q_ref[0, pl.ds(t0, QB), :]
        kw = k_ref[0, :, pl.ds(t0, 2 * QB)]
        vw = v_ref[0, :, pl.ds(t0, 2 * QB)]
        pkw = pk_ref[0, pl.ds(t0, 2 * QB), :]

        s = jnp.dot(q, kw, preferred_element_type=jnp.float32) / scale
        s = s + jnp.where(i == 0, b_ref[...], jnp.float32(0.0))
        s = jnp.where(win_keep, s, neg)
        top = jnp.max(s, axis=1, keepdims=True)
        p = jnp.exp(s - top)
        total = jnp.sum(p, axis=1, keepdims=True)
        window = _nt(p.astype(jnp.bfloat16), vw) / total

        logits = jnp.dot(q, fq, preferred_element_type=jnp.float32)
        m_lo = jnp.max(jnp.where(lo, logits, neg), axis=1, keepdims=True)
        m_hi = jnp.max(jnp.where(lo, neg, logits), axis=1, keepdims=True)
        e = jnp.exp(logits - jnp.where(lo, m_lo, m_hi))
        s_lo = jnp.sum(jnp.where(lo, e, 0.0), axis=1, keepdims=True)
        s_hi = jnp.sum(jnp.where(lo, 0.0, e), axis=1, keepdims=True)
        phi = (e / jnp.where(lo, s_lo, s_hi)).astype(jnp.bfloat16)

        aff = _nt(phi, pkw)
        aff = jnp.where(lin_keep, aff, jnp.float32(0.0)).astype(jnp.bfloat16)
        num = _nt(aff, vw)
        den = jnp.sum(aff.astype(jnp.float32), axis=1, keepdims=True)
        st_hi = st.astype(jnp.bfloat16)
        st_lo = (st - st_hi.astype(jnp.float32)).astype(jnp.bfloat16)
        num = num + _nt(phi, st_hi) + _nt(phi, st_lo)
        den = den + jnp.sum(phi.astype(jnp.float32) * z, axis=1, keepdims=True)
        linear = num / (den + 1.0)
        o_ref[pl.ds(t0, QB), :] = (g * window + (1.0 - g) * linear).astype(o_ref.dtype)

        vb = v_ref[0, :, pl.ds(t0, QB)]
        pkb = pk_ref[0, pl.ds(t0, QB), :]
        st = st + jnp.dot(vb, pkb, preferred_element_type=jnp.float32)
        z = z + jnp.sum(pkb.astype(jnp.float32), axis=0, keepdims=True)
        return st, z

    lax.fori_loop(0, length // QB, step, (st_ref[0], z_ref[0]))


def attend(q_tm, k_ext, v_ext, pk_ext, fq2, st0, z0, gate_rows, bias0):
    group, length, head_dim = q_tm.shape
    ext = k_ext.shape[2]
    feats = fq2.shape[2]
    return pl.pallas_call(
        attend_kernel,
        grid=(group,),
        in_specs=[
            pl.BlockSpec((1, length, head_dim), lambda h: (h, 0, 0)),
            pl.BlockSpec((1, head_dim, ext), lambda h: (h, 0, 0)),
            pl.BlockSpec((1, head_dim, ext), lambda h: (h, 0, 0)),
            pl.BlockSpec((1, ext, feats), lambda h: (h, 0, 0)),
            pl.BlockSpec((1, head_dim, feats), lambda h: (h, 0, 0)),
            pl.BlockSpec((1, head_dim, feats), lambda h: (h, 0, 0)),
            pl.BlockSpec((1, 1, feats), lambda h: (h, 0, 0)),
            pl.BlockSpec((1, 1, head_dim), lambda h: (h, 0, 0)),
            pl.BlockSpec((1, 2 * QB), lambda h: (0, 0)),
        ],
        out_specs=pl.BlockSpec((length, head_dim), lambda h: (0, h)),
        out_shape=jax.ShapeDtypeStruct((length, group * head_dim), jnp.bfloat16),
        interpret=INTERPRET,
    )(q_tm, k_ext, v_ext, pk_ext, fq2, st0, z0, gate_rows, bias0)


def local_part(q, k, v, before, earlier, feat_q, feat_k, prior_state, prior_norm, gate):
    group, head_dim, length = q.shape
    keep = earlier.astype(jnp.bfloat16)
    phi_k = feature_map(k, feat_k)
    phi_halo = feature_map(before[0], feat_k) * keep
    halo_state = jnp.einsum(
        "htf,hdt->hdf", phi_halo, before[1], preferred_element_type=jnp.float32
    )
    halo_norm = jnp.sum(phi_halo, axis=1, dtype=jnp.float32)
    feats = phi_k.shape[2]
    pad_k = jnp.zeros((group, head_dim, WIN), k.dtype)
    k_ext = jnp.concatenate([pad_k, before[0], k], axis=2)
    v_ext = jnp.concatenate([pad_k, before[1], v], axis=2)
    pk_ext = jnp.concatenate(
        [jnp.zeros((group, WIN, feats), phi_k.dtype), phi_halo, phi_k], axis=1
    )
    fq2 = jnp.concatenate([feat_q, -feat_q], axis=2)
    st0 = prior_state - halo_state
    z0 = (prior_norm - halo_norm)[:, None, :]
    gate_rows = jnp.broadcast_to(gate[:, None, None], (group, 1, head_dim)).astype(jnp.float32)
    halo_cols = (jnp.arange(2 * QB) >= WIN) & (jnp.arange(2 * QB) < 2 * WIN)
    bias0 = jnp.where(halo_cols & jnp.logical_not(earlier), jnp.float32(-1e30), jnp.float32(0.0))
    q_tm = q.transpose(0, 2, 1)
    return attend(q_tm, k_ext, v_ext, pk_ext, fq2, st0, z0, gate_rows, bias0[None, :])


def body(queries, keys, values, feat_q, feat_k, mix):
    shards = lax.axis_size("seq")
    place = lax.axis_index("seq")
    feature_rows = queries.shape[0]
    length = queries.shape[1] // shards
    group = feat_q.shape[0]
    head_dim = feat_q.shape[1]

    k = exchange(keys.reshape(feature_rows, shards, length), group, head_dim)
    v = exchange(values.reshape(feature_rows, shards, length), group, head_dim)
    q = exchange(queries.reshape(feature_rows, shards, length), group, head_dim)

    earlier = place > 0
    tails = jnp.stack([k[:, :, length - WIN :], v[:, :, length - WIN :]])
    before = passed_along(tails, "seq", 1)

    phi_own = feature_map(k, feat_k)
    own_state = jnp.einsum("htf,hdt->hdf", phi_own, v, preferred_element_type=jnp.float32)
    own_norm = jnp.sum(phi_own, axis=1, dtype=jnp.float32)
    gathered_state = lax.all_gather(own_state.astype(jnp.bfloat16), "seq")
    gathered_norm = lax.all_gather(own_norm.astype(jnp.bfloat16), "seq")
    below = (jnp.arange(shards) < place).astype(jnp.float32)
    prior_state = jnp.einsum(
        "s,shdf->hdf", below, gathered_state.astype(jnp.float32), precision=lax.Precision.HIGHEST
    )
    prior_norm = jnp.einsum(
        "s,shf->hf", below, gathered_norm.astype(jnp.float32), precision=lax.Precision.HIGHEST
    )
    gate = jax.nn.sigmoid(mix)
    return local_part(q, k, v, before, earlier, feat_q, feat_k, prior_state, prior_norm, gate)


def solution(mesh):
    return jax.shard_map(
        body,
        mesh=mesh,
        in_specs=(
            P(("heads", "seq"), None),
            P(("heads", "seq"), None),
            P(("heads", "seq"), None),
            P("heads", None, None),
            P("heads", None, None),
            P("heads"),
        ),
        out_specs=P("seq", "heads"),
        check_vma=False,
    )
```

time: 479 us -> 394 us (0.82)
  matrix products: 143 us -> 19.7 us
  local copies, waits for them, and re-layouts: 139 us -> 47.6 us
  Pallas kernels: 0 us -> 84.2 us
  waiting for transfers between devices: 59.7 us -> 120 us
  starting transfers between devices: 55.7 us -> 31.3 us
  blocking collectives: 24 us -> 31.2 us
    dot_general x40 -> x4, matrix products: 118 us -> 18.8 us  [the longest x1 8.23 us: body(): jnp.einsum('htf,hdt->hdf', phi_own, v, preferred_element_type=jnp.float32)]
    pallas_call x0 -> x1, Pallas kernels: none -> 84.2 us  [attend(): pl.pallas_call(attend_kernel, grid=(group,), in_specs=[pl.BlockSpec((1, l...]
    all_to_all x6 -> x3, waiting for transfers between devices: 51.3 us -> 120 us  [exchange(): moved = lax.all_to_all(rows, 'seq', split_axis=1, concat_axis=0, tiled=True)]
    slice x18 -> x0, local copies, waits for them, and re-layouts: 54.8 us -> none  [the longest x1 16.2 us: body(): q_parts = [exchange(qs[:, :, c, :], group, head_dim) for c in range(CHUNKS)]]
    sub x10 -> x2, matrix products: 24.4 us -> 0.83 us  [feature_map(): halves = [jax.nn.softmax(logits, axis=-1), jax.nn.softmax(-logits, axis=-1)]]
    all_to_all x6 -> x3, starting transfers between devices: 50.8 us -> 28.2 us  [exchange(): moved = lax.all_to_all(rows, 'seq', split_axis=1, concat_axis=0, tiled=True)]
    another operation x8 -> x0, local copies, waits for them, and re-layouts: 22.1 us -> none  [body(): qb = q.reshape(group, head_dim, nb, WIN)]
    unnamed x217 -> x9, local copies, waits for them, and re-layouts: 21 us -> 0.19 us
  transfers between devices with their start and end apart: 8 -> 5, of which waited for: 7 -> 3; matrix products, arithmetic and copies ran while one was open for 34% -> 22% of each run, Pallas kernels for 0% -> 0%
where the time goes in v2:
time: 394 us; the launch traced here: 387 us
  waiting for transfers between devices  120 us (30%)
  Pallas kernels  84.2 us (21%)
  local copies, waits for them, and re-layouts  47.6 us (12%)
  other arithmetic  39.7 us (10%)
  starting transfers between devices  31.3 us (8%)
  blocking collectives  31.2 us (8%)
  matrix products  19.7 us (5%)
  between operations  13.6 us (3%)
    all_to_all x3, waiting for transfers between devices, exchange(): moved = lax.all_to_all(rows, 'seq', split_axis=1, concat_axis=0, tiled=True)  120 us
    pallas_call x1, Pallas kernels, attend(): pl.pallas_call(attend_kernel, grid=(group,), in_specs=[pl.BlockSpec((1, l...  84.2 us
    all_gather x1, blocking collectives, body(): gathered_norm = lax.all_gather(own_norm.astype(jnp.bfloat16), 'seq')  31.2 us
    all_to_all x3, starting transfers between devices, exchange(): moved = lax.all_to_all(rows, 'seq', split_axis=1, concat_axis=0, tiled=True)  28.2 us
    another operation x3, other arithmetic  13.4 us
    dot_general x1, matrix products, body(): jnp.einsum('htf,hdt->hdf', phi_own, v, preferred_element_type=jnp.float32)  8.23 us
    concatenate x1, local copies, waits for them, and re-layouts, local_part(): v_ext = jnp.concatenate([pad_k, before[1], v], axis=2)  7.92 us
    concatenate x1, local copies, waits for them, and re-layouts, local_part(): k_ext = jnp.concatenate([pad_k, before[0], k], axis=2)  7.91 us
  transfers between devices with their start and end apart: 5, of which 3 were waited for; matrix products, arithmetic and copies ran while one was open for 22% of the time, Pallas kernels for 0%

profile of v2, /device:TPU:116, one launch (start us, length us, event | category | flops | bytes accessed | tf_op | source)
XLA Modules:
  0.0 387.2 jit_solution(2505190833627307441)
XLA Ops:
  6.5 0.0 copy-start
  6.5 4.7 %copy.80 = bf16[8,16,8,2048]{3,2,0,1:T(8,128)(2,1)} copy(bf16[8,16,8,2048]{3,2,1,0:T(8,128)(2,1)} %bitcast.72) | data formatting | bytes 8388608 | tf_op jit(solution)/shard_map/reshape | solution.py:154
  11.3 6.9 %all-to-all-start.1 = ((bf16[64,16,2048]{2,0,1:T(8,128)(2,1)}), bf16[64,16,2048]{2,0,1:T(8,128)(2,1)}, u32[]{:S(2)}, u32[]{:S(2)}) async-start(bf16[64,16,2048]{2,0,1:T(8,128)(2,1)} %bitcast.69), calls=%async_computation.1 | async-start | bytes 8388608 | tf_op jit(solution)/shard_map/all_to_all | solution.py:22
  18.2 4.8 %copy.79 = bf16[8,16,8,2048]{3,2,0,1:T(8,128)(2,1)} copy(bf16[8,16,8,2048]{3,2,1,0:T(8,128)(2,1)} %bitcast.73) | data formatting | bytes 8388608 | tf_op jit(solution)/shard_map/reshape | solution.py:155
  23.0 52.5 %all-to-all-done.1 = bf16[64,16,2048]{2,0,1:T(8,128)(2,1)} async-done(((bf16[64,16,2048]{2,0,1:T(8,128)(2,1)}), bf16[64,16,2048]{2,0,1:T(8,128)(2,1)}, u32[]{:S(2)}, u32[]{:S(2)}) %all-to-all-start.1) | async-done | bytes 4194336 | tf_op jit(solution)/shard_map/all_to_all | solution.py:22
  75.5 10.7 %all-to-all-start.2 = ((bf16[64,16,2048]{2,0,1:T(8,128)(2,1)}), bf16[64,16,2048]{2,0,1:T(8,128)(2,1)}, u32[]{:S(2)}, u32[]{:S(2)}) async-start(bf16[64,16,2048]{2,0,1:T(8,128)(2,1)} %bitcast.68), calls=%async_computation.2 | async-start | bytes 8388608 | tf_op jit(solution)/shard_map/all_to_all | solution.py:22
  86.2 0.0 all-gather.4.cloned.1.call-start
  86.3 0.0 copy-done
  86.3 4.8 %fusion.29 = (f32[8,2048]{1,0:T(8,128)S(1)}, f32[8,2048,64]{1,2,0:T(8,128)}) fusion(bf16[8,128,64]{1,2,0:T(8,128)(2,1)S(1)} %copy-done, bf16[8,128,2048]{2,1,0:T(8,128)(2,1)} %bitcast.6), kind=kOutput, calls=%fused_computation.52 | convolution fusion | flops 269467648 | bytes 8585216 | tf_op jit(solution)/shard_map/hdt,hdf->htf/dot_general | solution.py:27
  91.1 6.9 %copy.54 = f32[8,2048,64]{2,1,0:T(8,128)} copy(f32[8,2048,64]{1,2,0:T(8,128)} %get-tuple-element.12) | data formatting | bytes 8388608 | tf_op jit(solution)/shard_map/hdt,hdf->htf/dot_general | solution.py:27
  98.0 7.3 %fusion.3 = f32[8,2048]{1,0:T(8,128)S(1)} fusion(f32[8,2048,64]{2,1,0:T(8,128)} %copy.54, f32[8,2048]{1,0:T(8,128)S(1)} %get-tuple-element.11), kind=kLoop, calls=%fused_computation.7 | loop fusion | flops 2080768 | bytes 4325376 | tf_op jit(solution)/shard_map/reduce_sum | solution.py:28
  105.4 0.0 copy-done.1
  105.4 5.5 %fusion.28 = (f32[8,2048]{1,0:T(8,128)S(1)}, f32[8,2048,64]{2,1,0:T(8,128)}) fusion(f32[8,2048,64]{2,1,0:T(8,128)S(1)} %copy-done.1), kind=kOutput, calls=%fused_computation.51 | output fusion | flops 4194367 | bytes 8454144 | tf_op jit(solution)/shard_map/sub | solution.py:28
  110.8 6.9 %divide_convert_fusion = bf16[8,2048,64]{2,1,0:T(8,128)(2,1)} fusion(f32[8,2048,64]{2,1,0:T(8,128)} %get-tuple-element.10, f32[8,2048]{1,0:T(8,128)S(1)} %get-tuple-element.9), kind=kLoop, calls=%fused_computation.3 | loop fusion | flops 2097152 | bytes 6356992 | tf_op jit(solution)/shard_map/convert.2
  117.7 6.3 %divide_convert_fusion.1 = bf16[8,2048,64]{2,1,0:T(8,128)(2,1)} fusion(f32[8,2048,64]{2,1,0:T(8,128)S(1)} %copy-done.1, f32[8,2048]{1,0:T(8,128)S(1)} %fusion.3, f32[8,2048]{1,0:T(8,128)S(1)} %get-tuple-element.11), kind=kLoop, calls=%fused_computation.5 | loop fusion | flops 3145728 | bytes 6422528 | tf_op jit(solution)/shard_map/convert.1
  124.0 16.7 %all-to-all-done.2 = bf16[64,16,2048]{2,0,1:T(8,128)(2,1)} async-done(((bf16[64,16,2048]{2,0,1:T(8,128)(2,1)}), bf16[64,16,2048]{2,0,1:T(8,128)(2,1)}, u32[]{:S(2)}, u32[]{:S(2)}) %all-to-all-start.2) | async-done | bytes 4194336 | tf_op jit(solution)/shard_map/all_to_all | solution.py:22
  140.7 8.2 %fusion.11 = bf16[8,128,128]{1,2,0:T(8,128)(2,1)S(1)} fusion(bf16[8,128,2048]{2,1,0:T(8,128)(2,1)} %bitcast.10, bf16[8,2048,64]{2,1,0:T(8,128)(2,1)} %divide_convert_fusion, bf16[8,2048,64]{2,1,0:T(8,128)(2,1)} %divide_convert_fusion.1), kind=kOutput, calls=%fused_computation.21 | convolution fusion | flops 545390592 | bytes 8650752 | tf_op jit(solution)/shard_map/htf,hdt->hdf/dot_general | solution.py:163
  149.0 0.8 copy.59
  149.8 0.0 all-gather.4.cloned.1.call-update
  149.8 4.8 %copy.81 = bf16[8,16,8,2048]{3,2,0,1:T(8,128)(2,1)} copy(bf16[8,16,8,2048]{3,2,1,0:T(8,128)(2,1)} %bitcast.74) | data formatting | bytes 8388608 | tf_op jit(solution)/shard_map/reshape | solution.py:156
  154.6 10.6 %all-to-all-start = ((bf16[64,16,2048]{2,0,1:T(8,128)(2,1)}), bf16[64,16,2048]{2,0,1:T(8,128)(2,1)}, u32[]{:S(2)}, u32[]{:S(2)}) async-start(bf16[64,16,2048]{2,0,1:T(8,128)(2,1)} %bitcast.67), calls=%async_computation | async-start | bytes 8388608 | tf_op jit(solution)/shard_map/all_to_all | solution.py:22
  165.2 0.0 copy-done.2
  165.3 0.2 copy.56
  165.5 0.2 copy.57
  165.7 0.6 and_select_fusion.b_ref
  166.3 0.8 pad_maximum_fusion.3.fq_ref
  167.1 1.1 slice_bitcast_fusion.2
  168.2 1.1 slice_bitcast_fusion.3
  169.3 0.1 pad_maximum_fusion.2
  169.5 3.1 collective-permute-start
  172.5 4.7 %fusion.14 = bf16[8,128]{1,0:T(8,128)(2,1)S(1)} fusion(bf16[8,2048,64]{2,1,0:T(8,128)(2,1)} %divide_convert_fusion, bf16[8,2048,64]{2,1,0:T(8,128)(2,1)} %divide_convert_fusion.1), kind=kLoop, calls=%fused_computation.24 | loop fusion | flops 10484736 | bytes 4196352 | tf_op jit(solution)/shard_map/reduce_sum | solution.py:164
  177.2 50.5 %all-to-all-done = bf16[64,16,2048]{2,0,1:T(8,128)(2,1)} async-done(((bf16[64,16,2048]{2,0,1:T(8,128)(2,1)}), bf16[64,16,2048]{2,0,1:T(8,128)(2,1)}, u32[]{:S(2)}, u32[]{:S(2)}) %all-to-all-start) | async-done | bytes 4194336 | tf_op jit(solution)/shard_map/all_to_all | solution.py:22
  227.7 6.4 %copy.50 = bf16[8,128,2048]{1,2,0:T(8,128)(2,1)} copy(bf16[8,128,2048]{2,1,0:T(8,128)(2,1)} %bitcast.2) | data formatting | bytes 8388608 | tf_op jit(solution)/shard_map/reshape | solution.py:23
  234.2 31.2 %all-gather.1 = bf16[128,128]{1,0:T(8,128)(2,1)S(1)} all-gather(bf16[8,128]{1,0:T(8,128)(2,1)S(1)} %fusion.14), channel_id=3, replica_groups=mesh['heads'=8,'seq'=16] {'seq'}, dimensions={0}, use_global_device_ids=true | all-gather | bytes 34816 | tf_op jit(solution)/shard_map/all_gather | solution.py:166
  265.4 0.1 fusion.16
  265.6 0.0 collective-permute-done
  265.6 7.9 %concatenate.21.k_ref = bf16[8,128,2176]{2,1,0:T(8,128)(2,1)} concatenate(bf16[8,128,64]{2,1,0:T(8,128)(2,1)S(1)} %broadcast_in_dim.14, bf16[8,128,64]{2,1,0:T(8,128)(2,1)S(1)} %get-tuple-element.8, bf16[8,128,2048]{2,1,0:T(8,128)(2,1)} %bitcast.6), dimensions={2} | concatenate | bytes 8912896 | tf_op jit(solution)/shard_map/concatenate | solution.py:131
  273.6 7.9 %concatenate.22.v_ref = bf16[8,128,2176]{2,1,0:T(8,128)(2,1)} concatenate(bf16[8,128,64]{2,1,0:T(8,128)(2,1)S(1)} %broadcast_in_dim.14, bf16[8,128,64]{2,1,0:T(8,128)(2,1)S(1)} %get-tuple-element.7, bf16[8,128,2048]{2,1,0:T(8,128)(2,1)} %bitcast.10), dimensions={2} | concatenate | bytes 8912896 | tf_op jit(solution)/shard_map/concatenate | solution.py:132
  281.5 0.4 fusion.30
  281.9 0.4 fusion.31
  282.3 0.2 divide_convert_fusion.2
  282.5 0.1 convert_reduce_fusion
  282.7 0.6 sub.55
  283.3 6.5 %maximum_maximum_fusion.pk_ref = bf16[8,2176,128]{2,1,0:T(8,128)(2,1)} fusion(bf16[8,2048,64]{2,1,0:T(8,128)(2,1)} %divide_convert_fusion, bf16[8,2048,64]{2,1,0:T(8,128)(2,1)} %divide_convert_fusion.1, bf16[8,64,128]{2,1,0:T(8,128)(2,1)S(1)} %get-tuple-element.6, bf16[2176]{0:T(1024)(128)(2,1)S(1)} %pad.2.clone), kind=kLoop, calls=%fused_computation.10 | loop fusion | flops 17825792 | bytes 8786176 | tf_op jit(solution)/shard_map/concatenate | solution.py:133
  289.8 4.7 %fusion.7 = f32[1,8,128,128]{3,0,2,1:T(1,128)S(1)} fusion(bf16[16,8,128,128]{3,2,1,0:T(8,128)(2,1)} %bitcast.71, s32[]{:T(128)S(6)} %axis_index.12), kind=kOutput, calls=%fused_computation.15 | convolution fusion | flops 4194320 | bytes 4718596 | tf_op jit(solution)/shard_map/s,shdf->hdf/dot_general | solution.py:168
  294.5 1.0 convolution_subtract_fusion.st_ref
  295.5 0.7 broadcast_in_dim.17.g_ref
  296.2 84.2 %shard_map.64 = bf16[2048,1024]{1,0:T(8,128)(2,1)} custom-call(bf16[8,2048,128]{2,1,0:T(8,128)(2,1)} %bitcast.70, bf16[8,128,2176]{2,1,0:T(8,128)(2,1)} %concatenate.21.k_ref, bf16[8,128,2176]{2,1,0:T(8,128)(2,1)} %concatenate.22.v_ref, bf16[8,2176,128]{2,1,0:T(8,128)(2,1)} %maximum_maximum_fusion.pk_ref, bf16[8,128,128]{2,1,0:T(8,128)(2,1)} %pad_maximum_fusion.3.fq_ref, ...), custom_call_target="tpu_custom_call" | custom-call | tf_op jit(solution)/shard_map/pallas_call | solution.py:100
  (11 shorter events, 0.1 us)
Async XLA Ops:
  6.5 79.7 %copy-start = (bf16[8,128,64]{1,2,0:T(8,128)(2,1)S(1)}, bf16[8,128,64]{1,2,0:T(8,128)(2,1)}, u32[]{:S(2)}) copy-start(bf16[8,128,64]{1,2,0:T(8,128)(2,1)} %param.10) | copy-start | bytes 393220
  11.3 64.3 %all-to-all-start.1 = ((bf16[64,16,2048]{2,0,1:T(8,128)(2,1)}), bf16[64,16,2048]{2,0,1:T(8,128)(2,1)}, u32[]{:S(2)}, u32[]{:S(2)}) async-start(bf16[64,16,2048]{2,0,1:T(8,128)(2,1)} %bitcast.69), calls=%async_computation.1 | async-start | bytes 8388608 | tf_op jit(solution)/shard_map/all_to_all | solution.py:22
  75.5 65.2 %all-to-all-start.2 = ((bf16[64,16,2048]{2,0,1:T(8,128)(2,1)}), bf16[64,16,2048]{2,0,1:T(8,128)(2,1)}, u32[]{:S(2)}, u32[]{:S(2)}) async-start(bf16[64,16,2048]{2,0,1:T(8,128)(2,1)} %bitcast.68), calls=%async_computation.2 | async-start | bytes 8388608 | tf_op jit(solution)/shard_map/all_to_all | solution.py:22
  86.2 203.6 %all-gather.4.cloned.1.call-start = ((), (), s32[]{:S(2)}) async-start(), calls=%async_computation.3 | async-start | bytes 4456448 | tf_op jit(solution)/shard_map/all_gather | solution.py:165
  98.0 7.4 %copy-start.1 = (f32[8,2048,64]{2,1,0:T(8,128)S(1)}, f32[8,2048,64]{2,1,0:T(8,128)}, u32[]{:S(2)}) copy-start(f32[8,2048,64]{2,1,0:T(8,128)} %copy.54) | copy-start | bytes 12582916
  154.6 10.6 %copy-start.2 = (bf16[8,128,64]{1,2,0:T(8,128)(2,1)S(1)}, bf16[8,128,64]{1,2,0:T(8,128)(2,1)}, u32[]{:S(2)}) copy-start(bf16[8,128,64]{1,2,0:T(8,128)(2,1)} %param.9) | copy-start | bytes 393220
  154.6 12.5 %copy-start.3 = (f32[8]{0:T(128)S(1)}, f32[8]{0:T(128)}, u32[]{:S(2)}) copy-start(f32[8]{0:T(128)} %param.11) | copy-start | bytes 100
  154.6 73.1 %all-to-all-start = ((bf16[64,16,2048]{2,0,1:T(8,128)(2,1)}), bf16[64,16,2048]{2,0,1:T(8,128)(2,1)}, u32[]{:S(2)}, u32[]{:S(2)}) async-start(bf16[64,16,2048]{2,0,1:T(8,128)(2,1)} %bitcast.67), calls=%async_computation | async-start | bytes 8388608 | tf_op jit(solution)/shard_map/all_to_all | solution.py:22
  169.5 96.1 %collective-permute-start = (bf16[2,8,128,64]{3,2,1,0:T(8,128)(2,1)S(1)}, bf16[2,8,128,64]{3,2,1,0:T(8,128)(2,1)S(1)}, u32[]{:S(2)}, u32[]{:S(2)}) collective-permute-start(bf16[2,8,128,64]{3,2,1,0:T(8,128)(2,1)S(1)} %pad_maximum_fusion.2), channel_id=1, source_target_pairs={{0,1},{1,2},{2,3},{3,4},{4,5},{5,6},{6,7},{7,8},{8,9},{9,10},{10,1... | collective-permute-start | bytes 786440 | tf_op jit(solution)/shard_map/ppermute | solution.py:18
Sparse Core Ops, SparseCore 0:
  150.0 101.1 all-gather.3

commit v3 on v2

v3 whole, which is shorter than its diff:
```python
import functools

import jax
import jax.numpy as jnp
from jax import lax
from jax.experimental import pallas as pl
from jax.experimental.pallas import tpu as pltpu
from jax.sharding import PartitionSpec as P

WIN = 64
QB = 128
INTERPRET = False


def passed_along(block, axis, distance):
    devices = range(lax.axis_size(axis))
    route = [(i - distance, i) for i in devices if i - distance in devices]
    return lax.ppermute(block, axis, route)


def exchange(rows, group, head_dim):
    moved = lax.all_to_all(rows, "seq", split_axis=1, concat_axis=0, tiled=True)
    return moved.reshape(group, head_dim, -1)


def feature_map(rows, weight):
    logits = jnp.einsum("hdt,hdf->htf", rows, weight, preferred_element_type=jnp.float32)
    halves = [jax.nn.softmax(logits, axis=-1), jax.nn.softmax(-logits, axis=-1)]
    return jnp.concatenate(halves, axis=-1).astype(jnp.bfloat16)


def _nt(a, b):
    return lax.dot_general(a, b, (((1,), (1,)), ((), ())), preferred_element_type=jnp.float32)


def _tn(a, b):
    return lax.dot_general(a, b, (((0,), (0,)), ((), ())), preferred_element_type=jnp.float32)


def attend_kernel(
    q_ref, k_ref, v_ref, pk_ref, kh_ref, vh_ref, pkh_ref, fq_ref, st_ref, z_ref, g_ref, b_ref, o_ref
):
    length = q_ref.shape[2]
    head_dim = q_ref.shape[1]
    feats = fq_ref.shape[2]
    half = feats // 2
    inv_scale = 1.0 / jnp.sqrt(jnp.float32(head_dim))
    fq = fq_ref[0]
    g = g_ref[0]
    lane = lax.broadcasted_iota(jnp.int32, (QB, feats), 1)
    lo = lane < half
    tq = lax.broadcasted_iota(jnp.int32, (QB, 2 * QB), 0)
    wk = lax.broadcasted_iota(jnp.int32, (QB, 2 * QB), 1)
    win_keep = (wk > tq + WIN) & (wk <= tq + QB)
    lin_keep = wk <= tq + WIN
    neg = jnp.float32(-1e30)

    def step(t0, st, z, kw, vw, pkw, bias):
        q = q_ref[0, :, pl.ds(t0, QB)]
        s = _tn(q, kw) * inv_scale
        if bias is not None:
            s = s + bias
        s = jnp.where(win_keep, s, neg)
        top = jnp.max(s, axis=1, keepdims=True)
        p = jnp.exp(s - top)
        total = jnp.sum(p, axis=1, keepdims=True)
        window = _nt(p.astype(jnp.bfloat16), vw) * (1.0 / total)

        logits = _tn(q, fq)
        m_lo = jnp.max(jnp.where(lo, logits, neg), axis=1, keepdims=True)
        m_hi = jnp.max(jnp.where(lo, neg, logits), axis=1, keepdims=True)
        e = jnp.exp(logits - jnp.where(lo, m_lo, m_hi))
        s_lo = jnp.sum(jnp.where(lo, e, 0.0), axis=1, keepdims=True)
        s_hi = jnp.sum(jnp.where(lo, 0.0, e), axis=1, keepdims=True)
        phi = (e * jnp.where(lo, 1.0 / s_lo, 1.0 / s_hi)).astype(jnp.bfloat16)

        aff = _nt(phi, pkw)
        aff = jnp.where(lin_keep, aff, jnp.float32(0.0)).astype(jnp.bfloat16)
        num = _nt(aff, vw)
        den = jnp.sum(aff.astype(jnp.float32), axis=1, keepdims=True)
        st_hi = st.astype(jnp.bfloat16)
        st_lo = (st - st_hi.astype(jnp.float32)).astype(jnp.bfloat16)
        num = num + _nt(phi, st_hi) + _nt(phi, st_lo)
        den = den + jnp.sum(phi.astype(jnp.float32) * z, axis=1, keepdims=True)
        linear = num * (1.0 / (den + 1.0))
        o_ref[pl.ds(t0, QB), :] = (g * window + (1.0 - g) * linear).astype(o_ref.dtype)

        vb = vw[:, :QB]
        pkb = pkw[:QB]
        st = st + jnp.dot(vb, pkb, preferred_element_type=jnp.float32)
        z = z + jnp.sum(pkb.astype(jnp.float32), axis=0, keepdims=True)
        return st, z

    kw0 = jnp.concatenate([kh_ref[0], k_ref[0, :, pl.ds(0, QB)]], axis=1)
    vw0 = jnp.concatenate([vh_ref[0], v_ref[0, :, pl.ds(0, QB)]], axis=1)
    pkw0 = jnp.concatenate([pkh_ref[0], pk_ref[0, pl.ds(0, QB), :]], axis=0)
    carry = step(0, st_ref[0], z_ref[0], kw0, vw0, pkw0, b_ref[...])

    def loop(i, carry):
        t0 = pl.multiple_of(i * QB, QB)
        base = pl.multiple_of(t0 - QB, QB)
        kw = k_ref[0, :, pl.ds(base, 2 * QB)]
        vw = v_ref[0, :, pl.ds(base, 2 * QB)]
        pkw = pk_ref[0, pl.ds(base, 2 * QB), :]
        return step(t0, carry[0], carry[1], kw, vw, pkw, None)

    lax.fori_loop(1, length // QB, loop, carry)


def attend(q, k, v, pk, kh, vh, pkh, fq2, st0, z0, gate_rows, bias0):
    group, head_dim, length = q.shape
    feats = fq2.shape[2]
    return pl.pallas_call(
        attend_kernel,
        grid=(group,),
        in_specs=[
            pl.BlockSpec((1, head_dim, length), lambda h: (h, 0, 0)),
            pl.BlockSpec((1, head_dim, length), lambda h: (h, 0, 0)),
            pl.BlockSpec((1, head_dim, length), lambda h: (h, 0, 0)),
            pl.BlockSpec((1, length, feats), lambda h: (h, 0, 0)),
            pl.BlockSpec((1, head_dim, QB), lambda h: (h, 0, 0)),
            pl.BlockSpec((1, head_dim, QB), lambda h: (h, 0, 0)),
            pl.BlockSpec((1, QB, feats), lambda h: (h, 0, 0)),
            pl.BlockSpec((1, head_dim, feats), lambda h: (h, 0, 0)),
            pl.BlockSpec((1, head_dim, feats), lambda h: (h, 0, 0)),
            pl.BlockSpec((1, 1, feats), lambda h: (h, 0, 0)),
            pl.BlockSpec((1, 1, head_dim), lambda h: (h, 0, 0)),
            pl.BlockSpec((1, 2 * QB), lambda h: (0, 0)),
        ],
        out_specs=pl.BlockSpec((length, head_dim), lambda h: (0, h)),
        out_shape=jax.ShapeDtypeStruct((length, group * head_dim), jnp.bfloat16),
        interpret=INTERPRET,
    )(q, k, v, pk, kh, vh, pkh, fq2, st0, z0, gate_rows, bias0)


def local_part(q, k, v, before, earlier, feat_q, feat_k, prior_state, prior_norm, gate):
    group, head_dim, length = q.shape
    keep = earlier.astype(jnp.bfloat16)
    phi_k = feature_map(k, feat_k)
    phi_halo = feature_map(before[0], feat_k) * keep
    halo_state = jnp.einsum(
        "htf,hdt->hdf", phi_halo, before[1], preferred_element_type=jnp.float32
    )
    halo_norm = jnp.sum(phi_halo, axis=1, dtype=jnp.float32)
    feats = phi_k.shape[2]
    pad_k = jnp.zeros((group, head_dim, QB - WIN), k.dtype)
    kh = jnp.concatenate([pad_k, before[0]], axis=2)
    vh = jnp.concatenate([pad_k, before[1]], axis=2)
    pkh = jnp.concatenate([jnp.zeros((group, QB - WIN, feats), phi_k.dtype), phi_halo], axis=1)
    fq2 = jnp.concatenate([feat_q, -feat_q], axis=2)
    st0 = prior_state - halo_state
    z0 = (prior_norm - halo_norm)[:, None, :]
    gate_rows = jnp.broadcast_to(gate[:, None, None], (group, 1, head_dim)).astype(jnp.float32)
    halo_cols = (jnp.arange(2 * QB) >= QB - WIN) & (jnp.arange(2 * QB) < QB)
    bias0 = jnp.where(halo_cols & jnp.logical_not(earlier), jnp.float32(-1e30), jnp.float32(0.0))
    return attend(q, k, v, phi_k, kh, vh, pkh, fq2, st0, z0, gate_rows, bias0[None, :])


def body(queries, keys, values, feat_q, feat_k, mix):
    shards = lax.axis_size("seq")
    place = lax.axis_index("seq")
    feature_rows = queries.shape[0]
    length = queries.shape[1] // shards
    group = feat_q.shape[0]
    head_dim = feat_q.shape[1]

    k = exchange(keys.reshape(feature_rows, shards, length), group, head_dim)
    v = exchange(values.reshape(feature_rows, shards, length), group, head_dim)
    q = exchange(queries.reshape(feature_rows, shards, length), group, head_dim)

    earlier = place > 0
    tails = jnp.stack([k[:, :, length - WIN :], v[:, :, length - WIN :]])
    before = passed_along(tails, "seq", 1)

    phi_own = feature_map(k, feat_k)
    own_state = jnp.einsum("htf,hdt->hdf", phi_own, v, preferred_element_type=jnp.float32)
    own_norm = jnp.sum(phi_own, axis=1, dtype=jnp.float32)
    own = jnp.concatenate(
        [own_state.reshape(group * head_dim, -1), own_norm], axis=0
    ).astype(jnp.bfloat16)
    gathered = lax.all_gather(own, "seq").astype(jnp.float32)
    below = (jnp.arange(shards) < place).astype(jnp.float32)
    prior = jnp.einsum("s,srf->rf", below, gathered, precision=lax.Precision.HIGHEST)
    prior_state = prior[: group * head_dim].reshape(own_state.shape)
    prior_norm = prior[group * head_dim :]
    gate = jax.nn.sigmoid(mix)
    return local_part(q, k, v, before, earlier, feat_q, feat_k, prior_state, prior_norm, gate)


def solution(mesh):
    return jax.shard_map(
        body,
        mesh=mesh,
        in_specs=(
            P(("heads", "seq"), None),
            P(("heads", "seq"), None),
            P(("heads", "seq"), None),
            P("heads", None, None),
            P("heads", None, None),
            P("heads"),
        ),
        out_specs=P("seq", "heads"),
        check_vma=False,
    )
```

time: 394 us -> 357 us (0.906)
  blocking collectives: 31.2 us -> 0 us
  waiting for transfers between devices: 120 us -> 144 us
  local copies, waits for them, and re-layouts: 47.6 us -> 27 us
  other arithmetic: 39.7 us -> 30.2 us
  Pallas kernels: 84.2 us -> 89.8 us
  matrix products: 19.7 us -> 14.4 us
    ppermute x1, waiting for transfers between devices: 0.01 us -> 75.5 us  [passed_along(): return lax.ppermute(block, axis, route)]
    all_to_all x3, waiting for transfers between devices: 120 us -> 68.2 us  [exchange(): moved = lax.all_to_all(rows, 'seq', split_axis=1, concat_axis=0, tiled=True)]
    all_gather x1 -> x0, blocking collectives: 31.2 us -> none  [body(): gathered_norm = lax.all_gather(own_norm.astype(jnp.bfloat16), 'seq')]
    concatenate x3, local copies, waits for them, and re-layouts: 15.8 us -> 2.43 us  [the longest x1 0.85 us: local_part(): kh = jnp.concatenate([pad_k, before[0]], axis=2)]
    reshape x1 -> x0, local copies, waits for them, and re-layouts: 6.44 us -> none  [exchange(): return moved.reshape(group, head_dim, -1)]
    concatenate x1, other arithmetic: 6.54 us -> 0.71 us  [body(): jnp.concatenate([own_state.reshape(group * head_dim, -1), own_norm], axis=0)]
    pallas_call x1, Pallas kernels: 84.2 us -> 89.8 us  [attend(): pl.pallas_call(attend_kernel, grid=(group,), in_specs=[pl.BlockSpec((1, h...]
  transfers between devices with their start and end apart: 5 -> 5, of which waited for: 3 -> 3; matrix products, arithmetic and copies ran while one was open for 22% -> 17% of each run, Pallas kernels for 0% -> 0%
where the time goes in v3:
time: 357 us; the launch traced here: 350 us
  waiting for transfers between devices  144 us (40%)
  Pallas kernels  89.8 us (25%)
  starting transfers between devices  31.3 us (9%)
  other arithmetic  30.2 us (8%)
  local copies, waits for them, and re-layouts  27 us (8%)
  matrix products  14.4 us (4%)
  between operations  13.6 us (4%)
    pallas_call x1, Pallas kernels, attend(): pl.pallas_call(attend_kernel, grid=(group,), in_specs=[pl.BlockSpec((1, h...  89.8 us
    ppermute x1, waiting for transfers between devices, passed_along(): return lax.ppermute(block, axis, route)  75.5 us
    all_to_all x3, waiting for transfers between devices, exchange(): moved = lax.all_to_all(rows, 'seq', split_axis=1, concat_axis=0, tiled=True)  68.2 us
    all_to_all x3, starting transfers between devices, exchange(): moved = lax.all_to_all(rows, 'seq', split_axis=1, concat_axis=0, tiled=True)  28.2 us
    another operation x3, other arithmetic  10.4 us
    reduce_sum x1, other arithmetic, feature_map(): halves = [jax.nn.softmax(logits, axis=-1), jax.nn.softmax(-logits, axis=-1)]  7.34 us
  transfers between devices with their start and end apart: 5, of which 3 were waited for; matrix products, arithmetic and copies ran while one was open for 17% of the time, Pallas kernels for 0%

profile of v3, /device:TPU:116, one launch (start us, length us, event | category | flops | bytes accessed | tf_op | source)
XLA Modules:
  0.0 350.0 jit_solution(11794381989438670759)
XLA Ops:
  6.5 0.0 copy-start
  6.5 4.8 %copy.47 = bf16[8,16,8,2048]{3,2,0,1:T(8,128)(2,1)} copy(bf16[8,16,8,2048]{3,2,1,0:T(8,128)(2,1)} %bitcast.64) | data formatting | bytes 8388608 | tf_op jit(solution)/shard_map/reshape | solution.py:167
  11.4 6.9 %all-to-all-start.1 = ((bf16[64,16,2048]{2,0,1:T(8,128)(2,1)}), bf16[64,16,2048]{2,0,1:T(8,128)(2,1)}, u32[]{:S(2)}, u32[]{:S(2)}) async-start(bf16[64,16,2048]{2,0,1:T(8,128)(2,1)} %bitcast.63), calls=%async_computation.1 | async-start | bytes 8388608 | tf_op jit(solution)/shard_map/all_to_all | solution.py:22
  18.3 4.7 %copy.46 = bf16[8,16,8,2048]{3,2,0,1:T(8,128)(2,1)} copy(bf16[8,16,8,2048]{3,2,1,0:T(8,128)(2,1)} %bitcast.65) | data formatting | bytes 8388608 | tf_op jit(solution)/shard_map/reshape | solution.py:168
  23.0 52.6 %all-to-all-done.1 = bf16[64,16,2048]{2,0,1:T(8,128)(2,1)} async-done(((bf16[64,16,2048]{2,0,1:T(8,128)(2,1)}), bf16[64,16,2048]{2,0,1:T(8,128)(2,1)}, u32[]{:S(2)}, u32[]{:S(2)}) %all-to-all-start.1) | async-done | bytes 4194336 | tf_op jit(solution)/shard_map/all_to_all | solution.py:22
  75.6 10.7 %all-to-all-start.2 = ((bf16[64,16,2048]{2,0,1:T(8,128)(2,1)}), bf16[64,16,2048]{2,0,1:T(8,128)(2,1)}, u32[]{:S(2)}, u32[]{:S(2)}) async-start(bf16[64,16,2048]{2,0,1:T(8,128)(2,1)} %bitcast.62), calls=%async_computation.2 | async-start | bytes 8388608 | tf_op jit(solution)/shard_map/all_to_all | solution.py:22
  86.3 0.0 all-gather.2.cloned.1.call-start
  86.3 0.0 copy-done
  86.4 4.9 %fusion.21 = (f32[8,2048]{1,0:T(8,128)S(1)}, f32[8,2048,64]{1,2,0:T(8,128)}) fusion(bf16[8,128,64]{1,2,0:T(8,128)(2,1)S(1)} %copy-done, bf16[8,128,2048]{2,1,0:T(8,128)(2,1)} %bitcast.5.k_ref), kind=kOutput, calls=%fused_computation.45 | convolution fusion | flops 269467648 | bytes 8585216 | tf_op jit(solution)/shard_map/hdt,hdf->htf/dot_general | solution.py:27
  91.3 6.9 %copy.28 = f32[8,2048,64]{2,1,0:T(8,128)} copy(f32[8,2048,64]{1,2,0:T(8,128)} %get-tuple-element.14) | data formatting | bytes 8388608 | tf_op jit(solution)/shard_map/hdt,hdf->htf/dot_general | solution.py:27
  98.2 0.0 copy-start.1
  98.2 7.3 %fusion.3 = f32[8,2048]{1,0:T(8,128)S(1)} fusion(f32[8,2048,64]{2,1,0:T(8,128)} %copy.28, f32[8,2048]{1,0:T(8,128)S(1)} %get-tuple-element.13), kind=kLoop, calls=%fused_computation.7 | loop fusion | flops 2080768 | bytes 4325376 | tf_op jit(solution)/shard_map/reduce_sum | solution.py:28
  105.5 0.0 copy-done.1
  105.6 5.5 %fusion.20 = (f32[8,2048]{1,0:T(8,128)S(1)}, f32[8,2048,64]{2,1,0:T(8,128)}) fusion(f32[8,2048,64]{2,1,0:T(8,128)S(1)} %copy-done.1), kind=kOutput, calls=%fused_computation.44 | output fusion | flops 4194367 | bytes 8454144 | tf_op jit(solution)/shard_map/sub | solution.py:28
  111.0 5.2 %divide_convert_fusion = bf16[8,2048,64]{2,1,0:T(8,128)(2,1)S(1)} fusion(f32[8,2048,64]{2,1,0:T(8,128)} %get-tuple-element.12, f32[8,2048]{1,0:T(8,128)S(1)} %get-tuple-element.11), kind=kLoop, calls=%fused_computation.3 | loop fusion | flops 2097152 | bytes 6356992 | tf_op jit(solution)/shard_map/convert.8
  116.3 5.0 %divide_convert_fusion.1 = bf16[8,2048,64]{2,1,0:T(8,128)(2,1)S(1)} fusion(f32[8,2048,64]{2,1,0:T(8,128)S(1)} %copy-done.1, f32[8,2048]{1,0:T(8,128)S(1)} %fusion.3, f32[8,2048]{1,0:T(8,128)S(1)} %get-tuple-element.13), kind=kLoop, calls=%fused_computation.5 | loop fusion | flops 3145728 | bytes 6422528 | tf_op jit(solution)/shard_map/convert.7
  121.3 3.9 %fusion.19 = (bf16[8,128]{1,0:T(8,128)(2,1)S(1)}, bf16[8,2048,128]{2,1,0:T(8,128)(2,1)}) fusion(bf16[8,2048,64]{2,1,0:T(8,128)(2,1)S(1)} %divide_convert_fusion, bf16[8,2048,64]{2,1,0:T(8,128)(2,1)S(1)} %divide_convert_fusion.1), kind=kLoop, calls=%fused_computation.43 | loop fusion | flops 10484736 | bytes 8390656 | tf_op jit(solution)/shard_map/reduce_sum | solution.py:177
  125.2 15.7 %all-to-all-done.2 = bf16[64,16,2048]{2,0,1:T(8,128)(2,1)} async-done(((bf16[64,16,2048]{2,0,1:T(8,128)(2,1)}), bf16[64,16,2048]{2,0,1:T(8,128)(2,1)}, u32[]{:S(2)}, u32[]{:S(2)}) %all-to-all-start.2) | async-done | bytes 4194336 | tf_op jit(solution)/shard_map/all_to_all | solution.py:22
  140.8 4.7 %convolution_convert_fusion = bf16[8,128,128]{1,2,0:T(8,128)(2,1)S(1)} fusion(bf16[8,128,2048]{2,1,0:T(8,128)(2,1)} %bitcast.8.v_ref, bf16[8,2048,128]{2,1,0:T(8,128)(2,1)} %get-tuple-element.8.pk_ref), kind=kOutput, calls=%fused_computation.19 | convolution fusion | flops 537001984 | bytes 8650752 | tf_op jit(solution)/shard_map/htf,hdt->hdf/dot_general | solution.py:176
  145.5 0.7 pad_maximum_fusion.2
  146.3 0.0 all-gather.2.cloned.1.call-update
  146.3 4.8 %copy.48 = bf16[8,16,8,2048]{3,2,0,1:T(8,128)(2,1)} copy(bf16[8,16,8,2048]{3,2,1,0:T(8,128)(2,1)} %bitcast.66) | data formatting | bytes 8388608 | tf_op jit(solution)/shard_map/reshape | solution.py:169
  151.1 0.0 copy-start.2
  151.1 10.6 %all-to-all-start = ((bf16[64,16,2048]{2,0,1:T(8,128)(2,1)}), bf16[64,16,2048]{2,0,1:T(8,128)(2,1)}, u32[]{:S(2)}, u32[]{:S(2)}) async-start(bf16[64,16,2048]{2,0,1:T(8,128)(2,1)} %bitcast.61), calls=%async_computation | async-start | bytes 8388608 | tf_op jit(solution)/shard_map/all_to_all | solution.py:22
  161.7 0.0 copy-done.2
  161.7 0.2 copy.31
  161.9 0.2 copy.32
  162.1 0.9 pad_maximum_fusion.3.fq_ref
  162.9 1.1 slice_bitcast_fusion.2
  164.0 1.1 slice_bitcast_fusion.3
  165.1 0.1 pad_maximum_fusion.1
  165.2 3.1 collective-permute-start
  168.3 0.6 and_select_fusion.b_ref
  168.9 0.0 copy-done.3
  169.0 75.5 %collective-permute-done = bf16[2,8,128,64]{3,2,1,0:T(8,128)(2,1)S(1)} collective-permute-done((bf16[2,8,128,64]{3,2,1,0:T(8,128)(2,1)S(1)}, bf16[2,8,128,64]{3,2,1,0:T(8,128)(2,1)S(1)}, u32[]{:S(2)}, u32[]{:S(2)}) %collective-permute-start) | collective-permute-done | bytes 262176 | tf_op jit(solution)/shard_map/ppermute | solution.py:18
  244.5 0.4 fusion.22
  244.9 0.4 fusion.23
  245.3 0.2 divide_convert_fusion.2
  245.5 0.1 convert_reduce_fusion
  245.6 0.7 concatenate.40.pkh_ref
  246.4 0.9 concatenate.37.kh_ref
  247.3 0.8 concatenate.38.vh_ref
  248.1 2.9 fusion.7
  251.1 0.6 slice_subtract_fusion
  251.7 1.0 convolution_subtract_fusion.st_ref
  252.7 0.0 all-to-all-done
  252.7 0.7 broadcast_in_dim.11.g_ref
  253.3 89.8 %shard_map.64 = bf16[2048,1024]{1,0:T(8,128)(2,1)} custom-call(bf16[8,128,2048]{2,1,0:T(8,128)(2,1)} %bitcast.2.q_ref, bf16[8,128,2048]{2,1,0:T(8,128)(2,1)} %bitcast.5.k_ref, bf16[8,128,2048]{2,1,0:T(8,128)(2,1)} %bitcast.8.v_ref, bf16[8,2048,128]{2,1,0:T(8,128)(2,1)} %get-tuple-element.8.pk_ref, bf16[8,128,128]{2,1,0:T(8,128)(2,1)} %concatenate.37.kh_ref, ...), custom_call_target="tpu_custom_call" | custom-call | tf_op jit(solution)/shard_map/pallas_call | solution.py:113
  (6 shorter events, 0.1 us)
Async XLA Ops:
  6.5 79.8 %copy-start = (bf16[8,128,64]{1,2,0:T(8,128)(2,1)S(1)}, bf16[8,128,64]{1,2,0:T(8,128)(2,1)}, u32[]{:S(2)}) copy-start(bf16[8,128,64]{1,2,0:T(8,128)(2,1)} %param.10) | copy-start | bytes 393220
  11.4 64.3 %all-to-all-start.1 = ((bf16[64,16,2048]{2,0,1:T(8,128)(2,1)}), bf16[64,16,2048]{2,0,1:T(8,128)(2,1)}, u32[]{:S(2)}, u32[]{:S(2)}) async-start(bf16[64,16,2048]{2,0,1:T(8,128)(2,1)} %bitcast.63), calls=%async_computation.1 | async-start | bytes 8388608 | tf_op jit(solution)/shard_map/all_to_all | solution.py:22
  75.6 65.2 %all-to-all-start.2 = ((bf16[64,16,2048]{2,0,1:T(8,128)(2,1)}), bf16[64,16,2048]{2,0,1:T(8,128)(2,1)}, u32[]{:S(2)}, u32[]{:S(2)}) async-start(bf16[64,16,2048]{2,0,1:T(8,128)(2,1)} %bitcast.62), calls=%async_computation.2 | async-start | bytes 8388608 | tf_op jit(solution)/shard_map/all_to_all | solution.py:22
  86.3 161.8 %all-gather.2.cloned.1.call-start = ((), (), s32[]{:S(2)}) async-start(), calls=%async_computation.3 | async-start | bytes 4491264 | tf_op jit(solution)/shard_map/all_gather | solution.py:181
  98.2 7.4 %copy-start.1 = (f32[8,2048,64]{2,1,0:T(8,128)S(1)}, f32[8,2048,64]{2,1,0:T(8,128)}, u32[]{:S(2)}) copy-start(f32[8,2048,64]{2,1,0:T(8,128)} %copy.28) | copy-start | bytes 12582916
  151.1 10.6 %copy-start.2 = (bf16[8,128,64]{1,2,0:T(8,128)(2,1)S(1)}, bf16[8,128,64]{1,2,0:T(8,128)(2,1)}, u32[]{:S(2)}) copy-start(bf16[8,128,64]{1,2,0:T(8,128)(2,1)} %param.9) | copy-start | bytes 393220
  151.1 17.9 %copy-start.3 = (f32[8]{0:T(128)S(1)}, f32[8]{0:T(128)}, u32[]{:S(2)}) copy-start(f32[8]{0:T(128)} %param.11) | copy-start | bytes 100
  151.1 101.6 %all-to-all-start = ((bf16[64,16,2048]{2,0,1:T(8,128)(2,1)}), bf16[64,16,2048]{2,0,1:T(8,128)(2,1)}, u32[]{:S(2)}, u32[]{:S(2)}) async-start(bf16[64,16,2048]{2,0,1:T(8,128)(2,1)} %bitcast.61), calls=%async_computation | async-start | bytes 8388608 | tf_op jit(solution)/shard_map/all_to_all | solution.py:22
  165.2 79.2 %collective-permute-start = (bf16[2,8,128,64]{3,2,1,0:T(8,128)(2,1)S(1)}, bf16[2,8,128,64]{3,2,1,0:T(8,128)(2,1)S(1)}, u32[]{:S(2)}, u32[]{:S(2)}) collective-permute-start(bf16[2,8,128,64]{3,2,1,0:T(8,128)(2,1)S(1)} %pad_maximum_fusion.1), channel_id=1, source_target_pairs={{0,1},{1,2},{2,3},{3,4},{4,5},{5,6},{6,7},{7,8},{8,9},{9,10},{10,1... | collective-permute-start | bytes 786440 | tf_op jit(solution)/shard_map/ppermute | solution.py:18
Sparse Core Ops, SparseCore 0:
  146.4 101.2 all-gather.1

commit v4 on v3

v4 whole, which is shorter than its diff:
```python
import functools

import jax
import jax.numpy as jnp
from jax import lax
from jax.experimental import pallas as pl
from jax.experimental.pallas import tpu as pltpu
from jax.sharding import PartitionSpec as P

WIN = 64
QB = 128
HEADS_PER_STEP = 2
INTERPRET = False


def passed_along(block, axis, distance):
    devices = range(lax.axis_size(axis))
    route = [(i - distance, i) for i in devices if i - distance in devices]
    return lax.ppermute(block, axis, route)


def exchange(rows, group, head_dim):
    moved = lax.all_to_all(rows, "seq", split_axis=1, concat_axis=0, tiled=True)
    return moved.reshape(group, head_dim, -1)


def feature_map(rows, weight):
    logits = jnp.einsum("hdt,hdf->htf", rows, weight, preferred_element_type=jnp.float32)
    halves = [jax.nn.softmax(logits, axis=-1), jax.nn.softmax(-logits, axis=-1)]
    return jnp.concatenate(halves, axis=-1).astype(jnp.bfloat16)


def _nt(a, b):
    return lax.dot_general(a, b, (((1,), (1,)), ((), ())), preferred_element_type=jnp.float32)


def _tn(a, b):
    return lax.dot_general(a, b, (((0,), (0,)), ((), ())), preferred_element_type=jnp.float32)


def attend_kernel(
    q_ref, k_ref, v_ref, pk_ref, kh_ref, vh_ref, pkh_ref, fq_ref, st_ref, z_ref, g_ref, b_ref, o_ref
):
    heads = q_ref.shape[0]
    length = q_ref.shape[2]
    head_dim = q_ref.shape[1]
    feats = fq_ref.shape[1]
    half = feats // 2
    inv_scale = 1.0 / jnp.sqrt(jnp.float32(head_dim))
    row = lax.broadcasted_iota(jnp.int32, (feats, QB), 0)
    lo = row < half
    wk = lax.broadcasted_iota(jnp.int32, (2 * QB, QB), 0)
    tq = lax.broadcasted_iota(jnp.int32, (2 * QB, QB), 1)
    win_keep = (wk > tq + WIN) & (wk <= tq + QB)
    lin_keep = wk <= tq + WIN
    zrow = lax.broadcasted_iota(jnp.int32, (8, feats), 0)
    neg = jnp.float32(-1e30)

    def step(hh, t0, st, z, kw, vw, pkw, bias):
        q = q_ref[hh, :, pl.ds(t0, QB)]
        g = g_ref[hh]
        s = jnp.dot(kw, q, preferred_element_type=jnp.float32) * inv_scale
        if bias is not None:
            s = s + bias
        s = jnp.where(win_keep, s, neg)
        top = jnp.max(s, axis=0, keepdims=True)
        p = jnp.exp(s - top)
        total = jnp.sum(p, axis=0, keepdims=True)
        window = jnp.dot(vw, p.astype(jnp.bfloat16), preferred_element_type=jnp.float32) * (1.0 / total)

        logits = jnp.dot(fq_ref[hh], q, preferred_element_type=jnp.float32)
        m_lo = jnp.max(logits[:half], axis=0, keepdims=True)
        m_hi = jnp.max(logits[half:], axis=0, keepdims=True)
        e = jnp.exp(logits - jnp.where(lo, m_lo, m_hi))
        s_lo = jnp.sum(e[:half], axis=0, keepdims=True)
        s_hi = jnp.sum(e[half:], axis=0, keepdims=True)
        phi = (e * jnp.where(lo, 1.0 / s_lo, 1.0 / s_hi)).astype(jnp.bfloat16)

        aff = jnp.dot(pkw, phi, preferred_element_type=jnp.float32)
        aff = jnp.where(lin_keep, aff, jnp.float32(0.0)).astype(jnp.bfloat16)
        num = jnp.dot(vw, aff, preferred_element_type=jnp.float32)
        den = jnp.sum(aff.astype(jnp.float32), axis=0, keepdims=True)
        st_hi = st.astype(jnp.bfloat16)
        st_lo = (st - st_hi.astype(jnp.float32)).astype(jnp.bfloat16)
        num = num + jnp.dot(st_hi, phi, preferred_element_type=jnp.float32)
        num = num + jnp.dot(st_lo, phi, preferred_element_type=jnp.float32)
        z_hi = z.astype(jnp.bfloat16)
        z_lo = (z - z_hi.astype(jnp.float32)).astype(jnp.bfloat16)
        zz = jnp.where(zrow == 0, z_hi, jnp.where(zrow == 1, z_lo, jnp.zeros_like(z_lo)))
        cross = jnp.dot(zz, phi, preferred_element_type=jnp.float32)
        den = den + (cross[0:1] + cross[1:2])
        linear = num * (1.0 / (den + 1.0))
        out = g * window + (1.0 - g) * linear
        o_ref[pl.ds(t0, QB), pl.ds(hh * head_dim, head_dim)] = out.T.astype(o_ref.dtype)

        vb = vw[:, :QB]
        pkb = pkw[:QB]
        st = st + jnp.dot(vb, pkb, preferred_element_type=jnp.float32)
        z = z + jnp.sum(pkb.astype(jnp.float32), axis=0, keepdims=True)
        return st, z

    carry = []
    for hh in range(heads):
        kw0 = jnp.concatenate([kh_ref[hh], k_ref[hh, pl.ds(0, QB), :]], axis=0)
        vw0 = jnp.concatenate([vh_ref[hh], v_ref[hh, :, pl.ds(0, QB)]], axis=1)
        pkw0 = jnp.concatenate([pkh_ref[hh], pk_ref[hh, pl.ds(0, QB), :]], axis=0)
        carry.append(step(hh, 0, st_ref[hh], z_ref[hh][0:1], kw0, vw0, pkw0, b_ref[...]))

    def loop(i, carry):
        t0 = pl.multiple_of(i * QB, QB)
        base = pl.multiple_of(t0 - QB, QB)
        out = []
        for hh in range(heads):
            kw = k_ref[hh, pl.ds(base, 2 * QB), :]
            vw = v_ref[hh, :, pl.ds(base, 2 * QB)]
            pkw = pk_ref[hh, pl.ds(base, 2 * QB), :]
            out.append(step(hh, t0, carry[hh][0], carry[hh][1], kw, vw, pkw, None))
        return tuple(out)

    lax.fori_loop(1, length // QB, loop, tuple(carry))


def attend(q, k_tm, v, pk, kh, vh, pkh, fq_t, st0, z0, gate_rows, bias0):
    group, head_dim, length = q.shape
    feats = fq_t.shape[1]
    hb = HEADS_PER_STEP
    return pl.pallas_call(
        attend_kernel,
        grid=(group // hb,),
        in_specs=[
            pl.BlockSpec((hb, head_dim, length), lambda h: (h, 0, 0)),
            pl.BlockSpec((hb, length, head_dim), lambda h: (h, 0, 0)),
            pl.BlockSpec((hb, head_dim, length), lambda h: (h, 0, 0)),
            pl.BlockSpec((hb, length, feats), lambda h: (h, 0, 0)),
            pl.BlockSpec((hb, QB, head_dim), lambda h: (h, 0, 0)),
            pl.BlockSpec((hb, head_dim, QB), lambda h: (h, 0, 0)),
            pl.BlockSpec((hb, QB, feats), lambda h: (h, 0, 0)),
            pl.BlockSpec((hb, feats, head_dim), lambda h: (h, 0, 0)),
            pl.BlockSpec((hb, head_dim, feats), lambda h: (h, 0, 0)),
            pl.BlockSpec((hb, 8, feats), lambda h: (h, 0, 0)),
            pl.BlockSpec((hb, 1, QB), lambda h: (h, 0, 0)),
            pl.BlockSpec((2 * QB, QB), lambda h: (0, 0)),
        ],
        out_specs=pl.BlockSpec((length, hb * head_dim), lambda h: (0, h)),
        out_shape=jax.ShapeDtypeStruct((length, group * head_dim), jnp.bfloat16),
        interpret=INTERPRET,
    )(q, k_tm, v, pk, kh, vh, pkh, fq_t, st0, z0, gate_rows, bias0)


def local_part(q, k, v, before, earlier, feat_q, feat_k, prior_state, prior_norm, gate):
    group, head_dim, length = q.shape
    keep = earlier.astype(jnp.bfloat16)
    phi_k = feature_map(k, feat_k)
    phi_halo = feature_map(before[0], feat_k) * keep
    halo_state = jnp.einsum(
        "htf,hdt->hdf", phi_halo, before[1], preferred_element_type=jnp.float32
    )
    halo_norm = jnp.sum(phi_halo, axis=1, dtype=jnp.float32)
    feats = phi_k.shape[2]
    pad_k = jnp.zeros((group, head_dim, QB - WIN), k.dtype)
    kh = jnp.concatenate([pad_k, before[0]], axis=2).transpose(0, 2, 1)
    vh = jnp.concatenate([pad_k, before[1]], axis=2)
    pkh = jnp.concatenate([jnp.zeros((group, QB - WIN, feats), phi_k.dtype), phi_halo], axis=1)
    fq_t = jnp.concatenate([feat_q, -feat_q], axis=2).transpose(0, 2, 1)
    st0 = prior_state - halo_state
    z0 = jnp.pad((prior_norm - halo_norm)[:, None, :], ((0, 0), (0, 7), (0, 0)))
    gate_rows = jnp.broadcast_to(gate[:, None, None], (group, 1, QB)).astype(jnp.float32)
    halo_rows = (jnp.arange(2 * QB) >= QB - WIN) & (jnp.arange(2 * QB) < QB)
    bias0 = jnp.where(halo_rows & jnp.logical_not(earlier), jnp.float32(-1e30), jnp.float32(0.0))
    bias0 = jnp.broadcast_to(bias0[:, None], (2 * QB, QB))
    k_tm = k.transpose(0, 2, 1)
    return attend(q, k_tm, v, phi_k, kh, vh, pkh, fq_t, st0, z0, gate_rows, bias0)


def body(queries, keys, values, feat_q, feat_k, mix):
    shards = lax.axis_size("seq")
    place = lax.axis_index("seq")
    feature_rows = queries.shape[0]
    length = queries.shape[1] // shards
    group = feat_q.shape[0]
    head_dim = feat_q.shape[1]

    k = exchange(keys.reshape(feature_rows, shards, length), group, head_dim)
    v = exchange(values.reshape(feature_rows, shards, length), group, head_dim)
    q = exchange(queries.reshape(feature_rows, shards, length), group, head_dim)

    earlier = place > 0
    tails = jnp.stack([k[:, :, length - WIN :], v[:, :, length - WIN :]])
    before = passed_along(tails, "seq", 1)

    phi_own = feature_map(k, feat_k)
    own_state = jnp.einsum("htf,hdt->hdf", phi_own, v, preferred_element_type=jnp.float32)
    own_norm = jnp.sum(phi_own, axis=1, dtype=jnp.float32)
    own = jnp.concatenate(
        [own_state.reshape(group * head_dim, -1), own_norm], axis=0
    ).astype(jnp.bfloat16)
    gathered = lax.all_gather(own, "seq").astype(jnp.float32)
    below = (jnp.arange(shards) < place).astype(jnp.float32)
    prior = jnp.einsum("s,srf->rf", below, gathered, precision=lax.Precision.HIGHEST)
    prior_state = prior[: group * head_dim].reshape(own_state.shape)
    prior_norm = prior[group * head_dim :]
    gate = jax.nn.sigmoid(mix)
    return local_part(q, k, v, before, earlier, feat_q, feat_k, prior_state, prior_norm, gate)


def solution(mesh):
    return jax.shard_map(
        body,
        mesh=mesh,
        in_specs=(
            P(("heads", "seq"), None),
            P(("heads", "seq"), None),
            P(("heads", "seq"), None),
            P("heads", None, None),
            P("heads", None, None),
            P("heads"),
        ),
        out_specs=P("seq", "heads"),
        check_vma=False,
    )
```

time: 357 us -> 349 us (0.978)
  Pallas kernels: 89.8 us -> 81.5 us
  local copies, waits for them, and re-layouts: 27 us -> 34.5 us
  waiting for transfers between devices: 144 us -> 138 us
    pallas_call x1, Pallas kernels: 89.8 us -> 81.5 us  [attend(): pl.pallas_call(attend_kernel, grid=(group // hb,), in_specs=[pl.BlockSpec...]
    transpose x0 -> x3, local copies, waits for them, and re-layouts: none -> 7.44 us  [the longest x1 6.46 us: local_part(): k_tm = k.transpose(0, 2, 1)]
    ppermute x1, waiting for transfers between devices: 75.5 us -> 69.2 us  [passed_along(): return lax.ppermute(block, axis, route)]
  transfers between devices with their start and end apart: 5 -> 5, of which waited for: 3 -> 4; matrix products, arithmetic and copies ran while one was open for 17% -> 19% of each run, Pallas kernels for 0% -> 0%
where the time goes in v4:
time: 349 us; the launch traced here: 342 us
  waiting for transfers between devices  138 us (40%)
  Pallas kernels  81.5 us (23%)
  local copies, waits for them, and re-layouts  34.5 us (10%)
  starting transfers between devices  31.5 us (9%)
  other arithmetic  28.9 us (8%)
  matrix products  14.4 us (4%)
  between operations  13.6 us (4%)
    pallas_call x1, Pallas kernels, attend(): pl.pallas_call(attend_kernel, grid=(group // hb,), in_specs=[pl.BlockSpec...  81.5 us
    ppermute x1, waiting for transfers between devices, passed_along(): return lax.ppermute(block, axis, route)  69.2 us
    all_to_all x3, waiting for transfers between devices, exchange(): moved = lax.all_to_all(rows, 'seq', split_axis=1, concat_axis=0, tiled=True)  68.3 us
    all_to_all x3, starting transfers between devices, exchange(): moved = lax.all_to_all(rows, 'seq', split_axis=1, concat_axis=0, tiled=True)  28.2 us
    another operation x3, other arithmetic  10.4 us
    reduce_sum x1, other arithmetic, feature_map(): halves = [jax.nn.softmax(logits, axis=-1), jax.nn.softmax(-logits, axis=-1)]  7.34 us
  transfers between devices with their start and end apart: 5, of which 4 were waited for; matrix products, arithmetic and copies ran while one was open for 19% of the time, Pallas kernels for 0%

profile of v4, /device:TPU:116, one launch (start us, length us, event | category | flops | bytes accessed | tf_op | source)
XLA Modules:
  0.0 342.1 jit_solution(17298421859125846456)
XLA Ops:
  6.5 0.0 copy-start
  6.5 4.8 %copy.38 = bf16[8,16,8,2048]{3,2,0,1:T(8,128)(2,1)} copy(bf16[8,16,8,2048]{3,2,1,0:T(8,128)(2,1)} %bitcast.70) | data formatting | bytes 8388608 | tf_op jit(solution)/shard_map/reshape | solution.py:183
  11.4 6.9 %all-to-all-start.1 = ((bf16[64,16,2048]{2,0,1:T(8,128)(2,1)}), bf16[64,16,2048]{2,0,1:T(8,128)(2,1)}, u32[]{:S(2)}, u32[]{:S(2)}) async-start(bf16[64,16,2048]{2,0,1:T(8,128)(2,1)} %bitcast.69), calls=%async_computation.1 | async-start | bytes 8388608 | tf_op jit(solution)/shard_map/all_to_all | solution.py:23
  18.3 4.7 %copy.37 = bf16[8,16,8,2048]{3,2,0,1:T(8,128)(2,1)} copy(bf16[8,16,8,2048]{3,2,1,0:T(8,128)(2,1)} %bitcast.71) | data formatting | bytes 8388608 | tf_op jit(solution)/shard_map/reshape | solution.py:184
  23.0 52.6 %all-to-all-done.1 = bf16[64,16,2048]{2,0,1:T(8,128)(2,1)} async-done(((bf16[64,16,2048]{2,0,1:T(8,128)(2,1)}), bf16[64,16,2048]{2,0,1:T(8,128)(2,1)}, u32[]{:S(2)}, u32[]{:S(2)}) %all-to-all-start.1) | async-done | bytes 4194336 | tf_op jit(solution)/shard_map/all_to_all | solution.py:23
  75.6 10.7 %all-to-all-start.2 = ((bf16[64,16,2048]{2,0,1:T(8,128)(2,1)}), bf16[64,16,2048]{2,0,1:T(8,128)(2,1)}, u32[]{:S(2)}, u32[]{:S(2)}) async-start(bf16[64,16,2048]{2,0,1:T(8,128)(2,1)} %bitcast.68), calls=%async_computation.2 | async-start | bytes 8388608 | tf_op jit(solution)/shard_map/all_to_all | solution.py:23
  86.3 0.0 all-gather.2.cloned.1.call-start
  86.3 0.0 copy-done
  86.4 4.9 %fusion.21 = (f32[8,2048]{1,0:T(8,128)S(1)}, f32[8,2048,64]{1,2,0:T(8,128)}) fusion(bf16[8,128,64]{1,2,0:T(8,128)(2,1)S(1)} %copy-done, bf16[8,128,2048]{2,1,0:T(8,128)(2,1)} %bitcast.5), kind=kOutput, calls=%fused_computation.46 | convolution fusion | flops 269467648 | bytes 8585216 | tf_op jit(solution)/shard_map/hdt,hdf->htf/dot_general | solution.py:28
  91.3 6.9 %copy.19 = f32[8,2048,64]{2,1,0:T(8,128)} copy(f32[8,2048,64]{1,2,0:T(8,128)} %get-tuple-element.14) | data formatting | bytes 8388608 | tf_op jit(solution)/shard_map/hdt,hdf->htf/dot_general | solution.py:28
  98.2 0.0 copy-start.1
  98.2 7.3 %fusion.3 = f32[8,2048]{1,0:T(8,128)S(1)} fusion(f32[8,2048,64]{2,1,0:T(8,128)} %copy.19, f32[8,2048]{1,0:T(8,128)S(1)} %get-tuple-element.13), kind=kLoop, calls=%fused_computation.7 | loop fusion | flops 2080768 | bytes 4325376 | tf_op jit(solution)/shard_map/reduce_sum | solution.py:29
  105.5 0.0 copy-done.1
  105.6 5.5 %fusion.20 = (f32[8,2048]{1,0:T(8,128)S(1)}, f32[8,2048,64]{2,1,0:T(8,128)}) fusion(f32[8,2048,64]{2,1,0:T(8,128)S(1)} %copy-done.1), kind=kOutput, calls=%fused_computation.45 | output fusion | flops 4194367 | bytes 8454144 | tf_op jit(solution)/shard_map/sub | solution.py:29
  111.0 5.2 %divide_convert_fusion = bf16[8,2048,64]{2,1,0:T(8,128)(2,1)S(1)} fusion(f32[8,2048,64]{2,1,0:T(8,128)} %get-tuple-element.12, f32[8,2048]{1,0:T(8,128)S(1)} %get-tuple-element.11), kind=kLoop, calls=%fused_computation.3 | loop fusion | flops 2097152 | bytes 6356992 | tf_op jit(solution)/shard_map/convert.8
  116.3 5.0 %divide_convert_fusion.1 = bf16[8,2048,64]{2,1,0:T(8,128)(2,1)S(1)} fusion(f32[8,2048,64]{2,1,0:T(8,128)S(1)} %copy-done.1, f32[8,2048]{1,0:T(8,128)S(1)} %fusion.3, f32[8,2048]{1,0:T(8,128)S(1)} %get-tuple-element.13), kind=kLoop, calls=%fused_computation.5 | loop fusion | flops 3145728 | bytes 6422528 | tf_op jit(solution)/shard_map/convert.7
  121.3 4.0 %fusion.19 = (bf16[8,128]{1,0:T(8,128)(2,1)S(1)}, bf16[8,2048,128]{2,1,0:T(8,128)(2,1)}) fusion(bf16[8,2048,64]{2,1,0:T(8,128)(2,1)S(1)} %divide_convert_fusion, bf16[8,2048,64]{2,1,0:T(8,128)(2,1)S(1)} %divide_convert_fusion.1), kind=kLoop, calls=%fused_computation.44 | loop fusion | flops 10484736 | bytes 8390656 | tf_op jit(solution)/shard_map/reduce_sum | solution.py:193
  125.2 15.6 %all-to-all-done.2 = bf16[64,16,2048]{2,0,1:T(8,128)(2,1)} async-done(((bf16[64,16,2048]{2,0,1:T(8,128)(2,1)}), bf16[64,16,2048]{2,0,1:T(8,128)(2,1)}, u32[]{:S(2)}, u32[]{:S(2)}) %all-to-all-start.2) | async-done | bytes 4194336 | tf_op jit(solution)/shard_map/all_to_all | solution.py:23
  140.8 4.7 %convolution_convert_fusion = bf16[8,128,128]{1,2,0:T(8,128)(2,1)S(1)} fusion(bf16[8,128,2048]{2,1,0:T(8,128)(2,1)} %bitcast.9.v_ref, bf16[8,2048,128]{2,1,0:T(8,128)(2,1)} %get-tuple-element.8.pk_ref), kind=kOutput, calls=%fused_computation.19 | convolution fusion | flops 537001984 | bytes 8650752 | tf_op jit(solution)/shard_map/htf,hdt->hdf/dot_general | solution.py:192
  145.5 0.7 pad_maximum_fusion.2
  146.3 0.0 all-gather.2.cloned.1.call-update
  146.3 4.8 %copy.39 = bf16[8,16,8,2048]{3,2,0,1:T(8,128)(2,1)} copy(bf16[8,16,8,2048]{3,2,1,0:T(8,128)(2,1)} %bitcast.72) | data formatting | bytes 8388608 | tf_op jit(solution)/shard_map/reshape | solution.py:185
  151.1 10.6 %all-to-all-start = ((bf16[64,16,2048]{2,0,1:T(8,128)(2,1)}), bf16[64,16,2048]{2,0,1:T(8,128)(2,1)}, u32[]{:S(2)}, u32[]{:S(2)}) async-start(bf16[64,16,2048]{2,0,1:T(8,128)(2,1)} %bitcast.67), calls=%async_computation | async-start | bytes 8388608 | tf_op jit(solution)/shard_map/all_to_all | solution.py:23
  161.7 0.0 copy-done.2
  161.7 0.7 maximum_bitcast_fusion.fq_ref
  162.4 1.1 slice_bitcast_fusion.2
  163.5 1.1 slice_bitcast_fusion.3
  164.6 0.1 pad_maximum_fusion.1
  164.8 3.3 collective-permute-start
  168.0 0.0 copy-done.3
  168.1 6.5 %copy.23.k_ref = bf16[8,2048,128]{2,1,0:T(8,128)(2,1)} copy(bf16[8,2048,128]{1,2,0:T(8,128)(2,1)} %bitcast.6) | data formatting | bytes 8388608 | tf_op jit(solution)/shard_map/transpose | solution.py:171
  174.5 69.2 %collective-permute-done = bf16[2,8,128,64]{3,2,1,0:T(8,128)(2,1)S(1)} collective-permute-done((bf16[2,8,128,64]{3,2,1,0:T(8,128)(2,1)S(1)}, bf16[2,8,128,64]{3,2,1,0:T(8,128)(2,1)S(1)}, u32[]{:S(2)}, u32[]{:S(2)}) %collective-permute-start) | collective-permute-done | bytes 262176 | tf_op jit(solution)/shard_map/ppermute | solution.py:19
  243.8 0.1 pad_bitcast_fusion
  243.9 0.8 copy.24.kh_ref
  244.8 0.4 fusion.22
  245.2 0.4 fusion.23
  245.6 0.2 divide_convert_fusion.2
  245.8 0.1 convert_reduce_fusion
  245.9 0.7 concatenate.40.pkh_ref
  246.7 0.8 concatenate.38.vh_ref
  247.5 0.2 all-gather.2.cloned.1.call-done
  247.7 2.9 fusion.7
  250.7 0.6 pad.7.z_ref
  251.3 1.0 convolution_subtract_fusion.st_ref
  252.3 0.0 all-to-all-done
  252.3 0.8 broadcast_in_dim.16.b_ref
  253.1 0.7 broadcast_in_dim.13.g_ref
  253.7 81.5 %shard_map.64 = bf16[2048,1024]{1,0:T(8,128)(2,1)} custom-call(bf16[8,128,2048]{2,1,0:T(8,128)(2,1)} %bitcast.2.q_ref, bf16[8,2048,128]{2,1,0:T(8,128)(2,1)} %copy.23.k_ref, bf16[8,128,2048]{2,1,0:T(8,128)(2,1)} %bitcast.9.v_ref, bf16[8,2048,128]{2,1,0:T(8,128)(2,1)} %get-tuple-element.8.pk_ref, bf16[8,128,128]{2,1,0:T(8,128)(2,1)} %copy.24.kh_ref, ...), custom_call_target="tpu_custom_call" | custom-call | tf_op jit(solution)/shard_map/pallas_call | solution.py:127
  (8 shorter events, 0.1 us)
Async XLA Ops:
  6.5 79.8 %copy-start = (bf16[8,128,64]{1,2,0:T(8,128)(2,1)S(1)}, bf16[8,128,64]{1,2,0:T(8,128)(2,1)}, u32[]{:S(2)}) copy-start(bf16[8,128,64]{1,2,0:T(8,128)(2,1)} %param.10) | copy-start | bytes 393220
  11.4 64.3 %all-to-all-start.1 = ((bf16[64,16,2048]{2,0,1:T(8,128)(2,1)}), bf16[64,16,2048]{2,0,1:T(8,128)(2,1)}, u32[]{:S(2)}, u32[]{:S(2)}) async-start(bf16[64,16,2048]{2,0,1:T(8,128)(2,1)} %bitcast.69), calls=%async_computation.1 | async-start | bytes 8388608 | tf_op jit(solution)/shard_map/all_to_all | solution.py:23
  75.6 65.2 %all-to-all-start.2 = ((bf16[64,16,2048]{2,0,1:T(8,128)(2,1)}), bf16[64,16,2048]{2,0,1:T(8,128)(2,1)}, u32[]{:S(2)}, u32[]{:S(2)}) async-start(bf16[64,16,2048]{2,0,1:T(8,128)(2,1)} %bitcast.68), calls=%async_computation.2 | async-start | bytes 8388608 | tf_op jit(solution)/shard_map/all_to_all | solution.py:23
  86.3 161.4 %all-gather.2.cloned.1.call-start = ((), (), s32[]{:S(2)}) async-start(), calls=%async_computation.3 | async-start | bytes 4491264 | tf_op jit(solution)/shard_map/all_gather | solution.py:197
  98.2 7.4 %copy-start.1 = (f32[8,2048,64]{2,1,0:T(8,128)S(1)}, f32[8,2048,64]{2,1,0:T(8,128)}, u32[]{:S(2)}) copy-start(f32[8,2048,64]{2,1,0:T(8,128)} %copy.19) | copy-start | bytes 12582916
  151.1 10.6 %copy-start.2 = (bf16[8,128,64]{1,2,0:T(8,128)(2,1)S(1)}, bf16[8,128,64]{1,2,0:T(8,128)(2,1)}, u32[]{:S(2)}) copy-start(bf16[8,128,64]{1,2,0:T(8,128)(2,1)} %param.9) | copy-start | bytes 393220
  151.1 17.0 %copy-start.3 = (f32[8]{0:T(128)S(1)}, f32[8]{0:T(128)}, u32[]{:S(2)}) copy-start(f32[8]{0:T(128)} %param.11) | copy-start | bytes 100
  151.1 101.2 %all-to-all-start = ((bf16[64,16,2048]{2,0,1:T(8,128)(2,1)}), bf16[64,16,2048]{2,0,1:T(8,128)(2,1)}, u32[]{:S(2)}, u32[]{:S(2)}) async-start(bf16[64,16,2048]{2,0,1:T(8,128)(2,1)} %bitcast.67), calls=%async_computation | async-start | bytes 8388608 | tf_op jit(solution)/shard_map/all_to_all | solution.py:23
  164.8 79.0 %collective-permute-start = (bf16[2,8,128,64]{3,2,1,0:T(8,128)(2,1)S(1)}, bf16[2,8,128,64]{3,2,1,0:T(8,128)(2,1)S(1)}, u32[]{:S(2)}, u32[]{:S(2)}) collective-permute-start(bf16[2,8,128,64]{3,2,1,0:T(8,128)(2,1)S(1)} %pad_maximum_fusion.1), channel_id=1, source_target_pairs={{0,1},{1,2},{2,3},{3,4},{4,5},{5,6},{6,7},{7,8},{8,9},{9,10},{10,1... | collective-permute-start | bytes 786440 | tf_op jit(solution)/shard_map/ppermute | solution.py:19
Sparse Core Ops, SparseCore 0:
  146.4 101.2 all-gather.1

commit v5 on v4

v5 whole, which is shorter than its diff:
```python
import functools

import jax
import jax.numpy as jnp
from jax import lax
from jax.experimental import pallas as pl
from jax.experimental.pallas import tpu as pltpu
from jax.sharding import PartitionSpec as P

WIN = 64
QB = 128
HEADS_PER_STEP = 2
Q_PIECES = 2
INTERPRET = False


def passed_along(block, axis, distance):
    devices = range(lax.axis_size(axis))
    route = [(i - distance, i) for i in devices if i - distance in devices]
    return lax.ppermute(block, axis, route)


def exchange(rows, group, head_dim):
    moved = lax.all_to_all(rows, "seq", split_axis=1, concat_axis=0, tiled=True)
    return moved.reshape(group, head_dim, -1)


def feature_map(rows, weight):
    logits = jnp.einsum("hdt,hdf->htf", rows, weight, preferred_element_type=jnp.float32)
    halves = [jax.nn.softmax(logits, axis=-1), jax.nn.softmax(-logits, axis=-1)]
    return jnp.concatenate(halves, axis=-1).astype(jnp.bfloat16)


def _nt(a, b):
    return lax.dot_general(a, b, (((1,), (1,)), ((), ())), preferred_element_type=jnp.float32)


def _tn(a, b):
    return lax.dot_general(a, b, (((0,), (0,)), ((), ())), preferred_element_type=jnp.float32)


def make_kernel(t_begin, blocks):
    first = t_begin == 0

    def attend_kernel(*refs):
        (q_ref, k_ref, v_ref, pk_ref, kh_ref, vh_ref, pkh_ref, fq_ref, st_ref, z_ref, g_ref, b_ref) = refs[:12]
        if first:
            o_ref, st_out, z_out = refs[12:]
        else:
            o_ref = refs[13]
        heads = q_ref.shape[0]
        head_dim = q_ref.shape[1]
        feats = fq_ref.shape[1]
        half = feats // 2
        inv_scale = 1.0 / jnp.sqrt(jnp.float32(head_dim))
        row = lax.broadcasted_iota(jnp.int32, (feats, QB), 0)
        lo = row < half
        wk = lax.broadcasted_iota(jnp.int32, (2 * QB, QB), 0)
        tq = lax.broadcasted_iota(jnp.int32, (2 * QB, QB), 1)
        win_keep = (wk > tq + WIN) & (wk <= tq + QB)
        lin_keep = wk <= tq + WIN
        zrow = lax.broadcasted_iota(jnp.int32, (8, feats), 0)
        neg = jnp.float32(-1e30)

        def step(hh, t0, st, z, kw, vw, pkw, bias):
            q = q_ref[hh, :, pl.ds(t0 - t_begin, QB)]
            g = g_ref[hh]
            s = jnp.dot(kw, q, preferred_element_type=jnp.float32) * inv_scale
            if bias is not None:
                s = s + bias
            s = jnp.where(win_keep, s, neg)
            top = jnp.max(s, axis=0, keepdims=True)
            p = jnp.exp(s - top)
            total = jnp.sum(p, axis=0, keepdims=True)
            window = jnp.dot(vw, p.astype(jnp.bfloat16), preferred_element_type=jnp.float32)
            window = window * (1.0 / total)

            logits = jnp.dot(fq_ref[hh], q, preferred_element_type=jnp.float32)
            m_lo = jnp.max(logits[:half], axis=0, keepdims=True)
            m_hi = jnp.max(logits[half:], axis=0, keepdims=True)
            e = jnp.exp(logits - jnp.where(lo, m_lo, m_hi))
            s_lo = jnp.sum(e[:half], axis=0, keepdims=True)
            s_hi = jnp.sum(e[half:], axis=0, keepdims=True)
            phi = (e * jnp.where(lo, 1.0 / s_lo, 1.0 / s_hi)).astype(jnp.bfloat16)

            aff = jnp.dot(pkw, phi, preferred_element_type=jnp.float32)
            aff = jnp.where(lin_keep, aff, jnp.float32(0.0)).astype(jnp.bfloat16)
            num = jnp.dot(vw, aff, preferred_element_type=jnp.float32)
            den = jnp.sum(aff.astype(jnp.float32), axis=0, keepdims=True)
            st_hi = st.astype(jnp.bfloat16)
            st_lo = (st - st_hi.astype(jnp.float32)).astype(jnp.bfloat16)
            num = num + jnp.dot(st_hi, phi, preferred_element_type=jnp.float32)
            num = num + jnp.dot(st_lo, phi, preferred_element_type=jnp.float32)
            z_hi = z.astype(jnp.bfloat16)
            z_lo = (z - z_hi.astype(jnp.float32)).astype(jnp.bfloat16)
            zz = jnp.where(zrow == 0, z_hi, jnp.where(zrow == 1, z_lo, jnp.zeros_like(z_lo)))
            cross = jnp.dot(zz, phi, preferred_element_type=jnp.float32)
            den = den + (cross[0:1] + cross[1:2])
            linear = num * (1.0 / (den + 1.0))
            out = g * window + (1.0 - g) * linear
            rows = pl.ds(t0 - t_begin, QB)
            o_ref[rows, pl.ds(hh * head_dim, head_dim)] = out.T.astype(o_ref.dtype)

            vb = vw[:, :QB]
            pkb = pkw[:QB]
            st = st + jnp.dot(vb, pkb, preferred_element_type=jnp.float32)
            z = z + jnp.sum(pkb.astype(jnp.float32), axis=0, keepdims=True)
            return st, z

        carry = []
        for hh in range(heads):
            if first:
                kw0 = jnp.concatenate([kh_ref[hh], k_ref[hh, pl.ds(0, QB), :]], axis=0)
                vw0 = jnp.concatenate([vh_ref[hh], v_ref[hh, :, pl.ds(0, QB)]], axis=1)
                pkw0 = jnp.concatenate([pkh_ref[hh], pk_ref[hh, pl.ds(0, QB), :]], axis=0)
                carry.append(step(hh, 0, st_ref[hh], z_ref[hh][0:1], kw0, vw0, pkw0, b_ref[...]))
            else:
                carry.append((st_ref[hh], z_ref[hh][0:1]))

        def loop(i, carry):
            t0 = pl.multiple_of(i * QB, QB)
            base = pl.multiple_of(t0 - QB, QB)
            out = []
            for hh in range(heads):
                kw = k_ref[hh, pl.ds(base, 2 * QB), :]
                vw = v_ref[hh, :, pl.ds(base, 2 * QB)]
                pkw = pk_ref[hh, pl.ds(base, 2 * QB), :]
                out.append(step(hh, t0, carry[hh][0], carry[hh][1], kw, vw, pkw, None))
            return tuple(out)

        lo_blk = t_begin // QB + (1 if first else 0)
        final = lax.fori_loop(lo_blk, t_begin // QB + blocks, loop, tuple(carry))
        if first:
            for hh in range(heads):
                st_out[hh] = final[hh][0]
                z_out[hh] = jnp.broadcast_to(final[hh][1], (8, feats))

    return attend_kernel


def attend(q, t_begin, k_tm, v, pk, kh, vh, pkh, fq_t, st0, z0, gate_rows, bias0, prev):
    group, head_dim, span = q.shape
    length = v.shape[2]
    feats = fq_t.shape[1]
    hb = HEADS_PER_STEP
    first = prev is None
    in_specs = [
        pl.BlockSpec((hb, head_dim, span), lambda h: (h, 0, 0)),
        pl.BlockSpec((hb, length, head_dim), lambda h: (h, 0, 0)),
        pl.BlockSpec((hb, head_dim, length), lambda h: (h, 0, 0)),
        pl.BlockSpec((hb, length, feats), lambda h: (h, 0, 0)),
        pl.BlockSpec((hb, QB, head_dim), lambda h: (h, 0, 0)),
        pl.BlockSpec((hb, head_dim, QB), lambda h: (h, 0, 0)),
        pl.BlockSpec((hb, QB, feats), lambda h: (h, 0, 0)),
        pl.BlockSpec((hb, feats, head_dim), lambda h: (h, 0, 0)),
        pl.BlockSpec((hb, head_dim, feats), lambda h: (h, 0, 0)),
        pl.BlockSpec((hb, 8, feats), lambda h: (h, 0, 0)),
        pl.BlockSpec((hb, 1, QB), lambda h: (h, 0, 0)),
        pl.BlockSpec((2 * QB, QB), lambda h: (0, 0)),
    ]
    args = [q, k_tm, v, pk, kh, vh, pkh, fq_t, st0, z0, gate_rows, bias0]
    piece = t_begin // span
    out_spec = pl.BlockSpec((span, hb * head_dim), lambda h: (piece, h))
    out_shape = jax.ShapeDtypeStruct((length, group * head_dim), jnp.bfloat16)
    if first:
        out_specs = [
            out_spec,
            pl.BlockSpec((hb, head_dim, feats), lambda h: (h, 0, 0)),
            pl.BlockSpec((hb, 8, feats), lambda h: (h, 0, 0)),
        ]
        out_shapes = [
            out_shape,
            jax.ShapeDtypeStruct(st0.shape, jnp.float32),
            jax.ShapeDtypeStruct(z0.shape, jnp.float32),
        ]
        aliases = {}
    else:
        in_specs.append(pl.BlockSpec(memory_space=pl.ANY))
        args.append(prev)
        out_specs = out_spec
        out_shapes = out_shape
        aliases = {12: 0}
    return pl.pallas_call(
        make_kernel(t_begin, span // QB),
        grid=(group // hb,),
        in_specs=in_specs,
        out_specs=out_specs,
        out_shape=out_shapes,
        input_output_aliases=aliases,
        interpret=INTERPRET,
    )(*args)


def local_part(q_parts, k, v, before, earlier, feat_q, feat_k, prior_state, prior_norm, gate):
    group, head_dim, length = k.shape
    keep = earlier.astype(jnp.bfloat16)
    phi_k = feature_map(k, feat_k)
    phi_halo = feature_map(before[0], feat_k) * keep
    halo_state = jnp.einsum(
        "htf,hdt->hdf", phi_halo, before[1], preferred_element_type=jnp.float32
    )
    halo_norm = jnp.sum(phi_halo, axis=1, dtype=jnp.float32)
    feats = phi_k.shape[2]
    pad_k = jnp.zeros((group, head_dim, QB - WIN), k.dtype)
    kh = jnp.concatenate([pad_k, before[0]], axis=2).transpose(0, 2, 1)
    vh = jnp.concatenate([pad_k, before[1]], axis=2)
    pkh = jnp.concatenate([jnp.zeros((group, QB - WIN, feats), phi_k.dtype), phi_halo], axis=1)
    fq_t = jnp.concatenate([feat_q, -feat_q], axis=2).transpose(0, 2, 1)
    st = prior_state - halo_state
    z = jnp.pad((prior_norm - halo_norm)[:, None, :], ((0, 0), (0, 7), (0, 0)))
    gate_rows = jnp.broadcast_to(gate[:, None, None], (group, 1, QB)).astype(jnp.float32)
    halo_rows = (jnp.arange(2 * QB) >= QB - WIN) & (jnp.arange(2 * QB) < QB)
    bias0 = jnp.where(halo_rows & jnp.logical_not(earlier), jnp.float32(-1e30), jnp.float32(0.0))
    bias0 = jnp.broadcast_to(bias0[:, None], (2 * QB, QB))
    k_tm = k.transpose(0, 2, 1)
    span = q_parts[0].shape[2]
    out, st, z = attend(q_parts[0], 0, k_tm, v, phi_k, kh, vh, pkh, fq_t, st, z, gate_rows, bias0, None)
    for c in range(1, len(q_parts)):
        out = attend(q_parts[c], c * span, k_tm, v, phi_k, kh, vh, pkh, fq_t, st, z, gate_rows, bias0, out)
    return out


def body(queries, keys, values, feat_q, feat_k, mix):
    shards = lax.axis_size("seq")
    place = lax.axis_index("seq")
    feature_rows = queries.shape[0]
    length = queries.shape[1] // shards
    group = feat_q.shape[0]
    head_dim = feat_q.shape[1]

    k = exchange(keys.reshape(feature_rows, shards, length), group, head_dim)
    v = exchange(values.reshape(feature_rows, shards, length), group, head_dim)
    halves = queries.reshape(feature_rows, shards, Q_PIECES, length // Q_PIECES).transpose(2, 1, 0, 3)
    q_parts = [
        lax.all_to_all(halves[c], "seq", split_axis=0, concat_axis=0, tiled=True).reshape(
            group, head_dim, -1
        )
        for c in range(Q_PIECES)
    ]

    earlier = place > 0
    tails = jnp.stack([k[:, :, length - WIN :], v[:, :, length - WIN :]])
    before = passed_along(tails, "seq", 1)

    phi_own = feature_map(k, feat_k)
    own_state = jnp.einsum("htf,hdt->hdf", phi_own, v, preferred_element_type=jnp.float32)
    own_norm = jnp.sum(phi_own, axis=1, dtype=jnp.float32)
    own = jnp.concatenate(
        [own_state.reshape(group * head_dim, -1), own_norm], axis=0
    ).astype(jnp.bfloat16)
    gathered = lax.all_gather(own, "seq").astype(jnp.float32)
    below = (jnp.arange(shards) < place).astype(jnp.float32)
    prior = jnp.einsum("s,srf->rf", below, gathered, precision=lax.Precision.HIGHEST)
    prior_state = prior[: group * head_dim].reshape(own_state.shape)
    prior_norm = prior[group * head_dim :]
    gate = jax.nn.sigmoid(mix)
    return local_part(q_parts, k, v, before, earlier, feat_q, feat_k, prior_state, prior_norm, gate)


def solution(mesh):
    return jax.shard_map(
        body,
        mesh=mesh,
        in_specs=(
            P(("heads", "seq"), None),
            P(("heads", "seq"), None),
            P(("heads", "seq"), None),
            P("heads", None, None),
            P("heads", None, None),
            P("heads"),
        ),
        out_specs=P("seq", "heads"),
        check_vma=False,
    )
```

time: 349 us -> 343 us (0.983)
  the two profiles are of different devices: /device:TPU:116 before, /device:TPU:41 now
where the time goes in v5:
time: 343 us; the launch traced here: 342 us
  waiting for transfers between devices  128 us (37%)
  Pallas kernels  85.1 us (25%)
  local copies, waits for them, and re-layouts  44.5 us (13%)
  other arithmetic  28.9 us (8%)
  starting transfers between devices  27.4 us (8%)
  matrix products  14.4 us (4%)
  between operations  13.6 us (4%)
    pallas_call x2, Pallas kernels, attend(): pl.pallas_call(make_kernel(t_begin, span // QB), grid=(group // hb,), in_...  85.1 us
    all_to_all x2, waiting for transfers between devices, exchange(): moved = lax.all_to_all(rows, 'seq', split_axis=1, concat_axis=0, tiled=True)  76.4 us
    all_gather x1, waiting for transfers between devices, body(): gathered = lax.all_gather(own, 'seq').astype(jnp.float32)  20.5 us
    ppermute x1, waiting for transfers between devices, passed_along(): return lax.ppermute(block, axis, route)  16.5 us
    all_to_all x2, waiting for transfers between devices, body(): lax.all_to_all(halves[c], 'seq', split_axis=0, concat_axis=0, tiled=True)  14.7 us
    all_to_all x2, starting transfers between devices, exchange(): moved = lax.all_to_all(rows, 'seq', split_axis=1, concat_axis=0, tiled=True)  13.1 us
    reshape x2, local copies, waits for them, and re-layouts, body(): queries.reshape(feature_rows, shards, Q_PIECES, length // Q_PIECES)  12.3 us
    all_to_all x2, starting transfers between devices, body(): lax.all_to_all(halves[c], 'seq', split_axis=0, concat_axis=0, tiled=True)  11.2 us
  transfers between devices with their start and end apart: 6, of which 5 were waited for; matrix products, arithmetic and copies ran while one was open for 23% of the time, Pallas kernels for 12%

profile of v5, /device:TPU:41, one launch (start us, length us, event | category | flops | bytes accessed | tf_op | source)
XLA Modules:
  0.0 342.1 jit_solution(18028764922812077284)
XLA Ops:
  6.5 0.0 copy-start
  6.5 4.8 %copy.42 = bf16[8,16,8,2048]{3,2,0,1:T(8,128)(2,1)} copy(bf16[8,16,8,2048]{3,2,1,0:T(8,128)(2,1)} %bitcast.71) | data formatting | bytes 8388608 | tf_op jit(solution)/shard_map/reshape | solution.py:231
  11.4 7.3 %all-to-all-start.1 = ((bf16[64,16,2048]{2,0,1:T(8,128)(2,1)}), bf16[64,16,2048]{2,0,1:T(8,128)(2,1)}, u32[]{:S(2)}, u32[]{:S(2)}) async-start(bf16[64,16,2048]{2,0,1:T(8,128)(2,1)} %bitcast.68), calls=%async_computation.1 | async-start | bytes 8388608 | tf_op jit(solution)/shard_map/all_to_all | solution.py:24
  18.7 4.7 %copy.41 = bf16[8,16,8,2048]{3,2,0,1:T(8,128)(2,1)} copy(bf16[8,16,8,2048]{3,2,1,0:T(8,128)(2,1)} %bitcast.72) | data formatting | bytes 8388608 | tf_op jit(solution)/shard_map/reshape | solution.py:232
  23.4 56.5 %all-to-all-done.1 = bf16[64,16,2048]{2,0,1:T(8,128)(2,1)} async-done(((bf16[64,16,2048]{2,0,1:T(8,128)(2,1)}), bf16[64,16,2048]{2,0,1:T(8,128)(2,1)}, u32[]{:S(2)}, u32[]{:S(2)}) %all-to-all-start.1) | async-done | bytes 4194336 | tf_op jit(solution)/shard_map/all_to_all | solution.py:24
  79.9 5.7 %all-to-all-start.2 = ((bf16[64,16,2048]{2,0,1:T(8,128)(2,1)}), bf16[64,16,2048]{2,0,1:T(8,128)(2,1)}, u32[]{:S(2)}, u32[]{:S(2)}) async-start(bf16[64,16,2048]{2,0,1:T(8,128)(2,1)} %bitcast.67), calls=%async_computation.2 | async-start | bytes 8388608 | tf_op jit(solution)/shard_map/all_to_all | solution.py:24
  85.6 0.0 all-gather.2.cloned.1.call-start
  85.7 4.9 %fusion.21 = (f32[8,2048]{1,0:T(8,128)S(1)}, f32[8,2048,64]{1,2,0:T(8,128)}) fusion(bf16[8,128,64]{1,2,0:T(8,128)(2,1)S(1)} %copy-done, bf16[8,128,2048]{2,1,0:T(8,128)(2,1)} %bitcast.5), kind=kOutput, calls=%fused_computation.48 | convolution fusion | flops 269467648 | bytes 8585216 | tf_op jit(solution)/shard_map/hdt,hdf->htf/dot_general | solution.py:29
  90.6 6.9 %copy.22 = f32[8,2048,64]{2,1,0:T(8,128)} copy(f32[8,2048,64]{1,2,0:T(8,128)} %get-tuple-element.22) | data formatting | bytes 8388608 | tf_op jit(solution)/shard_map/hdt,hdf->htf/dot_general | solution.py:29
  97.5 7.3 %fusion.3 = f32[8,2048]{1,0:T(8,128)S(1)} fusion(f32[8,2048,64]{2,1,0:T(8,128)} %copy.22, f32[8,2048]{1,0:T(8,128)S(1)} %get-tuple-element.21), kind=kLoop, calls=%fused_computation.7 | loop fusion | flops 2080768 | bytes 4325376 | tf_op jit(solution)/shard_map/reduce_sum | solution.py:30
  104.9 5.5 %fusion.20 = (f32[8,2048]{1,0:T(8,128)S(1)}, f32[8,2048,64]{2,1,0:T(8,128)}) fusion(f32[8,2048,64]{2,1,0:T(8,128)S(1)} %copy-done.1), kind=kOutput, calls=%fused_computation.47 | output fusion | flops 4194367 | bytes 8454144 | tf_op jit(solution)/shard_map/sub | solution.py:30
  110.3 5.2 %divide_convert_fusion = bf16[8,2048,64]{2,1,0:T(8,128)(2,1)S(1)} fusion(f32[8,2048,64]{2,1,0:T(8,128)} %get-tuple-element.20, f32[8,2048]{1,0:T(8,128)S(1)} %get-tuple-element.19), kind=kLoop, calls=%fused_computation.3 | loop fusion | flops 2097152 | bytes 6356992 | tf_op jit(solution)/shard_map/convert.8
  115.6 5.0 %divide_convert_fusion.1 = bf16[8,2048,64]{2,1,0:T(8,128)(2,1)S(1)} fusion(f32[8,2048,64]{2,1,0:T(8,128)S(1)} %copy-done.1, f32[8,2048]{1,0:T(8,128)S(1)} %fusion.3, f32[8,2048]{1,0:T(8,128)S(1)} %get-tuple-element.21), kind=kLoop, calls=%fused_computation.5 | loop fusion | flops 3145728 | bytes 6422528 | tf_op jit(solution)/shard_map/convert.7
  120.6 4.0 %fusion.19 = (bf16[8,128]{1,0:T(8,128)(2,1)S(1)}, bf16[8,2048,128]{2,1,0:T(8,128)(2,1)}) fusion(bf16[8,2048,64]{2,1,0:T(8,128)(2,1)S(1)} %divide_convert_fusion, bf16[8,2048,64]{2,1,0:T(8,128)(2,1)S(1)} %divide_convert_fusion.1), kind=kLoop, calls=%fused_computation.46 | loop fusion | flops 10484736 | bytes 8390656 | tf_op jit(solution)/shard_map/reduce_sum | solution.py:247
  124.5 19.9 %all-to-all-done.2 = bf16[64,16,2048]{2,0,1:T(8,128)(2,1)} async-done(((bf16[64,16,2048]{2,0,1:T(8,128)(2,1)}), bf16[64,16,2048]{2,0,1:T(8,128)(2,1)}, u32[]{:S(2)}, u32[]{:S(2)}) %all-to-all-start.2) | async-done | bytes 4194336 | tf_op jit(solution)/shard_map/all_to_all | solution.py:24
  144.4 4.7 %convolution_convert_fusion = bf16[8,128,128]{1,2,0:T(8,128)(2,1)S(1)} fusion(bf16[8,128,2048]{2,1,0:T(8,128)(2,1)} %bitcast.9.refs_2_, bf16[8,2048,128]{2,1,0:T(8,128)(2,1)} %get-tuple-element.14.refs_3_), kind=kOutput, calls=%fused_computation.21 | convolution fusion | flops 537001984 | bytes 8650752 | tf_op jit(solution)/shard_map/htf,hdt->hdf/dot_general | solution.py:246
  149.2 0.7 pad_maximum_fusion.2
  149.9 0.0 all-gather.2.cloned.1.call-update
  149.9 7.8 %reshape.81 = bf16[64,16,2,1024]{3,2,1,0:T(2,128)(2,1)} reshape(bf16[64,32768]{1,0:T(8,128)(2,1)} %param.6) | data formatting | bytes 8388608 | tf_op jit(solution)/shard_map/reshape | solution.py:233
  157.7 4.5 %copy.43 = bf16[64,16,2,1024]{3,0,1,2:T(8,128)(2,1)S(1)} copy(bf16[64,16,2,1024]{3,2,1,0:T(2,128)(2,1)} %reshape.81) | data formatting | bytes 8388608 | tf_op jit(solution)/shard_map/reshape | solution.py:233
  162.2 2.5 slice_bitcast_fusion
  164.7 4.8 %all-to-all-start.3 = ((bf16[16,64,1024]{2,1,0:T(8,128)(2,1)}), bf16[16,64,1024]{2,1,0:T(8,128)(2,1)S(1)}, u32[]{:S(2)}, u32[]{:S(2)}) async-start(bf16[16,64,1024]{2,1,0:T(8,128)(2,1)} %get-tuple-element.15), calls=%async_computation.3 | async-start | bytes 4194304 | tf_op jit(solution)/shard_map/all_to_all | solution.py:235
  169.6 0.7 maximum_bitcast_fusion.refs_7_
  170.3 1.1 slice_bitcast_fusion.4
  171.4 1.1 slice_bitcast_fusion.5
  172.5 0.1 pad_maximum_fusion.1
  172.6 3.1 collective-permute-start
  175.7 6.4 %copy.28.refs_1_ = bf16[8,2048,128]{2,1,0:T(8,128)(2,1)} copy(bf16[8,2048,128]{1,2,0:T(8,128)(2,1)} %bitcast.6) | data formatting | bytes 8388608 | tf_op jit(solution)/shard_map/transpose | solution.py:215
  182.2 14.7 %all-to-all-done.3 = bf16[16,64,1024]{2,1,0:T(8,128)(2,1)S(1)} async-done(((bf16[16,64,1024]{2,1,0:T(8,128)(2,1)}), bf16[16,64,1024]{2,1,0:T(8,128)(2,1)S(1)}, u32[]{:S(2)}, u32[]{:S(2)}) %all-to-all-start.3) | async-done | bytes 2097184 | tf_op jit(solution)/shard_map/all_to_all | solution.py:235
  196.8 6.5 %all-to-all-start = ((bf16[16,64,1024]{2,1,0:T(8,128)(2,1)}), bf16[16,64,1024]{2,1,0:T(8,128)(2,1)}, u32[]{:S(2)}, u32[]{:S(2)}) async-start(bf16[16,64,1024]{2,1,0:T(8,128)(2,1)} %get-tuple-element.16), calls=%async_computation | async-start | bytes 4194304 | tf_op jit(solution)/shard_map/all_to_all | solution.py:235
  203.3 16.5 %collective-permute-done = bf16[2,8,128,64]{3,2,1,0:T(8,128)(2,1)S(1)} collective-permute-done((bf16[2,8,128,64]{3,2,1,0:T(8,128)(2,1)S(1)}, bf16[2,8,128,64]{3,2,1,0:T(8,128)(2,1)S(1)}, u32[]{:S(2)}, u32[]{:S(2)}) %collective-permute-start) | collective-permute-done | bytes 262176 | tf_op jit(solution)/shard_map/ppermute | solution.py:20
  219.8 0.1 pad_bitcast_fusion
  220.0 0.8 copy.29.refs_4_
  220.8 0.4 fusion.22
  221.2 0.4 fusion.23
  221.6 0.2 divide_convert_fusion.2
  221.9 0.1 convert_reduce_fusion
  222.0 0.7 concatenate.40.refs_6_
  222.7 0.8 concatenate.38.refs_5_
  223.6 20.5 %all-gather.2.cloned.1.call-done = bf16[16,1032,128]{2,1,0:T(8,128)(2,1)} async-done(((bf16[1,1032,128]{2,1,0:T(8,128)(2,1)}), bf16[16,1032,128]{2,1,0:T(8,128)(2,1)}) %all-gather.2.cloned.1.call-update) | async-done | bytes 4227088 | tf_op jit(solution)/shard_map/all_gather | solution.py:251
  244.1 2.9 fusion.7
  247.1 0.6 pad.7.refs_9_
  247.7 1.0 convolution_subtract_fusion.refs_8_
  248.7 0.7 broadcast_in_dim.16.refs_11_
  249.4 0.7 broadcast_in_dim.13.refs_10_
  250.1 42.5 %shard_map.64 = (bf16[2048,1024]{1,0:T(8,128)(2,1)}, f32[8,128,128]{2,1,0:T(8,128)}, f32[8,8,128]{2,1,0:T(8,128)}) custom-call(bf16[8,128,1024]{2,1,0:T(8,128)(2,1)} %bitcast.70, bf16[8,2048,128]{2,1,0:T(8,128)(2,1)} %copy.28.refs_1_, bf16[8,128,2048]{2,1,0:T(8,128)(2,1)} %bitcast.9.refs_2_, bf16[8,2048,128]{2,1,0:T(8,128)(2,1)} %get-tuple-element.14.refs_3_, ...), custom_call_target="tpu_custom_call" | custom-call | tf_op jit(solution)/shard_map/pallas_call | solution.py:183
  292.6 0.0 all-to-all-done
  292.6 42.6 %shard_map.65 = bf16[2048,1024]{1,0:T(8,128)(2,1)} custom-call(bf16[8,128,1024]{2,1,0:T(8,128)(2,1)} %bitcast.2.refs_0_, bf16[8,2048,128]{2,1,0:T(8,128)(2,1)} %copy.28.refs_1_, bf16[8,128,2048]{2,1,0:T(8,128)(2,1)} %bitcast.9.refs_2_, bf16[8,2048,128]{2,1,0:T(8,128)(2,1)} %get-tuple-element.14.refs_3_, ...), custom_call_target="tpu_custom_call", output_to_operand_aliasing={{}: (12, {})} | custom-call | tf_op jit(solution)/shard_map/pallas_call | solution.py:183
  (15 shorter events, 0.1 us)
Async XLA Ops:
  6.5 79.1 %copy-start = (bf16[8,128,64]{1,2,0:T(8,128)(2,1)S(1)}, bf16[8,128,64]{1,2,0:T(8,128)(2,1)}, u32[]{:S(2)}) copy-start(bf16[8,128,64]{1,2,0:T(8,128)(2,1)} %param.10) | copy-start | bytes 393220
  11.4 68.5 %all-to-all-start.1 = ((bf16[64,16,2048]{2,0,1:T(8,128)(2,1)}), bf16[64,16,2048]{2,0,1:T(8,128)(2,1)}, u32[]{:S(2)}, u32[]{:S(2)}) async-start(bf16[64,16,2048]{2,0,1:T(8,128)(2,1)} %bitcast.68), calls=%async_computation.1 | async-start | bytes 8388608 | tf_op jit(solution)/shard_map/all_to_all | solution.py:24
  79.9 64.6 %all-to-all-start.2 = ((bf16[64,16,2048]{2,0,1:T(8,128)(2,1)}), bf16[64,16,2048]{2,0,1:T(8,128)(2,1)}, u32[]{:S(2)}, u32[]{:S(2)}) async-start(bf16[64,16,2048]{2,0,1:T(8,128)(2,1)} %bitcast.67), calls=%async_computation.2 | async-start | bytes 8388608 | tf_op jit(solution)/shard_map/all_to_all | solution.py:24
  85.6 158.5 %all-gather.2.cloned.1.call-start = ((), (), s32[]{:S(2)}) async-start(), calls=%async_computation.4 | async-start | bytes 4491264 | tf_op jit(solution)/shard_map/all_gather | solution.py:251
  97.5 7.4 %copy-start.1 = (f32[8,2048,64]{2,1,0:T(8,128)S(1)}, f32[8,2048,64]{2,1,0:T(8,128)}, u32[]{:S(2)}) copy-start(f32[8,2048,64]{2,1,0:T(8,128)} %copy.22) | copy-start | bytes 12582916
  164.7 4.8 %copy-start.3 = (bf16[8,128,64]{1,2,0:T(8,128)(2,1)S(1)}, bf16[8,128,64]{1,2,0:T(8,128)(2,1)}, u32[]{:S(2)}) copy-start(bf16[8,128,64]{1,2,0:T(8,128)(2,1)} %param.9) | copy-start | bytes 393220
  164.7 11.0 %copy-start.4 = (f32[8]{0:T(128)S(1)}, f32[8]{0:T(128)}, u32[]{:S(2)}) copy-start(f32[8]{0:T(128)} %param.11) | copy-start | bytes 100
  164.7 32.1 %all-to-all-start.3 = ((bf16[16,64,1024]{2,1,0:T(8,128)(2,1)}), bf16[16,64,1024]{2,1,0:T(8,128)(2,1)S(1)}, u32[]{:S(2)}, u32[]{:S(2)}) async-start(bf16[16,64,1024]{2,1,0:T(8,128)(2,1)} %get-tuple-element.15), calls=%async_computation.3 | async-start | bytes 4194304 | tf_op jit(solution)/shard_map/all_to_all | solution.py:235
  172.6 47.2 %collective-permute-start = (bf16[2,8,128,64]{3,2,1,0:T(8,128)(2,1)S(1)}, bf16[2,8,128,64]{3,2,1,0:T(8,128)(2,1)S(1)}, u32[]{:S(2)}, u32[]{:S(2)}) collective-permute-start(bf16[2,8,128,64]{3,2,1,0:T(8,128)(2,1)S(1)} %pad_maximum_fusion.1), channel_id=1, source_target_pairs={{0,1},{1,2},{2,3},{3,4},{4,5},{5,6},{6,7},{7,8},{8,9},{9,10},{10,1... | collective-permute-start | bytes 786440 | tf_op jit(solution)/shard_map/ppermute | solution.py:20
  196.8 25.0 %copy-start.2 = (bf16[16,64,1024]{2,1,0:T(8,128)(2,1)}, bf16[16,64,1024]{2,1,0:T(8,128)(2,1)S(1)}, u32[]{:S(2)}) copy-start(bf16[16,64,1024]{2,1,0:T(8,128)(2,1)S(1)} %all-to-all-done.3) | copy-start | bytes 6291460
  196.8 95.8 %all-to-all-start = ((bf16[16,64,1024]{2,1,0:T(8,128)(2,1)}), bf16[16,64,1024]{2,1,0:T(8,128)(2,1)}, u32[]{:S(2)}, u32[]{:S(2)}) async-start(bf16[16,64,1024]{2,1,0:T(8,128)(2,1)} %get-tuple-element.16), calls=%async_computation | async-start | bytes 4194304 | tf_op jit(solution)/shard_map/all_to_all | solution.py:235
Sparse Core Ops, SparseCore 0:
  150.0 94.0 all-gather.1

commit v6 on v5

--- a/solution.py
+++ b/solution.py
@@ -228,9 +228,10 @@
     group = feat_q.shape[0]
     head_dim = feat_q.shape[1]
 
+    halves = queries.reshape(feature_rows, shards, Q_PIECES, length // Q_PIECES).transpose(2, 1, 0, 3)
+    halves, values = lax.optimization_barrier((halves, values))
     k = exchange(keys.reshape(feature_rows, shards, length), group, head_dim)
     v = exchange(values.reshape(feature_rows, shards, length), group, head_dim)
-    halves = queries.reshape(feature_rows, shards, Q_PIECES, length // Q_PIECES).transpose(2, 1, 0, 3)
     q_parts = [
         lax.all_to_all(halves[c], "seq", split_axis=0, concat_axis=0, tiled=True).reshape(
             group, head_dim, -1
@@ -245,12 +246,13 @@
     phi_own = feature_map(k, feat_k)
     own_state = jnp.einsum("htf,hdt->hdf", phi_own, v, preferred_element_type=jnp.float32)
     own_norm = jnp.sum(phi_own, axis=1, dtype=jnp.float32)
-    own = jnp.concatenate(
-        [own_state.reshape(group * head_dim, -1), own_norm], axis=0
-    ).astype(jnp.bfloat16)
-    gathered = lax.all_gather(own, "seq").astype(jnp.float32)
-    below = (jnp.arange(shards) < place).astype(jnp.float32)
-    prior = jnp.einsum("s,srf->rf", below, gathered, precision=lax.Precision.HIGHEST)
+    own = jnp.concatenate([own_state.reshape(group * head_dim, -1), own_norm], axis=0)
+    prior = own
+    distance = 1
+    while distance < shards:
+        prior = prior + passed_along(prior, "seq", distance)
+        distance *= 2
+    prior = prior - own
     prior_state = prior[: group * head_dim].reshape(own_state.shape)
     prior_norm = prior[group * head_dim :]
     gate = jax.nn.sigmoid(mix)

time: 343 us -> 345 us (level)
  the two profiles are of different devices: /device:TPU:41 before, /device:TPU:116 now
where the time goes in v6:
time: 345 us; the launch traced here: 339 us
  waiting for transfers between devices  109 us (32%)
  Pallas kernels  85.1 us (25%)
  local copies, waits for them, and re-layouts  47.8 us (14%)
  starting transfers between devices  47.2 us (14%)
  other arithmetic  34.8 us (10%)
  matrix products  14.1 us (4%)
    pallas_call x2, Pallas kernels, attend(): pl.pallas_call(make_kernel(t_begin, span // QB), grid=(group // hb,), in_...  85.1 us
    ppermute x5, waiting for transfers between devices, passed_along(): return lax.ppermute(block, axis, route)  58.8 us
    all_to_all x2, waiting for transfers between devices, exchange(): moved = lax.all_to_all(rows, 'seq', split_axis=1, concat_axis=0, tiled=True)  50.7 us
    all_to_all x2, starting transfers between devices, body(): lax.all_to_all(halves[c], 'seq', split_axis=0, concat_axis=0, tiled=True)  20.8 us
    all_to_all x2, starting transfers between devices, exchange(): moved = lax.all_to_all(rows, 'seq', split_axis=1, concat_axis=0, tiled=True)  17.6 us
    reshape x2, local copies, waits for them, and re-layouts, body(): queries.reshape(feature_rows, shards, Q_PIECES, length // Q_PIECES)  14.4 us
    another operation x3, other arithmetic  11.4 us
    ppermute x5, starting transfers between devices, passed_along(): return lax.ppermute(block, axis, route)  8.85 us
  transfers between devices with their start and end apart: 9, of which 6 were waited for; matrix products, arithmetic and copies ran while one was open for 27% of the time, Pallas kernels for 13%

profile of v6, /device:TPU:116, one launch (start us, length us, event | category | flops | bytes accessed | tf_op | source)
XLA Modules:
  0.0 338.7 jit_solution(12126659643803236460)
XLA Ops:
  0.0 4.7 %copy.27 = bf16[8,16,8,2048]{3,2,0,1:T(8,128)(2,1)} copy(bf16[8,16,8,2048]{3,2,1,0:T(8,128)(2,1)} %bitcast.66) | data formatting | bytes 8388608 | tf_op jit(solution)/shard_map/reshape | solution.py:233
  4.8 6.9 %all-to-all-start.1 = ((bf16[64,16,2048]{2,0,1:T(8,128)(2,1)}), bf16[64,16,2048]{2,0,1:T(8,128)(2,1)}, u32[]{:S(2)}, u32[]{:S(2)}) async-start(bf16[64,16,2048]{2,0,1:T(8,128)(2,1)} %bitcast.60), calls=%async_computation.1 | async-start | bytes 8388608 | tf_op jit(solution)/shard_map/all_to_all | solution.py:24
  11.7 7.8 %reshape.51 = bf16[64,16,2,1024]{3,2,1,0:T(2,128)(2,1)} reshape(bf16[64,32768]{1,0:T(8,128)(2,1)} %param.6) | data formatting | bytes 8388608 | tf_op jit(solution)/shard_map/reshape | solution.py:231
  19.5 6.6 %copy.28 = bf16[64,16,2,1024]{3,0,1,2:T(8,128)(2,1)} copy(bf16[64,16,2,1024]{3,2,1,0:T(2,128)(2,1)} %reshape.51) | data formatting | bytes 8388608 | tf_op jit(solution)/shard_map/reshape | solution.py:231
  26.1 2.3 copy.26
  28.5 4.9 %slice_bitcast_fusion = (bf16[16,64,1024]{2,1,0:T(8,128)(2,1)}, bf16[16,64,1024]{2,1,0:T(8,128)(2,1)}) fusion(bf16[2,16,64,1024]{3,2,1,0:T(8,128)(2,1)} %bitcast.61), kind=kLoop, calls=%fused_computation.15 | loop fusion | bytes 8388608 | tf_op jit(solution)/shard_map/squeeze | solution.py:236
  33.4 35.6 %all-to-all-done.1 = bf16[64,16,2048]{2,0,1:T(8,128)(2,1)} async-done(((bf16[64,16,2048]{2,0,1:T(8,128)(2,1)}), bf16[64,16,2048]{2,0,1:T(8,128)(2,1)}, u32[]{:S(2)}, u32[]{:S(2)}) %all-to-all-start.1) | async-done | bytes 4194336 | tf_op jit(solution)/shard_map/all_to_all | solution.py:24
  69.0 10.7 %all-to-all-start.2 = ((bf16[64,16,2048]{2,0,1:T(8,128)(2,1)}), bf16[64,16,2048]{2,0,1:T(8,128)(2,1)}, u32[]{:S(2)}, u32[]{:S(2)}) async-start(bf16[64,16,2048]{2,0,1:T(8,128)(2,1)} %bitcast.59), calls=%async_computation.2 | async-start | bytes 8388608 | tf_op jit(solution)/shard_map/all_to_all | solution.py:24
  79.7 0.7 maximum_bitcast_fusion.refs_7_
  80.4 4.9 %fusion.16 = (f32[8,2048]{1,0:T(8,128)S(1)}, f32[8,2048,64]{1,2,0:T(8,128)}) fusion(bf16[8,128,64]{1,2,0:T(8,128)(2,1)S(1)} %copy-done, bf16[8,128,2048]{2,1,0:T(8,128)(2,1)} %bitcast.5), kind=kOutput, calls=%fused_computation.43 | convolution fusion | flops 269467648 | bytes 8585216 | tf_op jit(solution)/shard_map/hdt,hdf->htf/dot_general | solution.py:29
  85.3 6.9 %copy.11 = f32[8,2048,64]{2,1,0:T(8,128)} copy(f32[8,2048,64]{1,2,0:T(8,128)} %get-tuple-element.26) | data formatting | bytes 8388608 | tf_op jit(solution)/shard_map/hdt,hdf->htf/dot_general | solution.py:29
  92.2 7.3 %fusion.3 = f32[8,2048]{1,0:T(8,128)S(1)} fusion(f32[8,2048,64]{2,1,0:T(8,128)} %copy.11, f32[8,2048]{1,0:T(8,128)S(1)} %get-tuple-element.25), kind=kLoop, calls=%fused_computation.8 | loop fusion | flops 2080768 | bytes 4325376 | tf_op jit(solution)/shard_map/reduce_sum | solution.py:30
  99.6 5.5 %fusion.15 = (f32[8,2048]{1,0:T(8,128)S(1)}, f32[8,2048,64]{2,1,0:T(8,128)}) fusion(f32[8,2048,64]{2,1,0:T(8,128)S(1)} %copy-done.1), kind=kOutput, calls=%fused_computation.42 | output fusion | flops 4194367 | bytes 8454144 | tf_op jit(solution)/shard_map/sub | solution.py:30
  105.0 5.2 %divide_convert_fusion = bf16[8,2048,64]{2,1,0:T(8,128)(2,1)S(1)} fusion(f32[8,2048,64]{2,1,0:T(8,128)} %get-tuple-element.24, f32[8,2048]{1,0:T(8,128)S(1)} %get-tuple-element.23), kind=kLoop, calls=%fused_computation.4 | loop fusion | flops 2097152 | bytes 6356992 | tf_op jit(solution)/shard_map/convert.3
  110.3 5.0 %divide_convert_fusion.1 = bf16[8,2048,64]{2,1,0:T(8,128)(2,1)S(1)} fusion(f32[8,2048,64]{2,1,0:T(8,128)S(1)} %copy-done.1, f32[8,2048]{1,0:T(8,128)S(1)} %fusion.3, f32[8,2048]{1,0:T(8,128)S(1)} %get-tuple-element.25), kind=kLoop, calls=%fused_computation.6 | loop fusion | flops 3145728 | bytes 6422528 | tf_op jit(solution)/shard_map/convert.2
  115.3 3.9 %convert_reduce_fusion = (f32[8,128]{1,0:T(8,128)S(1)}, bf16[8,2048,128]{2,1,0:T(8,128)(2,1)}) fusion(bf16[8,2048,64]{2,1,0:T(8,128)(2,1)S(1)} %divide_convert_fusion, bf16[8,2048,64]{2,1,0:T(8,128)(2,1)S(1)} %divide_convert_fusion.1), kind=kLoop, calls=%fused_computation.3 | loop fusion | flops 12581888 | bytes 8392704 | tf_op jit(solution)/shard_map/reduce_sum | solution.py:248
  119.2 15.1 %all-to-all-done.2 = bf16[64,16,2048]{2,0,1:T(8,128)(2,1)} async-done(((bf16[64,16,2048]{2,0,1:T(8,128)(2,1)}), bf16[64,16,2048]{2,0,1:T(8,128)(2,1)}, u32[]{:S(2)}, u32[]{:S(2)}) %all-to-all-start.2) | async-done | bytes 4194336 | tf_op jit(solution)/shard_map/all_to_all | solution.py:24
  134.3 10.1 %all-to-all-start.3 = ((bf16[16,64,1024]{2,1,0:T(8,128)(2,1)}), bf16[16,64,1024]{2,1,0:T(8,128)(2,1)S(1)}, u32[]{:S(2)}, u32[]{:S(2)}) async-start(bf16[16,64,1024]{2,1,0:T(8,128)(2,1)} %get-tuple-element.19), calls=%async_computation.3 | async-start | bytes 4194304 | tf_op jit(solution)/shard_map/all_to_all | solution.py:236
  144.4 4.7 %fusion.19 = f32[8,128,128]{2,1,0:T(8,128)S(1)} fusion(bf16[8,128,2048]{2,1,0:T(8,128)(2,1)} %bitcast.9.refs_2_, bf16[8,2048,128]{2,1,0:T(8,128)(2,1)} %get-tuple-element.18.refs_3_), kind=kOutput, calls=%fused_computation.46 | convolution fusion | flops 536870912 | bytes 8912896 | tf_op jit(solution)/shard_map/htf,hdt->hdf/dot_general | solution.py:247
  149.2 3.1 collective-permute-start.1
  152.2 1.1 slice_bitcast_fusion.4
  153.3 1.1 slice_bitcast_fusion.5
  154.4 0.9 pad_maximum_fusion.2
  155.3 1.9 collective-permute-start
  157.3 22.2 %collective-permute-done.1 = f32[1032,128]{1,0:T(8,128)S(1)} collective-permute-done((f32[1032,128]{1,0:T(8,128)S(1)}, f32[1032,128]{1,0:T(8,128)S(1)}, u32[]{:S(2)}, u32[]{:S(2)}) %collective-permute-start.1) | collective-permute-done | bytes 528416 | tf_op jit(solution)/shard_map/ppermute | solution.py:20
  179.5 1.3 collective-permute-start.2
  181.5 6.5 %copy.17.refs_1_ = bf16[8,2048,128]{2,1,0:T(8,128)(2,1)} copy(bf16[8,2048,128]{1,2,0:T(8,128)(2,1)} %bitcast.6) | data formatting | bytes 8388608 | tf_op jit(solution)/shard_map/transpose | solution.py:215
  188.0 10.6 %all-to-all-start = ((bf16[16,64,1024]{2,1,0:T(8,128)(2,1)}), bf16[16,64,1024]{2,1,0:T(8,128)(2,1)}, u32[]{:S(2)}, u32[]{:S(2)}) async-start(bf16[16,64,1024]{2,1,0:T(8,128)(2,1)} %get-tuple-element.20), calls=%async_computation | async-start | bytes 4194304 | tf_op jit(solution)/shard_map/all_to_all | solution.py:236
  198.6 11.0 %collective-permute-done = bf16[2,8,128,64]{3,2,1,0:T(8,128)(2,1)} collective-permute-done((bf16[2,8,128,64]{3,2,1,0:T(8,128)(2,1)}, bf16[2,8,128,64]{3,2,1,0:T(8,128)(2,1)}, u32[]{:S(2)}, u32[]{:S(2)}) %collective-permute-start) | collective-permute-done | bytes 262176 | tf_op jit(solution)/shard_map/ppermute | solution.py:20
  209.7 1.1 slice_bitcast_fusion.2
  210.7 1.9 add.24
  212.6 1.3 collective-permute-start.3
  214.1 0.9 copy.18.refs_4_
  214.9 2.0 fusion.17
  216.9 1.4 fusion.18
  218.3 13.8 %collective-permute-done.3 = f32[1032,128]{1,0:T(8,128)} collective-permute-done((f32[1032,128]{1,0:T(8,128)}, f32[1032,128]{1,0:T(8,128)}, u32[]{:S(2)}, u32[]{:S(2)}) %collective-permute-start.3) | collective-permute-done | bytes 528416 | tf_op jit(solution)/shard_map/ppermute | solution.py:20
  232.1 1.3 add.25
  233.4 1.3 collective-permute-start.4
  234.7 1.2 divide_convert_fusion.2
  236.0 0.8 concatenate.28.refs_6_
  236.8 0.8 concatenate.26.refs_5_
  237.6 1.2 fusion.13
  238.8 11.7 %collective-permute-done.4 = f32[1032,128]{1,0:T(8,128)S(1)} collective-permute-done((f32[1032,128]{1,0:T(8,128)S(1)}, f32[1032,128]{1,0:T(8,128)S(1)}, u32[]{:S(2)}, u32[]{:S(2)}) %collective-permute-start.4) | collective-permute-done | bytes 528416 | tf_op jit(solution)/shard_map/ppermute | solution.py:20
  251.2 0.9 sub.58.refs_8_
  252.1 0.8 broadcast_in_dim.16.refs_11_
  252.8 0.7 broadcast_in_dim.13.refs_10_
  253.5 42.5 %shard_map.64 = (bf16[2048,1024]{1,0:T(8,128)(2,1)}, f32[8,128,128]{2,1,0:T(8,128)}, f32[8,8,128]{2,1,0:T(8,128)}) custom-call(bf16[8,128,1024]{2,1,0:T(8,128)(2,1)} %bitcast.65, bf16[8,2048,128]{2,1,0:T(8,128)(2,1)} %copy.17.refs_1_, bf16[8,128,2048]{2,1,0:T(8,128)(2,1)} %bitcast.9.refs_2_, bf16[8,2048,128]{2,1,0:T(8,128)(2,1)} %get-tuple-element.18.refs_3_, ...), custom_call_target="tpu_custom_call" | custom-call | tf_op jit(solution)/shard_map/pallas_call | solution.py:183
  296.1 42.6 %shard_map.65 = bf16[2048,1024]{1,0:T(8,128)(2,1)} custom-call(bf16[8,128,1024]{2,1,0:T(8,128)(2,1)} %bitcast.2.refs_0_, bf16[8,2048,128]{2,1,0:T(8,128)(2,1)} %copy.17.refs_1_, bf16[8,128,2048]{2,1,0:T(8,128)(2,1)} %bitcast.9.refs_2_, bf16[8,2048,128]{2,1,0:T(8,128)(2,1)} %get-tuple-element.18.refs_3_, ...), custom_call_target="tpu_custom_call", output_to_operand_aliasing={{}: (12, {})} | custom-call | tf_op jit(solution)/shard_map/pallas_call | solution.py:183
  (28 shorter events, 1.8 us)
Async XLA Ops:
  0.0 80.4 %copy-start = (bf16[8,128,64]{1,2,0:T(8,128)(2,1)S(1)}, bf16[8,128,64]{1,2,0:T(8,128)(2,1)}, u32[]{:S(2)}) copy-start(bf16[8,128,64]{1,2,0:T(8,128)(2,1)} %param.10) | copy-start | bytes 393220
  4.8 64.3 %all-to-all-start.1 = ((bf16[64,16,2048]{2,0,1:T(8,128)(2,1)}), bf16[64,16,2048]{2,0,1:T(8,128)(2,1)}, u32[]{:S(2)}, u32[]{:S(2)}) async-start(bf16[64,16,2048]{2,0,1:T(8,128)(2,1)} %bitcast.60), calls=%async_computation.1 | async-start | bytes 8388608 | tf_op jit(solution)/shard_map/all_to_all | solution.py:24
  19.5 6.6 %copy-start.3 = (bf16[64,32768]{1,0:T(8,128)(2,1)S(1)}, bf16[64,32768]{1,0:T(8,128)(2,1)}, u32[]{:S(2)}) copy-start(bf16[64,32768]{1,0:T(8,128)(2,1)} %param.8) | copy-start | bytes 12582916
  26.1 2.3 copy-start.4
  69.0 65.3 %all-to-all-start.2 = ((bf16[64,16,2048]{2,0,1:T(8,128)(2,1)}), bf16[64,16,2048]{2,0,1:T(8,128)(2,1)}, u32[]{:S(2)}, u32[]{:S(2)}) async-start(bf16[64,16,2048]{2,0,1:T(8,128)(2,1)} %bitcast.59), calls=%async_computation.2 | async-start | bytes 8388608 | tf_op jit(solution)/shard_map/all_to_all | solution.py:24
  92.2 7.4 %copy-start.1 = (f32[8,2048,64]{2,1,0:T(8,128)S(1)}, f32[8,2048,64]{2,1,0:T(8,128)}, u32[]{:S(2)}) copy-start(f32[8,2048,64]{2,1,0:T(8,128)} %copy.11) | copy-start | bytes 12582916
  134.3 53.7 %all-to-all-start.3 = ((bf16[16,64,1024]{2,1,0:T(8,128)(2,1)}), bf16[16,64,1024]{2,1,0:T(8,128)(2,1)S(1)}, u32[]{:S(2)}, u32[]{:S(2)}) async-start(bf16[16,64,1024]{2,1,0:T(8,128)(2,1)} %get-tuple-element.19), calls=%async_computation.3 | async-start | bytes 4194304 | tf_op jit(solution)/shard_map/all_to_all | solution.py:236
  149.1 31.8 %copy-start.6 = (f32[8]{0:T(128)S(1)}, f32[8]{0:T(128)}, u32[]{:S(2)}) copy-start(f32[8]{0:T(128)} %param.11) | copy-start | bytes 100
  149.2 30.3 %collective-permute-start.1 = (f32[1032,128]{1,0:T(8,128)S(1)}, f32[1032,128]{1,0:T(8,128)S(1)}, u32[]{:S(2)}, u32[]{:S(2)}) collective-permute-start(f32[1032,128]{1,0:T(8,128)S(1)} %pad_maximum_fusion.1), channel_id=1, source_target_pairs={{0,1},{1,2},{2,3},{3,4},{4,5},{5,6},{6,7},{7,8},{8,9},{9,10},{10,1... | collective-permute-start | bytes 1585160 | tf_op jit(solution)/shard_map/ppermute | solution.py:20
  155.3 54.3 %collective-permute-start = (bf16[2,8,128,64]{3,2,1,0:T(8,128)(2,1)}, bf16[2,8,128,64]{3,2,1,0:T(8,128)(2,1)}, u32[]{:S(2)}, u32[]{:S(2)}) collective-permute-start(bf16[2,8,128,64]{3,2,1,0:T(8,128)(2,1)} %pad_maximum_fusion.2), channel_id=1, source_target_pairs={{0,1},{1,2},{2,3},{3,4},{4,5},{5,6},{6,7},{7,8},{8,9},{9,10},{10,1... | collective-permute-start | bytes 786440 | tf_op jit(solution)/shard_map/ppermute | solution.py:20
  179.5 31.2 %collective-permute-start.2 = (f32[1032,128]{1,0:T(8,128)S(1)}, f32[1032,128]{1,0:T(8,128)}, u32[]{:S(2)}, u32[]{:S(2)}) collective-permute-start(f32[1032,128]{1,0:T(8,128)S(1)} %fusion.14), channel_id=1, source_target_pairs={{0,2},{1,3},{2,4},{3,5},{4,6},{5,7},{6,8},{7,9},{8,10},{9,11},{10,... | collective-permute-start | bytes 1585160 | tf_op jit(solution)/shard_map/ppermute | solution.py:20
  188.0 28.9 %copy-start.2 = (bf16[16,64,1024]{2,1,0:T(8,128)(2,1)}, bf16[16,64,1024]{2,1,0:T(8,128)(2,1)S(1)}, u32[]{:S(2)}) copy-start(bf16[16,64,1024]{2,1,0:T(8,128)(2,1)S(1)} %all-to-all-done.3) | copy-start | bytes 6291460
  188.0 108.1 %all-to-all-start = ((bf16[16,64,1024]{2,1,0:T(8,128)(2,1)}), bf16[16,64,1024]{2,1,0:T(8,128)(2,1)}, u32[]{:S(2)}, u32[]{:S(2)}) async-start(bf16[16,64,1024]{2,1,0:T(8,128)(2,1)} %get-tuple-element.20), calls=%async_computation | async-start | bytes 4194304 | tf_op jit(solution)/shard_map/all_to_all | solution.py:236
  212.6 19.5 %collective-permute-start.3 = (f32[1032,128]{1,0:T(8,128)}, f32[1032,128]{1,0:T(8,128)}, u32[]{:S(2)}, u32[]{:S(2)}) collective-permute-start(f32[1032,128]{1,0:T(8,128)} %add.24), channel_id=1, source_target_pairs={{0,4},{1,5},{2,6},{3,7},{4,8},{5,9},{6,10},{7,11},{8,12},{9,13},{1... | collective-permute-start | bytes 1585160 | tf_op jit(solution)/shard_map/ppermute | solution.py:20
  233.4 19.5 %copy-start.5 = (f32[8]{0:T(128)S(1)}, f32[8]{0:T(128)}, u32[]{:S(2)}) copy-start(f32[8]{0:T(128)} %add_divide_fusion) | copy-start | bytes 100
  233.4 17.0 %collective-permute-start.4 = (f32[1032,128]{1,0:T(8,128)S(1)}, f32[1032,128]{1,0:T(8,128)S(1)}, u32[]{:S(2)}, u32[]{:S(2)}) collective-permute-start(f32[1032,128]{1,0:T(8,128)S(1)} %add.25), channel_id=1, source_target_pairs={{0,8},{1,9},{2,10},{3,11},{4,12},{5,13},{6,14},{7,15},{16,24},{17,... | collective-permute-start | bytes 1585160 | tf_op jit(solution)/shard_map/ppermute | solution.py:20

commit v7 on v6

--- a/solution.py
+++ b/solution.py
@@ -250,7 +250,7 @@
     prior = own
     distance = 1
     while distance < shards:
-        prior = prior + passed_along(prior, "seq", distance)
+        prior = prior + passed_along(prior.astype(jnp.bfloat16), "seq", distance).astype(jnp.float32)
         distance *= 2
     prior = prior - own
     prior_state = prior[: group * head_dim].reshape(own_state.shape)

time: 345 us -> 329 us (0.954); the launches traced: 339 us -> 328 us
  waiting for transfers between devices: 109 us -> 91.6 us
  local copies, waits for them, and re-layouts: 47.8 us -> 53.4 us
    ppermute x5, waiting for transfers between devices: 58.8 us -> 34.7 us  [passed_along(): return lax.ppermute(block, axis, route)]
    all_to_all x2, waiting for transfers between devices: 50.7 us -> 56.9 us  [exchange(): moved = lax.all_to_all(rows, 'seq', split_axis=1, concat_axis=0, tiled=True)]
  transfers between devices with their start and end apart: 9 -> 9, of which waited for: 6 -> 6; matrix products, arithmetic and copies ran while one was open for 27% -> 31% of each run, Pallas kernels for 13% -> 13%
where the time goes in v7:
time: 329 us; the launch traced here: 328 us
  waiting for transfers between devices  91.6 us (28%)
  Pallas kernels  85.1 us (26%)
  local copies, waits for them, and re-layouts  53.4 us (16%)
  starting transfers between devices  45.9 us (14%)
  other arithmetic  36.7 us (11%)
  matrix products  15.2 us (5%)
    pallas_call x2, Pallas kernels, attend(): pl.pallas_call(make_kernel(t_begin, span // QB), grid=(group // hb,), in_...  85.1 us
    all_to_all x2, waiting for transfers between devices, exchange(): moved = lax.all_to_all(rows, 'seq', split_axis=1, concat_axis=0, tiled=True)  56.9 us
    ppermute x5, waiting for transfers between devices, passed_along(): return lax.ppermute(block, axis, route)  34.7 us
    all_to_all x2, starting transfers between devices, body(): lax.all_to_all(halves[c], 'seq', split_axis=0, concat_axis=0, tiled=True)  19.1 us
    all_to_all x2, starting transfers between devices, exchange(): moved = lax.all_to_all(rows, 'seq', split_axis=1, concat_axis=0, tiled=True)  17.7 us
    reshape x2, local copies, waits for them, and re-layouts, body(): queries.reshape(feature_rows, shards, Q_PIECES, length // Q_PIECES)  14.4 us
    another operation x3, other arithmetic  13.1 us
    ppermute x5, starting transfers between devices, passed_along(): return lax.ppermute(block, axis, route)  9.03 us
  transfers between devices with their start and end apart: 9, of which 6 were waited for; matrix products, arithmetic and copies ran while one was open for 31% of the time, Pallas kernels for 13%

profile of v7, /device:TPU:116, one launch (start us, length us, event | category | flops | bytes accessed | tf_op | source)
XLA Modules:
  0.0 328.1 jit_solution(3158957812176344998)
XLA Ops:
  0.0 4.8 %copy.27 = bf16[8,16,8,2048]{3,2,0,1:T(8,128)(2,1)} copy(bf16[8,16,8,2048]{3,2,1,0:T(8,128)(2,1)} %bitcast.68) | data formatting | bytes 8388608 | tf_op jit(solution)/shard_map/reshape | solution.py:233
  4.8 6.9 %all-to-all-start.1 = ((bf16[64,16,2048]{2,0,1:T(8,128)(2,1)}), bf16[64,16,2048]{2,0,1:T(8,128)(2,1)}, u32[]{:S(2)}, u32[]{:S(2)}) async-start(bf16[64,16,2048]{2,0,1:T(8,128)(2,1)} %bitcast.66), calls=%async_computation.1 | async-start | bytes 8388608 | tf_op jit(solution)/shard_map/all_to_all | solution.py:24
  11.7 7.8 %reshape.51 = bf16[64,16,2,1024]{3,2,1,0:T(2,128)(2,1)} reshape(bf16[64,32768]{1,0:T(8,128)(2,1)} %param.6) | data formatting | bytes 8388608 | tf_op jit(solution)/shard_map/reshape | solution.py:231
  19.5 6.6 %copy.28 = bf16[64,16,2,1024]{3,0,1,2:T(8,128)(2,1)} copy(bf16[64,16,2,1024]{3,2,1,0:T(2,128)(2,1)} %reshape.51) | data formatting | bytes 8388608 | tf_op jit(solution)/shard_map/reshape | solution.py:231
  26.1 2.3 copy.26
  28.4 40.6 %all-to-all-done.1 = bf16[64,16,2048]{2,0,1:T(8,128)(2,1)} async-done(((bf16[64,16,2048]{2,0,1:T(8,128)(2,1)}), bf16[64,16,2048]{2,0,1:T(8,128)(2,1)}, u32[]{:S(2)}, u32[]{:S(2)}) %all-to-all-start.1) | async-done | bytes 4194336 | tf_op jit(solution)/shard_map/all_to_all | solution.py:24
  69.1 10.8 %all-to-all-start.2 = ((bf16[64,16,2048]{2,0,1:T(8,128)(2,1)}), bf16[64,16,2048]{2,0,1:T(8,128)(2,1)}, u32[]{:S(2)}, u32[]{:S(2)}) async-start(bf16[64,16,2048]{2,0,1:T(8,128)(2,1)} %bitcast.64), calls=%async_computation.2 | async-start | bytes 8388608 | tf_op jit(solution)/shard_map/all_to_all | solution.py:24
  81.2 4.9 %slice_bitcast_fusion = (bf16[16,64,1024]{2,1,0:T(8,128)(2,1)}, bf16[16,64,1024]{2,1,0:T(8,128)(2,1)}) fusion(bf16[2,16,64,1024]{3,2,1,0:T(8,128)(2,1)} %bitcast.65), kind=kLoop, calls=%fused_computation.15 | loop fusion | bytes 8388608 | tf_op jit(solution)/shard_map/squeeze | solution.py:236
  86.1 4.9 %fusion.19 = (f32[8,2048]{1,0:T(8,128)S(1)}, f32[8,2048,64]{1,2,0:T(8,128)}) fusion(bf16[8,128,64]{1,2,0:T(8,128)(2,1)S(1)} %copy-done, bf16[8,128,2048]{2,1,0:T(8,128)(2,1)} %bitcast.5), kind=kOutput, calls=%fused_computation.49 | convolution fusion | flops 269467648 | bytes 8585216 | tf_op jit(solution)/shard_map/hdt,hdf->htf/dot_general | solution.py:29
  91.0 6.9 %copy.11 = f32[8,2048,64]{2,1,0:T(8,128)} copy(f32[8,2048,64]{1,2,0:T(8,128)} %get-tuple-element.26) | data formatting | bytes 8388608 | tf_op jit(solution)/shard_map/hdt,hdf->htf/dot_general | solution.py:29
  97.9 1.1 slice_bitcast_fusion.5
  99.0 7.4 %fusion.3 = f32[8,2048]{1,0:T(8,128)S(1)} fusion(f32[8,2048,64]{2,1,0:T(8,128)} %copy.11, f32[8,2048]{1,0:T(8,128)S(1)} %get-tuple-element.25), kind=kLoop, calls=%fused_computation.8 | loop fusion | flops 2080768 | bytes 4325376 | tf_op jit(solution)/shard_map/reduce_sum | solution.py:30
  106.4 5.5 %fusion.18 = (f32[8,2048]{1,0:T(8,128)S(1)}, f32[8,2048,64]{2,1,0:T(8,128)}) fusion(f32[8,2048,64]{2,1,0:T(8,128)S(1)} %copy-done.1), kind=kOutput, calls=%fused_computation.48 | output fusion | flops 4194367 | bytes 8454144 | tf_op jit(solution)/shard_map/sub | solution.py:30
  111.8 6.3 %divide_convert_fusion.1 = bf16[8,2048,64]{2,1,0:T(8,128)(2,1)} fusion(f32[8,2048,64]{2,1,0:T(8,128)S(1)} %copy-done.1, f32[8,2048]{1,0:T(8,128)S(1)} %fusion.3, f32[8,2048]{1,0:T(8,128)S(1)} %get-tuple-element.25), kind=kLoop, calls=%fused_computation.6 | loop fusion | flops 3145728 | bytes 6422528 | tf_op jit(solution)/shard_map/convert.2
  118.2 16.3 %all-to-all-done.2 = bf16[64,16,2048]{2,0,1:T(8,128)(2,1)} async-done(((bf16[64,16,2048]{2,0,1:T(8,128)(2,1)}), bf16[64,16,2048]{2,0,1:T(8,128)(2,1)}, u32[]{:S(2)}, u32[]{:S(2)}) %all-to-all-start.2) | async-done | bytes 4194336 | tf_op jit(solution)/shard_map/all_to_all | solution.py:24
  134.4 10.1 %all-to-all-start.3 = ((bf16[16,64,1024]{2,1,0:T(8,128)(2,1)}), bf16[16,64,1024]{2,1,0:T(8,128)(2,1)S(1)}, u32[]{:S(2)}, u32[]{:S(2)}) async-start(bf16[16,64,1024]{2,1,0:T(8,128)(2,1)} %get-tuple-element.19), calls=%async_computation.3 | async-start | bytes 4194304 | tf_op jit(solution)/shard_map/all_to_all | solution.py:236
  144.5 1.1 slice_bitcast_fusion.4
  145.6 5.5 %divide_convert_fusion = bf16[8,2048,64]{2,1,0:T(8,128)(2,1)S(1)} fusion(f32[8,2048,64]{2,1,0:T(8,128)} %get-tuple-element.24, f32[8,2048]{1,0:T(8,128)S(1)} %get-tuple-element.23), kind=kLoop, calls=%fused_computation.4 | loop fusion | flops 2097152 | bytes 6356992 | tf_op jit(solution)/shard_map/convert.3
  151.1 2.6 convert_reduce_fusion
  153.8 4.9 %fusion.22 = f32[8,128,128]{2,1,0:T(8,128)S(1)} fusion(bf16[8,128,2048]{2,1,0:T(8,128)(2,1)} %bitcast.9.refs_2_, bf16[8,2048,128]{2,1,0:T(8,128)(2,1)S(1)} %get-tuple-element.18.refs_3_), kind=kOutput, calls=%fused_computation.52 | convolution fusion | flops 536870912 | bytes 8912896 | tf_op jit(solution)/shard_map/htf,hdt->hdf/dot_general | solution.py:247
  158.7 0.9 pad_maximum_fusion.2
  159.6 3.1 collective-permute-start
  163.4 2.1 collective-permute-start.1
  166.2 6.5 %copy.17.refs_1_ = bf16[8,2048,128]{2,1,0:T(8,128)(2,1)} copy(bf16[8,2048,128]{1,2,0:T(8,128)(2,1)} %bitcast.6) | data formatting | bytes 8388608 | tf_op jit(solution)/shard_map/transpose | solution.py:215
  172.7 6.3 %collective-permute-done = bf16[2,8,128,64]{3,2,1,0:T(8,128)(2,1)S(1)} collective-permute-done((bf16[2,8,128,64]{3,2,1,0:T(8,128)(2,1)}, bf16[2,8,128,64]{3,2,1,0:T(8,128)(2,1)S(1)}, u32[]{:S(2)}, u32[]{:S(2)}) %collective-permute-start) | collective-permute-done | bytes 262176 | tf_op jit(solution)/shard_map/ppermute | solution.py:20
  178.9 1.6 fusion.20
  180.6 3.6 %collective-permute-done.1 = bf16[1032,128]{1,0:T(8,128)(2,1)S(1)} collective-permute-done((bf16[1032,128]{1,0:T(8,128)(2,1)}, bf16[1032,128]{1,0:T(8,128)(2,1)S(1)}, u32[]{:S(2)}, u32[]{:S(2)}) %collective-permute-start.1) | collective-permute-done | bytes 264224 | tf_op jit(solution)/shard_map/ppermute | solution.py:20
  185.0 1.3 collective-permute-start.2
  186.3 2.6 fusion.21
  188.8 1.9 slice_bitcast_fusion.2
  190.7 6.1 %collective-permute-done.2 = bf16[1032,128]{1,0:T(8,128)(2,1)S(1)} collective-permute-done((bf16[1032,128]{1,0:T(8,128)(2,1)}, bf16[1032,128]{1,0:T(8,128)(2,1)S(1)}, u32[]{:S(2)}, u32[]{:S(2)}) %collective-permute-start.2) | collective-permute-done | bytes 264224 | tf_op jit(solution)/shard_map/ppermute | solution.py:20
  196.8 0.8 fusion.17
  197.6 1.3 collective-permute-start.3
  198.9 9.0 %all-to-all-start = ((bf16[16,64,1024]{2,1,0:T(8,128)(2,1)}), bf16[16,64,1024]{2,1,0:T(8,128)(2,1)}, u32[]{:S(2)}, u32[]{:S(2)}) async-start(bf16[16,64,1024]{2,1,0:T(8,128)(2,1)} %get-tuple-element.20), calls=%async_computation | async-start | bytes 4194304 | tf_op jit(solution)/shard_map/all_to_all | solution.py:236
  207.9 1.8 pad_bitcast_fusion
  209.7 1.2 divide_convert_fusion.2
  211.0 0.8 fusion.12
  211.8 1.3 collective-permute-start.4
  213.3 1.8 copy.18.refs_4_
  215.8 1.8 concatenate.26.refs_5_
  217.6 1.2 fusion.16
  218.8 18.7 %collective-permute-done.4 = bf16[1032,128]{1,0:T(8,128)(2,1)} collective-permute-done((bf16[1032,128]{1,0:T(8,128)(2,1)}, bf16[1032,128]{1,0:T(8,128)(2,1)}, u32[]{:S(2)}, u32[]{:S(2)}) %collective-permute-start.4) | collective-permute-done | bytes 264224 | tf_op jit(solution)/shard_map/ppermute | solution.py:20
  237.5 1.2 add_subtract_fusion
  239.4 0.8 sub.58.refs_8_
  240.2 1.4 broadcast_in_dim.16.refs_11_
  241.6 1.3 broadcast_in_dim.13.refs_10_
  242.9 42.5 %shard_map.64 = (bf16[2048,1024]{1,0:T(8,128)(2,1)}, f32[8,128,128]{2,1,0:T(8,128)}, f32[8,8,128]{2,1,0:T(8,128)}) custom-call(bf16[8,128,1024]{2,1,0:T(8,128)(2,1)} %bitcast.67, bf16[8,2048,128]{2,1,0:T(8,128)(2,1)} %copy.17.refs_1_, bf16[8,128,2048]{2,1,0:T(8,128)(2,1)} %bitcast.9.refs_2_, bf16[8,2048,128]{2,1,0:T(8,128)(2,1)} %copy-done.2, ...), custom_call_target="tpu_custom_call" | custom-call | tf_op jit(solution)/shard_map/pallas_call | solution.py:183
  285.5 42.6 %shard_map.65 = bf16[2048,1024]{1,0:T(8,128)(2,1)} custom-call(bf16[8,128,1024]{2,1,0:T(8,128)(2,1)} %bitcast.2.refs_0_, bf16[8,2048,128]{2,1,0:T(8,128)(2,1)} %copy.17.refs_1_, bf16[8,128,2048]{2,1,0:T(8,128)(2,1)} %bitcast.9.refs_2_, bf16[8,2048,128]{2,1,0:T(8,128)(2,1)} %copy-done.2, ...), custom_call_target="tpu_custom_call", output_to_operand_aliasing={{}: (12, {})} | custom-call | tf_op jit(solution)/shard_map/pallas_call | solution.py:183
  (34 shorter events, 5.0 us)
Async XLA Ops:
  0.0 86.1 %copy-start = (bf16[8,128,64]{1,2,0:T(8,128)(2,1)S(1)}, bf16[8,128,64]{1,2,0:T(8,128)(2,1)}, u32[]{:S(2)}) copy-start(bf16[8,128,64]{1,2,0:T(8,128)(2,1)} %param.10) | copy-start | bytes 393220
  4.8 64.3 %all-to-all-start.1 = ((bf16[64,16,2048]{2,0,1:T(8,128)(2,1)}), bf16[64,16,2048]{2,0,1:T(8,128)(2,1)}, u32[]{:S(2)}, u32[]{:S(2)}) async-start(bf16[64,16,2048]{2,0,1:T(8,128)(2,1)} %bitcast.66), calls=%async_computation.1 | async-start | bytes 8388608 | tf_op jit(solution)/shard_map/all_to_all | solution.py:24
  19.5 6.6 %copy-start.5 = (bf16[64,32768]{1,0:T(8,128)(2,1)S(1)}, bf16[64,32768]{1,0:T(8,128)(2,1)}, u32[]{:S(2)}) copy-start(bf16[64,32768]{1,0:T(8,128)(2,1)} %param.8) | copy-start | bytes 12582916
  69.0 10.8 %copy-start.8 = (bf16[8,128,64]{1,2,0:T(8,128)(2,1)S(1)}, bf16[8,128,64]{1,2,0:T(8,128)(2,1)}, u32[]{:S(2)}) copy-start(bf16[8,128,64]{1,2,0:T(8,128)(2,1)} %param.9) | copy-start | bytes 393220
  69.1 11.6 %copy-start.9 = (f32[8]{0:T(128)S(1)}, f32[8]{0:T(128)}, u32[]{:S(2)}) copy-start(f32[8]{0:T(128)} %param.11) | copy-start | bytes 100
  69.1 65.4 %all-to-all-start.2 = ((bf16[64,16,2048]{2,0,1:T(8,128)(2,1)}), bf16[64,16,2048]{2,0,1:T(8,128)(2,1)}, u32[]{:S(2)}, u32[]{:S(2)}) async-start(bf16[64,16,2048]{2,0,1:T(8,128)(2,1)} %bitcast.64), calls=%async_computation.2 | async-start | bytes 8388608 | tf_op jit(solution)/shard_map/all_to_all | solution.py:24
  99.0 7.4 %copy-start.1 = (f32[8,2048,64]{2,1,0:T(8,128)S(1)}, f32[8,2048,64]{2,1,0:T(8,128)}, u32[]{:S(2)}) copy-start(f32[8,2048,64]{2,1,0:T(8,128)} %copy.11) | copy-start | bytes 12582916
  134.4 64.5 %all-to-all-start.3 = ((bf16[16,64,1024]{2,1,0:T(8,128)(2,1)}), bf16[16,64,1024]{2,1,0:T(8,128)(2,1)S(1)}, u32[]{:S(2)}, u32[]{:S(2)}) async-start(bf16[16,64,1024]{2,1,0:T(8,128)(2,1)} %get-tuple-element.19), calls=%async_computation.3 | async-start | bytes 4194304 | tf_op jit(solution)/shard_map/all_to_all | solution.py:236
  145.6 5.5 %copy-start.3 = (bf16[8,2048,64]{2,1,0:T(8,128)(2,1)S(1)}, bf16[8,2048,64]{2,1,0:T(8,128)(2,1)}, u32[]{:S(2)}) copy-start(bf16[8,2048,64]{2,1,0:T(8,128)(2,1)} %divide_convert_fusion.1) | copy-start | bytes 6291460
  153.8 5.0 %copy-start.2 = (bf16[8,2048,128]{2,1,0:T(8,128)(2,1)}, bf16[8,2048,128]{2,1,0:T(8,128)(2,1)S(1)}, u32[]{:S(2)}) copy-start(bf16[8,2048,128]{2,1,0:T(8,128)(2,1)S(1)} %get-tuple-element.18.refs_3_) | copy-start | bytes 12582916
  159.6 19.3 %collective-permute-start = (bf16[2,8,128,64]{3,2,1,0:T(8,128)(2,1)}, bf16[2,8,128,64]{3,2,1,0:T(8,128)(2,1)S(1)}, u32[]{:S(2)}, u32[]{:S(2)}) collective-permute-start(bf16[2,8,128,64]{3,2,1,0:T(8,128)(2,1)} %pad_maximum_fusion.2), channel_id=1, source_target_pairs={{0,1},{1,2},{2,3},{3,4},{4,5},{5,6},{6,7},{7,8},{8,9},{9,10},{10,1... | collective-permute-start | bytes 786440 | tf_op jit(solution)/shard_map/ppermute | solution.py:20
  163.4 20.8 %collective-permute-start.1 = (bf16[1032,128]{1,0:T(8,128)(2,1)}, bf16[1032,128]{1,0:T(8,128)(2,1)S(1)}, u32[]{:S(2)}, u32[]{:S(2)}) collective-permute-start(bf16[1032,128]{1,0:T(8,128)(2,1)} %fusion.13), channel_id=1, source_target_pairs={{0,1},{1,2},{2,3},{3,4},{4,5},{5,6},{6,7},{7,8},{8,9},{9,10},{10,1... | collective-permute-start | bytes 792584 | tf_op jit(solution)/shard_map/ppermute | solution.py:20
  178.9 5.3 %copy-start.6 = (bf16[2,8,128,64]{3,2,1,0:T(8,128)(2,1)}, bf16[2,8,128,64]{3,2,1,0:T(8,128)(2,1)S(1)}, u32[]{:S(2)}) copy-start(bf16[2,8,128,64]{3,2,1,0:T(8,128)(2,1)S(1)} %collective-permute-done) | copy-start | bytes 786436
  185.0 11.8 %collective-permute-start.2 = (bf16[1032,128]{1,0:T(8,128)(2,1)}, bf16[1032,128]{1,0:T(8,128)(2,1)S(1)}, u32[]{:S(2)}, u32[]{:S(2)}) collective-permute-start(bf16[1032,128]{1,0:T(8,128)(2,1)} %fusion.11), channel_id=1, source_target_pairs={{0,2},{1,3},{2,4},{3,5},{4,6},{5,7},{6,8},{7,9},{8,10},{9,11},{10,... | collective-permute-start | bytes 792584 | tf_op jit(solution)/shard_map/ppermute | solution.py:20
  197.6 13.4 %collective-permute-start.3 = (bf16[1032,128]{1,0:T(8,128)(2,1)}, bf16[1032,128]{1,0:T(8,128)(2,1)S(1)}, u32[]{:S(2)}, u32[]{:S(2)}) collective-permute-start(bf16[1032,128]{1,0:T(8,128)(2,1)} %fusion.17), channel_id=1, source_target_pairs={{0,4},{1,5},{2,6},{3,7},{4,8},{5,9},{6,10},{7,11},{8,12},{9,13},{1... | collective-permute-start | bytes 792584 | tf_op jit(solution)/shard_map/ppermute | solution.py:20
  198.9 16.9 %copy-start.4 = (bf16[16,64,1024]{2,1,0:T(8,128)(2,1)}, bf16[16,64,1024]{2,1,0:T(8,128)(2,1)S(1)}, u32[]{:S(2)}) copy-start(bf16[16,64,1024]{2,1,0:T(8,128)(2,1)S(1)} %all-to-all-done.3) | copy-start | bytes 6291460
  198.9 86.6 %all-to-all-start = ((bf16[16,64,1024]{2,1,0:T(8,128)(2,1)}), bf16[16,64,1024]{2,1,0:T(8,128)(2,1)}, u32[]{:S(2)}, u32[]{:S(2)}) async-start(bf16[16,64,1024]{2,1,0:T(8,128)(2,1)} %get-tuple-element.20), calls=%async_computation | async-start | bytes 4194304 | tf_op jit(solution)/shard_map/all_to_all | solution.py:236
  211.0 2.1 copy-start.7
  211.8 25.6 %collective-permute-start.4 = (bf16[1032,128]{1,0:T(8,128)(2,1)}, bf16[1032,128]{1,0:T(8,128)(2,1)}, u32[]{:S(2)}, u32[]{:S(2)}) collective-permute-start(bf16[1032,128]{1,0:T(8,128)(2,1)} %fusion.12), channel_id=1, source_target_pairs={{0,8},{1,9},{2,10},{3,11},{4,12},{5,13},{6,14},{7,15},{16,24},{17,... | collective-permute-start | bytes 792584 | tf_op jit(solution)/shard_map/ppermute | solution.py:20

commit v8 on v7

--- a/solution.py
+++ b/solution.py
@@ -11,6 +11,7 @@
 QB = 128
 HEADS_PER_STEP = 2
 Q_PIECES = 2
+UNROLL = 2
 INTERPRET = False
 
 
@@ -117,9 +118,8 @@
             else:
                 carry.append((st_ref[hh], z_ref[hh][0:1]))
 
-        def loop(i, carry):
-            t0 = pl.multiple_of(i * QB, QB)
-            base = pl.multiple_of(t0 - QB, QB)
+        def one(t0, carry):
+            base = t0 - QB
             out = []
             for hh in range(heads):
                 kw = k_ref[hh, pl.ds(base, 2 * QB), :]
@@ -129,7 +129,18 @@
             return tuple(out)
 
         lo_blk = t_begin // QB + (1 if first else 0)
-        final = lax.fori_loop(lo_blk, t_begin // QB + blocks, loop, tuple(carry))
+        hi_blk = t_begin // QB + blocks
+        pairs = (hi_blk - lo_blk) // UNROLL
+
+        def loop(i, carry):
+            for u in range(UNROLL):
+                t0 = pl.multiple_of((lo_blk + i * UNROLL + u) * QB, QB)
+                carry = one(t0, carry)
+            return carry
+
+        final = lax.fori_loop(0, pairs, loop, tuple(carry))
+        for blk in range(lo_blk + pairs * UNROLL, hi_blk):
+            final = one(blk * QB, final)
         if first:
             for hh in range(heads):
                 st_out[hh] = final[hh][0]

time: 329 us -> 313 us (0.951)
  Pallas kernels: 85.1 us -> 68.3 us
    pallas_call x2, Pallas kernels: 85.1 us -> 68.3 us  [attend(): pl.pallas_call(make_kernel(t_begin, span // QB), grid=(group // hb,), in_...]
  transfers between devices with their start and end apart: 9 -> 9, of which waited for: 6 -> 6; matrix products, arithmetic and copies ran while one was open for 31% -> 32% of each run, Pallas kernels for 13% -> 11%
where the time goes in v8:
time: 313 us; the launch traced here: 311 us
  waiting for transfers between devices  91.6 us (29%)
  Pallas kernels  68.3 us (22%)
  local copies, waits for them, and re-layouts  53.4 us (17%)
  starting transfers between devices  45.9 us (15%)
  other arithmetic  36.7 us (12%)
  matrix products  15.2 us (5%)
    pallas_call x2, Pallas kernels, attend(): pl.pallas_call(make_kernel(t_begin, span // QB), grid=(group // hb,), in_...  68.3 us
    all_to_all x2, waiting for transfers between devices, exchange(): moved = lax.all_to_all(rows, 'seq', split_axis=1, concat_axis=0, tiled=True)  56.9 us
    ppermute x5, waiting for transfers between devices, passed_along(): return lax.ppermute(block, axis, route)  34.7 us
    all_to_all x2, starting transfers between devices, body(): lax.all_to_all(halves[c], 'seq', split_axis=0, concat_axis=0, tiled=True)  19.1 us
    all_to_all x2, starting transfers between devices, exchange(): moved = lax.all_to_all(rows, 'seq', split_axis=1, concat_axis=0, tiled=True)  17.7 us
    reshape x2, local copies, waits for them, and re-layouts, body(): queries.reshape(feature_rows, shards, Q_PIECES, length // Q_PIECES)  14.4 us
    another operation x3, other arithmetic  13.1 us
    ppermute x5, starting transfers between devices, passed_along(): return lax.ppermute(block, axis, route)  9.03 us
  transfers between devices with their start and end apart: 9, of which 6 were waited for; matrix products, arithmetic and copies ran while one was open for 32% of the time, Pallas kernels for 11%

profile of v8, /device:TPU:116, one launch (start us, length us, event | category | flops | bytes accessed | tf_op | source)
XLA Modules:
  0.0 311.3 jit_solution(8252902962637361469)
XLA Ops:
  0.0 4.8 %copy.27 = bf16[8,16,8,2048]{3,2,0,1:T(8,128)(2,1)} copy(bf16[8,16,8,2048]{3,2,1,0:T(8,128)(2,1)} %bitcast.68) | data formatting | bytes 8388608 | tf_op jit(solution)/shard_map/reshape | solution.py:244
  4.8 6.9 %all-to-all-start.1 = ((bf16[64,16,2048]{2,0,1:T(8,128)(2,1)}), bf16[64,16,2048]{2,0,1:T(8,128)(2,1)}, u32[]{:S(2)}, u32[]{:S(2)}) async-start(bf16[64,16,2048]{2,0,1:T(8,128)(2,1)} %bitcast.66), calls=%async_computation.1 | async-start | bytes 8388608 | tf_op jit(solution)/shard_map/all_to_all | solution.py:25
  11.7 7.8 %reshape.51 = bf16[64,16,2,1024]{3,2,1,0:T(2,128)(2,1)} reshape(bf16[64,32768]{1,0:T(8,128)(2,1)} %param.6) | data formatting | bytes 8388608 | tf_op jit(solution)/shard_map/reshape | solution.py:242
  19.5 6.6 %copy.28 = bf16[64,16,2,1024]{3,0,1,2:T(8,128)(2,1)} copy(bf16[64,16,2,1024]{3,2,1,0:T(2,128)(2,1)} %reshape.51) | data formatting | bytes 8388608 | tf_op jit(solution)/shard_map/reshape | solution.py:242
  26.1 2.3 copy.26
  28.4 40.6 %all-to-all-done.1 = bf16[64,16,2048]{2,0,1:T(8,128)(2,1)} async-done(((bf16[64,16,2048]{2,0,1:T(8,128)(2,1)}), bf16[64,16,2048]{2,0,1:T(8,128)(2,1)}, u32[]{:S(2)}, u32[]{:S(2)}) %all-to-all-start.1) | async-done | bytes 4194336 | tf_op jit(solution)/shard_map/all_to_all | solution.py:25
  69.1 10.8 %all-to-all-start.2 = ((bf16[64,16,2048]{2,0,1:T(8,128)(2,1)}), bf16[64,16,2048]{2,0,1:T(8,128)(2,1)}, u32[]{:S(2)}, u32[]{:S(2)}) async-start(bf16[64,16,2048]{2,0,1:T(8,128)(2,1)} %bitcast.64), calls=%async_computation.2 | async-start | bytes 8388608 | tf_op jit(solution)/shard_map/all_to_all | solution.py:25
  81.2 4.9 %slice_bitcast_fusion = (bf16[16,64,1024]{2,1,0:T(8,128)(2,1)}, bf16[16,64,1024]{2,1,0:T(8,128)(2,1)}) fusion(bf16[2,16,64,1024]{3,2,1,0:T(8,128)(2,1)} %bitcast.65), kind=kLoop, calls=%fused_computation.15 | loop fusion | bytes 8388608 | tf_op jit(solution)/shard_map/squeeze | solution.py:247
  86.1 4.9 %fusion.19 = (f32[8,2048]{1,0:T(8,128)S(1)}, f32[8,2048,64]{1,2,0:T(8,128)}) fusion(bf16[8,128,64]{1,2,0:T(8,128)(2,1)S(1)} %copy-done, bf16[8,128,2048]{2,1,0:T(8,128)(2,1)} %bitcast.5), kind=kOutput, calls=%fused_computation.49 | convolution fusion | flops 269467648 | bytes 8585216 | tf_op jit(solution)/shard_map/hdt,hdf->htf/dot_general | solution.py:30
  91.0 6.9 %copy.11 = f32[8,2048,64]{2,1,0:T(8,128)} copy(f32[8,2048,64]{1,2,0:T(8,128)} %get-tuple-element.26) | data formatting | bytes 8388608 | tf_op jit(solution)/shard_map/hdt,hdf->htf/dot_general | solution.py:30
  97.9 1.1 slice_bitcast_fusion.5
  99.0 7.4 %fusion.3 = f32[8,2048]{1,0:T(8,128)S(1)} fusion(f32[8,2048,64]{2,1,0:T(8,128)} %copy.11, f32[8,2048]{1,0:T(8,128)S(1)} %get-tuple-element.25), kind=kLoop, calls=%fused_computation.8 | loop fusion | flops 2080768 | bytes 4325376 | tf_op jit(solution)/shard_map/reduce_sum | solution.py:31
  106.4 5.5 %fusion.18 = (f32[8,2048]{1,0:T(8,128)S(1)}, f32[8,2048,64]{2,1,0:T(8,128)}) fusion(f32[8,2048,64]{2,1,0:T(8,128)S(1)} %copy-done.1), kind=kOutput, calls=%fused_computation.48 | output fusion | flops 4194367 | bytes 8454144 | tf_op jit(solution)/shard_map/sub | solution.py:31
  111.8 6.3 %divide_convert_fusion.1 = bf16[8,2048,64]{2,1,0:T(8,128)(2,1)} fusion(f32[8,2048,64]{2,1,0:T(8,128)S(1)} %copy-done.1, f32[8,2048]{1,0:T(8,128)S(1)} %fusion.3, f32[8,2048]{1,0:T(8,128)S(1)} %get-tuple-element.25), kind=kLoop, calls=%fused_computation.6 | loop fusion | flops 3145728 | bytes 6422528 | tf_op jit(solution)/shard_map/convert.2
  118.2 16.3 %all-to-all-done.2 = bf16[64,16,2048]{2,0,1:T(8,128)(2,1)} async-done(((bf16[64,16,2048]{2,0,1:T(8,128)(2,1)}), bf16[64,16,2048]{2,0,1:T(8,128)(2,1)}, u32[]{:S(2)}, u32[]{:S(2)}) %all-to-all-start.2) | async-done | bytes 4194336 | tf_op jit(solution)/shard_map/all_to_all | solution.py:25
  134.4 10.1 %all-to-all-start.3 = ((bf16[16,64,1024]{2,1,0:T(8,128)(2,1)}), bf16[16,64,1024]{2,1,0:T(8,128)(2,1)S(1)}, u32[]{:S(2)}, u32[]{:S(2)}) async-start(bf16[16,64,1024]{2,1,0:T(8,128)(2,1)} %get-tuple-element.19), calls=%async_computation.3 | async-start | bytes 4194304 | tf_op jit(solution)/shard_map/all_to_all | solution.py:247
  144.5 1.1 slice_bitcast_fusion.4
  145.6 5.5 %divide_convert_fusion = bf16[8,2048,64]{2,1,0:T(8,128)(2,1)S(1)} fusion(f32[8,2048,64]{2,1,0:T(8,128)} %get-tuple-element.24, f32[8,2048]{1,0:T(8,128)S(1)} %get-tuple-element.23), kind=kLoop, calls=%fused_computation.4 | loop fusion | flops 2097152 | bytes 6356992 | tf_op jit(solution)/shard_map/convert.3
  151.1 2.6 convert_reduce_fusion
  153.8 4.9 %fusion.22 = f32[8,128,128]{2,1,0:T(8,128)S(1)} fusion(bf16[8,128,2048]{2,1,0:T(8,128)(2,1)} %bitcast.9.refs_2_, bf16[8,2048,128]{2,1,0:T(8,128)(2,1)S(1)} %get-tuple-element.18.refs_3_), kind=kOutput, calls=%fused_computation.52 | convolution fusion | flops 536870912 | bytes 8912896 | tf_op jit(solution)/shard_map/htf,hdt->hdf/dot_general | solution.py:258
  158.7 0.9 pad_maximum_fusion.2
  159.6 3.1 collective-permute-start
  163.4 2.1 collective-permute-start.1
  166.2 6.5 %copy.17.refs_1_ = bf16[8,2048,128]{2,1,0:T(8,128)(2,1)} copy(bf16[8,2048,128]{1,2,0:T(8,128)(2,1)} %bitcast.6) | data formatting | bytes 8388608 | tf_op jit(solution)/shard_map/transpose | solution.py:226
  172.7 6.3 %collective-permute-done = bf16[2,8,128,64]{3,2,1,0:T(8,128)(2,1)S(1)} collective-permute-done((bf16[2,8,128,64]{3,2,1,0:T(8,128)(2,1)}, bf16[2,8,128,64]{3,2,1,0:T(8,128)(2,1)S(1)}, u32[]{:S(2)}, u32[]{:S(2)}) %collective-permute-start) | collective-permute-done | bytes 262176 | tf_op jit(solution)/shard_map/ppermute | solution.py:21
  178.9 1.6 fusion.20
  180.6 3.6 %collective-permute-done.1 = bf16[1032,128]{1,0:T(8,128)(2,1)S(1)} collective-permute-done((bf16[1032,128]{1,0:T(8,128)(2,1)}, bf16[1032,128]{1,0:T(8,128)(2,1)S(1)}, u32[]{:S(2)}, u32[]{:S(2)}) %collective-permute-start.1) | collective-permute-done | bytes 264224 | tf_op jit(solution)/shard_map/ppermute | solution.py:21
  185.0 1.3 collective-permute-start.2
  186.3 2.6 fusion.21
  188.8 1.9 slice_bitcast_fusion.2
  190.7 6.1 %collective-permute-done.2 = bf16[1032,128]{1,0:T(8,128)(2,1)S(1)} collective-permute-done((bf16[1032,128]{1,0:T(8,128)(2,1)}, bf16[1032,128]{1,0:T(8,128)(2,1)S(1)}, u32[]{:S(2)}, u32[]{:S(2)}) %collective-permute-start.2) | collective-permute-done | bytes 264224 | tf_op jit(solution)/shard_map/ppermute | solution.py:21
  196.8 0.8 fusion.17
  197.6 1.3 collective-permute-start.3
  198.9 9.0 %all-to-all-start = ((bf16[16,64,1024]{2,1,0:T(8,128)(2,1)}), bf16[16,64,1024]{2,1,0:T(8,128)(2,1)}, u32[]{:S(2)}, u32[]{:S(2)}) async-start(bf16[16,64,1024]{2,1,0:T(8,128)(2,1)} %get-tuple-element.20), calls=%async_computation | async-start | bytes 4194304 | tf_op jit(solution)/shard_map/all_to_all | solution.py:247
  207.9 1.8 pad_bitcast_fusion
  209.7 1.2 divide_convert_fusion.2
  211.0 0.8 fusion.12
  211.8 1.3 collective-permute-start.4
  213.3 1.8 copy.18.refs_4_
  215.8 1.8 concatenate.26.refs_5_
  217.6 1.2 fusion.16
  218.8 18.7 %collective-permute-done.4 = bf16[1032,128]{1,0:T(8,128)(2,1)} collective-permute-done((bf16[1032,128]{1,0:T(8,128)(2,1)}, bf16[1032,128]{1,0:T(8,128)(2,1)}, u32[]{:S(2)}, u32[]{:S(2)}) %collective-permute-start.4) | collective-permute-done | bytes 264224 | tf_op jit(solution)/shard_map/ppermute | solution.py:21
  237.5 1.2 add_subtract_fusion
  239.4 0.8 sub.58.refs_8_
  240.2 1.4 broadcast_in_dim.16.refs_11_
  241.6 1.3 broadcast_in_dim.13.refs_10_
  242.9 35.2 %shard_map.64 = (bf16[2048,1024]{1,0:T(8,128)(2,1)}, f32[8,128,128]{2,1,0:T(8,128)}, f32[8,8,128]{2,1,0:T(8,128)}) custom-call(bf16[8,128,1024]{2,1,0:T(8,128)(2,1)} %bitcast.67, bf16[8,2048,128]{2,1,0:T(8,128)(2,1)} %copy.17.refs_1_, bf16[8,128,2048]{2,1,0:T(8,128)(2,1)} %bitcast.9.refs_2_, bf16[8,2048,128]{2,1,0:T(8,128)(2,1)} %copy-done.2, ...), custom_call_target="tpu_custom_call" | custom-call | tf_op jit(solution)/shard_map/pallas_call | solution.py:194
  278.2 33.1 %shard_map.65 = bf16[2048,1024]{1,0:T(8,128)(2,1)} custom-call(bf16[8,128,1024]{2,1,0:T(8,128)(2,1)} %bitcast.2.refs_0_, bf16[8,2048,128]{2,1,0:T(8,128)(2,1)} %copy.17.refs_1_, bf16[8,128,2048]{2,1,0:T(8,128)(2,1)} %bitcast.9.refs_2_, bf16[8,2048,128]{2,1,0:T(8,128)(2,1)} %copy-done.2, ...), custom_call_target="tpu_custom_call", output_to_operand_aliasing={{}: (12, {})} | custom-call | tf_op jit(solution)/shard_map/pallas_call | solution.py:194
  (34 shorter events, 5.0 us)
Async XLA Ops:
  0.0 86.1 %copy-start = (bf16[8,128,64]{1,2,0:T(8,128)(2,1)S(1)}, bf16[8,128,64]{1,2,0:T(8,128)(2,1)}, u32[]{:S(2)}) copy-start(bf16[8,128,64]{1,2,0:T(8,128)(2,1)} %param.10) | copy-start | bytes 393220
  4.8 64.3 %all-to-all-start.1 = ((bf16[64,16,2048]{2,0,1:T(8,128)(2,1)}), bf16[64,16,2048]{2,0,1:T(8,128)(2,1)}, u32[]{:S(2)}, u32[]{:S(2)}) async-start(bf16[64,16,2048]{2,0,1:T(8,128)(2,1)} %bitcast.66), calls=%async_computation.1 | async-start | bytes 8388608 | tf_op jit(solution)/shard_map/all_to_all | solution.py:25
  19.5 6.6 %copy-start.5 = (bf16[64,32768]{1,0:T(8,128)(2,1)S(1)}, bf16[64,32768]{1,0:T(8,128)(2,1)}, u32[]{:S(2)}) copy-start(bf16[64,32768]{1,0:T(8,128)(2,1)} %param.8) | copy-start | bytes 12582916
  69.0 10.8 %copy-start.8 = (bf16[8,128,64]{1,2,0:T(8,128)(2,1)S(1)}, bf16[8,128,64]{1,2,0:T(8,128)(2,1)}, u32[]{:S(2)}) copy-start(bf16[8,128,64]{1,2,0:T(8,128)(2,1)} %param.9) | copy-start | bytes 393220
  69.1 11.6 %copy-start.9 = (f32[8]{0:T(128)S(1)}, f32[8]{0:T(128)}, u32[]{:S(2)}) copy-start(f32[8]{0:T(128)} %param.11) | copy-start | bytes 100
  69.1 65.4 %all-to-all-start.2 = ((bf16[64,16,2048]{2,0,1:T(8,128)(2,1)}), bf16[64,16,2048]{2,0,1:T(8,128)(2,1)}, u32[]{:S(2)}, u32[]{:S(2)}) async-start(bf16[64,16,2048]{2,0,1:T(8,128)(2,1)} %bitcast.64), calls=%async_computation.2 | async-start | bytes 8388608 | tf_op jit(solution)/shard_map/all_to_all | solution.py:25
  99.0 7.4 %copy-start.1 = (f32[8,2048,64]{2,1,0:T(8,128)S(1)}, f32[8,2048,64]{2,1,0:T(8,128)}, u32[]{:S(2)}) copy-start(f32[8,2048,64]{2,1,0:T(8,128)} %copy.11) | copy-start | bytes 12582916
  134.4 64.5 %all-to-all-start.3 = ((bf16[16,64,1024]{2,1,0:T(8,128)(2,1)}), bf16[16,64,1024]{2,1,0:T(8,128)(2,1)S(1)}, u32[]{:S(2)}, u32[]{:S(2)}) async-start(bf16[16,64,1024]{2,1,0:T(8,128)(2,1)} %get-tuple-element.19), calls=%async_computation.3 | async-start | bytes 4194304 | tf_op jit(solution)/shard_map/all_to_all | solution.py:247
  145.6 5.5 %copy-start.3 = (bf16[8,2048,64]{2,1,0:T(8,128)(2,1)S(1)}, bf16[8,2048,64]{2,1,0:T(8,128)(2,1)}, u32[]{:S(2)}) copy-start(bf16[8,2048,64]{2,1,0:T(8,128)(2,1)} %divide_convert_fusion.1) | copy-start | bytes 6291460
  153.8 5.0 %copy-start.2 = (bf16[8,2048,128]{2,1,0:T(8,128)(2,1)}, bf16[8,2048,128]{2,1,0:T(8,128)(2,1)S(1)}, u32[]{:S(2)}) copy-start(bf16[8,2048,128]{2,1,0:T(8,128)(2,1)S(1)} %get-tuple-element.18.refs_3_) | copy-start | bytes 12582916
  159.6 19.3 %collective-permute-start = (bf16[2,8,128,64]{3,2,1,0:T(8,128)(2,1)}, bf16[2,8,128,64]{3,2,1,0:T(8,128)(2,1)S(1)}, u32[]{:S(2)}, u32[]{:S(2)}) collective-permute-start(bf16[2,8,128,64]{3,2,1,0:T(8,128)(2,1)} %pad_maximum_fusion.2), channel_id=1, source_target_pairs={{0,1},{1,2},{2,3},{3,4},{4,5},{5,6},{6,7},{7,8},{8,9},{9,10},{10,1... | collective-permute-start | bytes 786440 | tf_op jit(solution)/shard_map/ppermute | solution.py:21
  163.4 20.8 %collective-permute-start.1 = (bf16[1032,128]{1,0:T(8,128)(2,1)}, bf16[1032,128]{1,0:T(8,128)(2,1)S(1)}, u32[]{:S(2)}, u32[]{:S(2)}) collective-permute-start(bf16[1032,128]{1,0:T(8,128)(2,1)} %fusion.13), channel_id=1, source_target_pairs={{0,1},{1,2},{2,3},{3,4},{4,5},{5,6},{6,7},{7,8},{8,9},{9,10},{10,1... | collective-permute-start | bytes 792584 | tf_op jit(solution)/shard_map/ppermute | solution.py:21
  178.9 5.3 %copy-start.6 = (bf16[2,8,128,64]{3,2,1,0:T(8,128)(2,1)}, bf16[2,8,128,64]{3,2,1,0:T(8,128)(2,1)S(1)}, u32[]{:S(2)}) copy-start(bf16[2,8,128,64]{3,2,1,0:T(8,128)(2,1)S(1)} %collective-permute-done) | copy-start | bytes 786436
  185.0 11.8 %collective-permute-start.2 = (bf16[1032,128]{1,0:T(8,128)(2,1)}, bf16[1032,128]{1,0:T(8,128)(2,1)S(1)}, u32[]{:S(2)}, u32[]{:S(2)}) collective-permute-start(bf16[1032,128]{1,0:T(8,128)(2,1)} %fusion.11), channel_id=1, source_target_pairs={{0,2},{1,3},{2,4},{3,5},{4,6},{5,7},{6,8},{7,9},{8,10},{9,11},{10,... | collective-permute-start | bytes 792584 | tf_op jit(solution)/shard_map/ppermute | solution.py:21
  197.6 13.4 %collective-permute-start.3 = (bf16[1032,128]{1,0:T(8,128)(2,1)}, bf16[1032,128]{1,0:T(8,128)(2,1)S(1)}, u32[]{:S(2)}, u32[]{:S(2)}) collective-permute-start(bf16[1032,128]{1,0:T(8,128)(2,1)} %fusion.17), channel_id=1, source_target_pairs={{0,4},{1,5},{2,6},{3,7},{4,8},{5,9},{6,10},{7,11},{8,12},{9,13},{1... | collective-permute-start | bytes 792584 | tf_op jit(solution)/shard_map/ppermute | solution.py:21
  198.9 16.9 %copy-start.4 = (bf16[16,64,1024]{2,1,0:T(8,128)(2,1)}, bf16[16,64,1024]{2,1,0:T(8,128)(2,1)S(1)}, u32[]{:S(2)}) copy-start(bf16[16,64,1024]{2,1,0:T(8,128)(2,1)S(1)} %all-to-all-done.3) | copy-start | bytes 6291460
  198.9 79.3 %all-to-all-start = ((bf16[16,64,1024]{2,1,0:T(8,128)(2,1)}), bf16[16,64,1024]{2,1,0:T(8,128)(2,1)}, u32[]{:S(2)}, u32[]{:S(2)}) async-start(bf16[16,64,1024]{2,1,0:T(8,128)(2,1)} %get-tuple-element.20), calls=%async_computation | async-start | bytes 4194304 | tf_op jit(solution)/shard_map/all_to_all | solution.py:247
  211.0 2.1 copy-start.7
  211.8 25.6 %collective-permute-start.4 = (bf16[1032,128]{1,0:T(8,128)(2,1)}, bf16[1032,128]{1,0:T(8,128)(2,1)}, u32[]{:S(2)}, u32[]{:S(2)}) collective-permute-start(bf16[1032,128]{1,0:T(8,128)(2,1)} %fusion.12), channel_id=1, source_target_pairs={{0,8},{1,9},{2,10},{3,11},{4,12},{5,13},{6,14},{7,15},{16,24},{17,... | collective-permute-start | bytes 792584 | tf_op jit(solution)/shard_map/ppermute | solution.py:21

commit v9 on v8

--- a/solution.py
+++ b/solution.py
@@ -11,7 +11,7 @@
 QB = 128
 HEADS_PER_STEP = 2
 Q_PIECES = 2
-UNROLL = 2
+UNROLL = 4
 INTERPRET = False
 
 

time: 313 us -> 299 us (0.955)
  Pallas kernels: 68.3 us -> 54.4 us
    pallas_call x2, Pallas kernels: 68.3 us -> 54.4 us  [attend(): pl.pallas_call(make_kernel(t_begin, span // QB), grid=(group // hb,), in_...]
  transfers between devices with their start and end apart: 9 -> 9, of which waited for: 6 -> 6; matrix products, arithmetic and copies ran while one was open for 32% -> 34% of each run, Pallas kernels for 11% -> 9%
where the time goes in v9:
time: 299 us; the launch traced here: 297 us
  waiting for transfers between devices  91.6 us (31%)
  Pallas kernels  54.4 us (18%)
  local copies, waits for them, and re-layouts  53.4 us (18%)
  starting transfers between devices  45.9 us (15%)
  other arithmetic  36.7 us (12%)
  matrix products  15.2 us (5%)
    all_to_all x2, waiting for transfers between devices, exchange(): moved = lax.all_to_all(rows, 'seq', split_axis=1, concat_axis=0, tiled=True)  56.9 us
    pallas_call x2, Pallas kernels, attend(): pl.pallas_call(make_kernel(t_begin, span // QB), grid=(group // hb,), in_...  54.4 us
    ppermute x5, waiting for transfers between devices, passed_along(): return lax.ppermute(block, axis, route)  34.7 us
    all_to_all x2, starting transfers between devices, body(): lax.all_to_all(halves[c], 'seq', split_axis=0, concat_axis=0, tiled=True)  19.1 us
    all_to_all x2, starting transfers between devices, exchange(): moved = lax.all_to_all(rows, 'seq', split_axis=1, concat_axis=0, tiled=True)  17.7 us
    reshape x2, local copies, waits for them, and re-layouts, body(): queries.reshape(feature_rows, shards, Q_PIECES, length // Q_PIECES)  14.4 us
    another operation x3, other arithmetic  13.1 us
    ppermute x5, starting transfers between devices, passed_along(): return lax.ppermute(block, axis, route)  9.03 us
  transfers between devices with their start and end apart: 9, of which 6 were waited for; matrix products, arithmetic and copies ran while one was open for 34% of the time, Pallas kernels for 9%

profile of v9, /device:TPU:116, one launch (start us, length us, event | category | flops | bytes accessed | tf_op | source)
XLA Modules:
  0.0 297.4 jit_solution(5193033280519078559)
XLA Ops:
  0.0 4.8 %copy.27 = bf16[8,16,8,2048]{3,2,0,1:T(8,128)(2,1)} copy(bf16[8,16,8,2048]{3,2,1,0:T(8,128)(2,1)} %bitcast.68) | data formatting | bytes 8388608 | tf_op jit(solution)/shard_map/reshape | solution.py:244
  4.8 6.9 %all-to-all-start.1 = ((bf16[64,16,2048]{2,0,1:T(8,128)(2,1)}), bf16[64,16,2048]{2,0,1:T(8,128)(2,1)}, u32[]{:S(2)}, u32[]{:S(2)}) async-start(bf16[64,16,2048]{2,0,1:T(8,128)(2,1)} %bitcast.66), calls=%async_computation.1 | async-start | bytes 8388608 | tf_op jit(solution)/shard_map/all_to_all | solution.py:25
  11.7 7.8 %reshape.51 = bf16[64,16,2,1024]{3,2,1,0:T(2,128)(2,1)} reshape(bf16[64,32768]{1,0:T(8,128)(2,1)} %param.6) | data formatting | bytes 8388608 | tf_op jit(solution)/shard_map/reshape | solution.py:242
  19.5 6.6 %copy.28 = bf16[64,16,2,1024]{3,0,1,2:T(8,128)(2,1)} copy(bf16[64,16,2,1024]{3,2,1,0:T(2,128)(2,1)} %reshape.51) | data formatting | bytes 8388608 | tf_op jit(solution)/shard_map/reshape | solution.py:242
  26.1 2.3 copy.26
  28.4 40.6 %all-to-all-done.1 = bf16[64,16,2048]{2,0,1:T(8,128)(2,1)} async-done(((bf16[64,16,2048]{2,0,1:T(8,128)(2,1)}), bf16[64,16,2048]{2,0,1:T(8,128)(2,1)}, u32[]{:S(2)}, u32[]{:S(2)}) %all-to-all-start.1) | async-done | bytes 4194336 | tf_op jit(solution)/shard_map/all_to_all | solution.py:25
  69.1 10.8 %all-to-all-start.2 = ((bf16[64,16,2048]{2,0,1:T(8,128)(2,1)}), bf16[64,16,2048]{2,0,1:T(8,128)(2,1)}, u32[]{:S(2)}, u32[]{:S(2)}) async-start(bf16[64,16,2048]{2,0,1:T(8,128)(2,1)} %bitcast.64), calls=%async_computation.2 | async-start | bytes 8388608 | tf_op jit(solution)/shard_map/all_to_all | solution.py:25
  81.2 4.9 %slice_bitcast_fusion = (bf16[16,64,1024]{2,1,0:T(8,128)(2,1)}, bf16[16,64,1024]{2,1,0:T(8,128)(2,1)}) fusion(bf16[2,16,64,1024]{3,2,1,0:T(8,128)(2,1)} %bitcast.65), kind=kLoop, calls=%fused_computation.15 | loop fusion | bytes 8388608 | tf_op jit(solution)/shard_map/squeeze | solution.py:247
  86.1 4.9 %fusion.19 = (f32[8,2048]{1,0:T(8,128)S(1)}, f32[8,2048,64]{1,2,0:T(8,128)}) fusion(bf16[8,128,64]{1,2,0:T(8,128)(2,1)S(1)} %copy-done, bf16[8,128,2048]{2,1,0:T(8,128)(2,1)} %bitcast.5), kind=kOutput, calls=%fused_computation.49 | convolution fusion | flops 269467648 | bytes 8585216 | tf_op jit(solution)/shard_map/hdt,hdf->htf/dot_general | solution.py:30
  91.0 6.9 %copy.11 = f32[8,2048,64]{2,1,0:T(8,128)} copy(f32[8,2048,64]{1,2,0:T(8,128)} %get-tuple-element.26) | data formatting | bytes 8388608 | tf_op jit(solution)/shard_map/hdt,hdf->htf/dot_general | solution.py:30
  97.9 1.1 slice_bitcast_fusion.5
  99.0 7.4 %fusion.3 = f32[8,2048]{1,0:T(8,128)S(1)} fusion(f32[8,2048,64]{2,1,0:T(8,128)} %copy.11, f32[8,2048]{1,0:T(8,128)S(1)} %get-tuple-element.25), kind=kLoop, calls=%fused_computation.8 | loop fusion | flops 2080768 | bytes 4325376 | tf_op jit(solution)/shard_map/reduce_sum | solution.py:31
  106.4 5.5 %fusion.18 = (f32[8,2048]{1,0:T(8,128)S(1)}, f32[8,2048,64]{2,1,0:T(8,128)}) fusion(f32[8,2048,64]{2,1,0:T(8,128)S(1)} %copy-done.1), kind=kOutput, calls=%fused_computation.48 | output fusion | flops 4194367 | bytes 8454144 | tf_op jit(solution)/shard_map/sub | solution.py:31
  111.8 6.3 %divide_convert_fusion.1 = bf16[8,2048,64]{2,1,0:T(8,128)(2,1)} fusion(f32[8,2048,64]{2,1,0:T(8,128)S(1)} %copy-done.1, f32[8,2048]{1,0:T(8,128)S(1)} %fusion.3, f32[8,2048]{1,0:T(8,128)S(1)} %get-tuple-element.25), kind=kLoop, calls=%fused_computation.6 | loop fusion | flops 3145728 | bytes 6422528 | tf_op jit(solution)/shard_map/convert.2
  118.2 16.3 %all-to-all-done.2 = bf16[64,16,2048]{2,0,1:T(8,128)(2,1)} async-done(((bf16[64,16,2048]{2,0,1:T(8,128)(2,1)}), bf16[64,16,2048]{2,0,1:T(8,128)(2,1)}, u32[]{:S(2)}, u32[]{:S(2)}) %all-to-all-start.2) | async-done | bytes 4194336 | tf_op jit(solution)/shard_map/all_to_all | solution.py:25
  134.4 10.1 %all-to-all-start.3 = ((bf16[16,64,1024]{2,1,0:T(8,128)(2,1)}), bf16[16,64,1024]{2,1,0:T(8,128)(2,1)S(1)}, u32[]{:S(2)}, u32[]{:S(2)}) async-start(bf16[16,64,1024]{2,1,0:T(8,128)(2,1)} %get-tuple-element.19), calls=%async_computation.3 | async-start | bytes 4194304 | tf_op jit(solution)/shard_map/all_to_all | solution.py:247
  144.5 1.1 slice_bitcast_fusion.4
  145.6 5.5 %divide_convert_fusion = bf16[8,2048,64]{2,1,0:T(8,128)(2,1)S(1)} fusion(f32[8,2048,64]{2,1,0:T(8,128)} %get-tuple-element.24, f32[8,2048]{1,0:T(8,128)S(1)} %get-tuple-element.23), kind=kLoop, calls=%fused_computation.4 | loop fusion | flops 2097152 | bytes 6356992 | tf_op jit(solution)/shard_map/convert.3
  151.1 2.6 convert_reduce_fusion
  153.8 4.9 %fusion.22 = f32[8,128,128]{2,1,0:T(8,128)S(1)} fusion(bf16[8,128,2048]{2,1,0:T(8,128)(2,1)} %bitcast.9.refs_2_, bf16[8,2048,128]{2,1,0:T(8,128)(2,1)S(1)} %get-tuple-element.18.refs_3_), kind=kOutput, calls=%fused_computation.52 | convolution fusion | flops 536870912 | bytes 8912896 | tf_op jit(solution)/shard_map/htf,hdt->hdf/dot_general | solution.py:258
  158.7 0.9 pad_maximum_fusion.2
  159.6 3.1 %collective-permute-start = (bf16[2,8,128,64]{3,2,1,0:T(8,128)(2,1)}, bf16[2,8,128,64]{3,2,1,0:T(8,128)(2,1)S(1)}, u32[]{:S(2)}, u32[]{:S(2)}) collective-permute-start(bf16[2,8,128,64]{3,2,1,0:T(8,128)(2,1)} %pad_maximum_fusion.2), channel_id=1, source_target_pairs={{0,1},{1,2},{2,3},{3,4},{4,5},{5,6},{6,7},{7,8},{8,9},{9,10},{10,1... | collective-permute-start | bytes 786440 | tf_op jit(solution)/shard_map/ppermute | solution.py:21
  163.4 2.1 collective-permute-start.1
  166.2 6.5 %copy.17.refs_1_ = bf16[8,2048,128]{2,1,0:T(8,128)(2,1)} copy(bf16[8,2048,128]{1,2,0:T(8,128)(2,1)} %bitcast.6) | data formatting | bytes 8388608 | tf_op jit(solution)/shard_map/transpose | solution.py:226
  172.7 6.3 %collective-permute-done = bf16[2,8,128,64]{3,2,1,0:T(8,128)(2,1)S(1)} collective-permute-done((bf16[2,8,128,64]{3,2,1,0:T(8,128)(2,1)}, bf16[2,8,128,64]{3,2,1,0:T(8,128)(2,1)S(1)}, u32[]{:S(2)}, u32[]{:S(2)}) %collective-permute-start) | collective-permute-done | bytes 262176 | tf_op jit(solution)/shard_map/ppermute | solution.py:21
  178.9 1.6 fusion.20
  180.6 3.6 %collective-permute-done.1 = bf16[1032,128]{1,0:T(8,128)(2,1)S(1)} collective-permute-done((bf16[1032,128]{1,0:T(8,128)(2,1)}, bf16[1032,128]{1,0:T(8,128)(2,1)S(1)}, u32[]{:S(2)}, u32[]{:S(2)}) %collective-permute-start.1) | collective-permute-done | bytes 264224 | tf_op jit(solution)/shard_map/ppermute | solution.py:21
  185.0 1.3 collective-permute-start.2
  186.3 2.6 fusion.21
  188.8 1.9 slice_bitcast_fusion.2
  190.7 6.1 %collective-permute-done.2 = bf16[1032,128]{1,0:T(8,128)(2,1)S(1)} collective-permute-done((bf16[1032,128]{1,0:T(8,128)(2,1)}, bf16[1032,128]{1,0:T(8,128)(2,1)S(1)}, u32[]{:S(2)}, u32[]{:S(2)}) %collective-permute-start.2) | collective-permute-done | bytes 264224 | tf_op jit(solution)/shard_map/ppermute | solution.py:21
  196.8 0.8 fusion.17
  197.6 1.3 collective-permute-start.3
  198.9 9.0 %all-to-all-start = ((bf16[16,64,1024]{2,1,0:T(8,128)(2,1)}), bf16[16,64,1024]{2,1,0:T(8,128)(2,1)}, u32[]{:S(2)}, u32[]{:S(2)}) async-start(bf16[16,64,1024]{2,1,0:T(8,128)(2,1)} %get-tuple-element.20), calls=%async_computation | async-start | bytes 4194304 | tf_op jit(solution)/shard_map/all_to_all | solution.py:247
  207.9 1.8 pad_bitcast_fusion
  209.7 1.2 divide_convert_fusion.2
  211.0 0.8 fusion.12
  211.8 1.3 collective-permute-start.4
  213.3 1.8 copy.18.refs_4_
  215.8 1.8 concatenate.26.refs_5_
  217.6 1.2 fusion.16
  218.8 18.7 %collective-permute-done.4 = bf16[1032,128]{1,0:T(8,128)(2,1)} collective-permute-done((bf16[1032,128]{1,0:T(8,128)(2,1)}, bf16[1032,128]{1,0:T(8,128)(2,1)}, u32[]{:S(2)}, u32[]{:S(2)}) %collective-permute-start.4) | collective-permute-done | bytes 264224 | tf_op jit(solution)/shard_map/ppermute | solution.py:21
  237.5 1.2 add_subtract_fusion
  239.4 0.8 sub.58.refs_8_
  240.2 1.4 broadcast_in_dim.16.refs_11_
  241.6 1.3 broadcast_in_dim.13.refs_10_
  242.9 26.0 %shard_map.64 = (bf16[2048,1024]{1,0:T(8,128)(2,1)}, f32[8,128,128]{2,1,0:T(8,128)}, f32[8,8,128]{2,1,0:T(8,128)}) custom-call(bf16[8,128,1024]{2,1,0:T(8,128)(2,1)} %bitcast.67, bf16[8,2048,128]{2,1,0:T(8,128)(2,1)} %copy.17.refs_1_, bf16[8,128,2048]{2,1,0:T(8,128)(2,1)} %bitcast.9.refs_2_, bf16[8,2048,128]{2,1,0:T(8,128)(2,1)} %copy-done.2, ...), custom_call_target="tpu_custom_call" | custom-call | tf_op jit(solution)/shard_map/pallas_call | solution.py:194
  269.0 28.4 %shard_map.65 = bf16[2048,1024]{1,0:T(8,128)(2,1)} custom-call(bf16[8,128,1024]{2,1,0:T(8,128)(2,1)} %bitcast.2.refs_0_, bf16[8,2048,128]{2,1,0:T(8,128)(2,1)} %copy.17.refs_1_, bf16[8,128,2048]{2,1,0:T(8,128)(2,1)} %bitcast.9.refs_2_, bf16[8,2048,128]{2,1,0:T(8,128)(2,1)} %copy-done.2, ...), custom_call_target="tpu_custom_call", output_to_operand_aliasing={{}: (12, {})} | custom-call | tf_op jit(solution)/shard_map/pallas_call | solution.py:194
  (34 shorter events, 5.0 us)
Async XLA Ops:
  0.0 86.1 %copy-start = (bf16[8,128,64]{1,2,0:T(8,128)(2,1)S(1)}, bf16[8,128,64]{1,2,0:T(8,128)(2,1)}, u32[]{:S(2)}) copy-start(bf16[8,128,64]{1,2,0:T(8,128)(2,1)} %param.10) | copy-start | bytes 393220
  4.8 64.3 %all-to-all-start.1 = ((bf16[64,16,2048]{2,0,1:T(8,128)(2,1)}), bf16[64,16,2048]{2,0,1:T(8,128)(2,1)}, u32[]{:S(2)}, u32[]{:S(2)}) async-start(bf16[64,16,2048]{2,0,1:T(8,128)(2,1)} %bitcast.66), calls=%async_computation.1 | async-start | bytes 8388608 | tf_op jit(solution)/shard_map/all_to_all | solution.py:25
  19.5 6.6 %copy-start.5 = (bf16[64,32768]{1,0:T(8,128)(2,1)S(1)}, bf16[64,32768]{1,0:T(8,128)(2,1)}, u32[]{:S(2)}) copy-start(bf16[64,32768]{1,0:T(8,128)(2,1)} %param.8) | copy-start | bytes 12582916
  69.0 10.8 %copy-start.8 = (bf16[8,128,64]{1,2,0:T(8,128)(2,1)S(1)}, bf16[8,128,64]{1,2,0:T(8,128)(2,1)}, u32[]{:S(2)}) copy-start(bf16[8,128,64]{1,2,0:T(8,128)(2,1)} %param.9) | copy-start | bytes 393220
  69.1 11.6 %copy-start.9 = (f32[8]{0:T(128)S(1)}, f32[8]{0:T(128)}, u32[]{:S(2)}) copy-start(f32[8]{0:T(128)} %param.11) | copy-start | bytes 100
  69.1 65.4 %all-to-all-start.2 = ((bf16[64,16,2048]{2,0,1:T(8,128)(2,1)}), bf16[64,16,2048]{2,0,1:T(8,128)(2,1)}, u32[]{:S(2)}, u32[]{:S(2)}) async-start(bf16[64,16,2048]{2,0,1:T(8,128)(2,1)} %bitcast.64), calls=%async_computation.2 | async-start | bytes 8388608 | tf_op jit(solution)/shard_map/all_to_all | solution.py:25
  99.0 7.4 %copy-start.1 = (f32[8,2048,64]{2,1,0:T(8,128)S(1)}, f32[8,2048,64]{2,1,0:T(8,128)}, u32[]{:S(2)}) copy-start(f32[8,2048,64]{2,1,0:T(8,128)} %copy.11) | copy-start | bytes 12582916
  134.4 64.5 %all-to-all-start.3 = ((bf16[16,64,1024]{2,1,0:T(8,128)(2,1)}), bf16[16,64,1024]{2,1,0:T(8,128)(2,1)S(1)}, u32[]{:S(2)}, u32[]{:S(2)}) async-start(bf16[16,64,1024]{2,1,0:T(8,128)(2,1)} %get-tuple-element.19), calls=%async_computation.3 | async-start | bytes 4194304 | tf_op jit(solution)/shard_map/all_to_all | solution.py:247
  145.6 5.5 %copy-start.3 = (bf16[8,2048,64]{2,1,0:T(8,128)(2,1)S(1)}, bf16[8,2048,64]{2,1,0:T(8,128)(2,1)}, u32[]{:S(2)}) copy-start(bf16[8,2048,64]{2,1,0:T(8,128)(2,1)} %divide_convert_fusion.1) | copy-start | bytes 6291460
  153.8 5.0 %copy-start.2 = (bf16[8,2048,128]{2,1,0:T(8,128)(2,1)}, bf16[8,2048,128]{2,1,0:T(8,128)(2,1)S(1)}, u32[]{:S(2)}) copy-start(bf16[8,2048,128]{2,1,0:T(8,128)(2,1)S(1)} %get-tuple-element.18.refs_3_) | copy-start | bytes 12582916
  159.6 19.3 %collective-permute-start = (bf16[2,8,128,64]{3,2,1,0:T(8,128)(2,1)}, bf16[2,8,128,64]{3,2,1,0:T(8,128)(2,1)S(1)}, u32[]{:S(2)}, u32[]{:S(2)}) collective-permute-start(bf16[2,8,128,64]{3,2,1,0:T(8,128)(2,1)} %pad_maximum_fusion.2), channel_id=1, source_target_pairs={{0,1},{1,2},{2,3},{3,4},{4,5},{5,6},{6,7},{7,8},{8,9},{9,10},{10,1... | collective-permute-start | bytes 786440 | tf_op jit(solution)/shard_map/ppermute | solution.py:21
  163.4 20.8 %collective-permute-start.1 = (bf16[1032,128]{1,0:T(8,128)(2,1)}, bf16[1032,128]{1,0:T(8,128)(2,1)S(1)}, u32[]{:S(2)}, u32[]{:S(2)}) collective-permute-start(bf16[1032,128]{1,0:T(8,128)(2,1)} %fusion.13), channel_id=1, source_target_pairs={{0,1},{1,2},{2,3},{3,4},{4,5},{5,6},{6,7},{7,8},{8,9},{9,10},{10,1... | collective-permute-start | bytes 792584 | tf_op jit(solution)/shard_map/ppermute | solution.py:21
  178.9 5.3 %copy-start.6 = (bf16[2,8,128,64]{3,2,1,0:T(8,128)(2,1)}, bf16[2,8,128,64]{3,2,1,0:T(8,128)(2,1)S(1)}, u32[]{:S(2)}) copy-start(bf16[2,8,128,64]{3,2,1,0:T(8,128)(2,1)S(1)} %collective-permute-done) | copy-start | bytes 786436
  185.0 11.8 %collective-permute-start.2 = (bf16[1032,128]{1,0:T(8,128)(2,1)}, bf16[1032,128]{1,0:T(8,128)(2,1)S(1)}, u32[]{:S(2)}, u32[]{:S(2)}) collective-permute-start(bf16[1032,128]{1,0:T(8,128)(2,1)} %fusion.11), channel_id=1, source_target_pairs={{0,2},{1,3},{2,4},{3,5},{4,6},{5,7},{6,8},{7,9},{8,10},{9,11},{10,... | collective-permute-start | bytes 792584 | tf_op jit(solution)/shard_map/ppermute | solution.py:21
  197.6 13.4 %collective-permute-start.3 = (bf16[1032,128]{1,0:T(8,128)(2,1)}, bf16[1032,128]{1,0:T(8,128)(2,1)S(1)}, u32[]{:S(2)}, u32[]{:S(2)}) collective-permute-start(bf16[1032,128]{1,0:T(8,128)(2,1)} %fusion.17), channel_id=1, source_target_pairs={{0,4},{1,5},{2,6},{3,7},{4,8},{5,9},{6,10},{7,11},{8,12},{9,13},{1... | collective-permute-start | bytes 792584 | tf_op jit(solution)/shard_map/ppermute | solution.py:21
  198.9 16.9 %copy-start.4 = (bf16[16,64,1024]{2,1,0:T(8,128)(2,1)}, bf16[16,64,1024]{2,1,0:T(8,128)(2,1)S(1)}, u32[]{:S(2)}) copy-start(bf16[16,64,1024]{2,1,0:T(8,128)(2,1)S(1)} %all-to-all-done.3) | copy-start | bytes 6291460
  198.9 70.1 %all-to-all-start = ((bf16[16,64,1024]{2,1,0:T(8,128)(2,1)}), bf16[16,64,1024]{2,1,0:T(8,128)(2,1)}, u32[]{:S(2)}, u32[]{:S(2)}) async-start(bf16[16,64,1024]{2,1,0:T(8,128)(2,1)} %get-tuple-element.20), calls=%async_computation | async-start | bytes 4194304 | tf_op jit(solution)/shard_map/all_to_all | solution.py:247
  211.0 2.1 copy-start.7
  211.8 25.6 %collective-permute-start.4 = (bf16[1032,128]{1,0:T(8,128)(2,1)}, bf16[1032,128]{1,0:T(8,128)(2,1)}, u32[]{:S(2)}, u32[]{:S(2)}) collective-permute-start(bf16[1032,128]{1,0:T(8,128)(2,1)} %fusion.12), channel_id=1, source_target_pairs={{0,8},{1,9},{2,10},{3,11},{4,12},{5,13},{6,14},{7,15},{16,24},{17,... | collective-permute-start | bytes 792584 | tf_op jit(solution)/shard_map/ppermute | solution.py:21

commit v10 on v9

--- a/solution.py
+++ b/solution.py
@@ -11,7 +11,7 @@
 QB = 128
 HEADS_PER_STEP = 2
 Q_PIECES = 2
-UNROLL = 4
+UNROLL = 8
 INTERPRET = False
 
 

time: 299 us -> 296 us (0.990)
  no operation moved by 1% of the time
where the time goes in v10:
time: 296 us; the launch traced here: 295 us
  waiting for transfers between devices  91.6 us (31%)
  local copies, waits for them, and re-layouts  53.4 us (18%)
  Pallas kernels  51.8 us (18%)
  starting transfers between devices  45.9 us (16%)
  other arithmetic  36.7 us (12%)
  matrix products  15.2 us (5%)
    all_to_all x2, waiting for transfers between devices, exchange(): moved = lax.all_to_all(rows, 'seq', split_axis=1, concat_axis=0, tiled=True)  56.9 us
    pallas_call x2, Pallas kernels, attend(): pl.pallas_call(make_kernel(t_begin, span // QB), grid=(group // hb,), in_...  51.8 us
    ppermute x5, waiting for transfers between devices, passed_along(): return lax.ppermute(block, axis, route)  34.7 us
    all_to_all x2, starting transfers between devices, body(): lax.all_to_all(halves[c], 'seq', split_axis=0, concat_axis=0, tiled=True)  19.1 us
    all_to_all x2, starting transfers between devices, exchange(): moved = lax.all_to_all(rows, 'seq', split_axis=1, concat_axis=0, tiled=True)  17.7 us
    reshape x2, local copies, waits for them, and re-layouts, body(): queries.reshape(feature_rows, shards, Q_PIECES, length // Q_PIECES)  14.4 us
    another operation x3, other arithmetic  13.1 us
    ppermute x5, starting transfers between devices, passed_along(): return lax.ppermute(block, axis, route)  9.03 us
  transfers between devices with their start and end apart: 9, of which 6 were waited for; matrix products, arithmetic and copies ran while one was open for 34% of the time, Pallas kernels for 9%

profile of v10, /device:TPU:116, one launch (start us, length us, event | category | flops | bytes accessed | tf_op | source)
XLA Modules:
  0.0 294.7 jit_solution(961021721293970635)
XLA Ops:
  0.0 4.8 %copy.27 = bf16[8,16,8,2048]{3,2,0,1:T(8,128)(2,1)} copy(bf16[8,16,8,2048]{3,2,1,0:T(8,128)(2,1)} %bitcast.68) | data formatting | bytes 8388608 | tf_op jit(solution)/shard_map/reshape | solution.py:244
  4.8 6.9 %all-to-all-start.1 = ((bf16[64,16,2048]{2,0,1:T(8,128)(2,1)}), bf16[64,16,2048]{2,0,1:T(8,128)(2,1)}, u32[]{:S(2)}, u32[]{:S(2)}) async-start(bf16[64,16,2048]{2,0,1:T(8,128)(2,1)} %bitcast.66), calls=%async_computation.1 | async-start | bytes 8388608 | tf_op jit(solution)/shard_map/all_to_all | solution.py:25
  11.7 7.8 %reshape.51 = bf16[64,16,2,1024]{3,2,1,0:T(2,128)(2,1)} reshape(bf16[64,32768]{1,0:T(8,128)(2,1)} %param.6) | data formatting | bytes 8388608 | tf_op jit(solution)/shard_map/reshape | solution.py:242
  19.5 6.6 %copy.28 = bf16[64,16,2,1024]{3,0,1,2:T(8,128)(2,1)} copy(bf16[64,16,2,1024]{3,2,1,0:T(2,128)(2,1)} %reshape.51) | data formatting | bytes 8388608 | tf_op jit(solution)/shard_map/reshape | solution.py:242
  26.1 2.3 copy.26
  28.4 40.6 %all-to-all-done.1 = bf16[64,16,2048]{2,0,1:T(8,128)(2,1)} async-done(((bf16[64,16,2048]{2,0,1:T(8,128)(2,1)}), bf16[64,16,2048]{2,0,1:T(8,128)(2,1)}, u32[]{:S(2)}, u32[]{:S(2)}) %all-to-all-start.1) | async-done | bytes 4194336 | tf_op jit(solution)/shard_map/all_to_all | solution.py:25
  69.1 10.8 %all-to-all-start.2 = ((bf16[64,16,2048]{2,0,1:T(8,128)(2,1)}), bf16[64,16,2048]{2,0,1:T(8,128)(2,1)}, u32[]{:S(2)}, u32[]{:S(2)}) async-start(bf16[64,16,2048]{2,0,1:T(8,128)(2,1)} %bitcast.64), calls=%async_computation.2 | async-start | bytes 8388608 | tf_op jit(solution)/shard_map/all_to_all | solution.py:25
  81.2 4.9 %slice_bitcast_fusion = (bf16[16,64,1024]{2,1,0:T(8,128)(2,1)}, bf16[16,64,1024]{2,1,0:T(8,128)(2,1)}) fusion(bf16[2,16,64,1024]{3,2,1,0:T(8,128)(2,1)} %bitcast.65), kind=kLoop, calls=%fused_computation.15 | loop fusion | bytes 8388608 | tf_op jit(solution)/shard_map/squeeze | solution.py:247
  86.1 4.9 %fusion.19 = (f32[8,2048]{1,0:T(8,128)S(1)}, f32[8,2048,64]{1,2,0:T(8,128)}) fusion(bf16[8,128,64]{1,2,0:T(8,128)(2,1)S(1)} %copy-done, bf16[8,128,2048]{2,1,0:T(8,128)(2,1)} %bitcast.5), kind=kOutput, calls=%fused_computation.49 | convolution fusion | flops 269467648 | bytes 8585216 | tf_op jit(solution)/shard_map/hdt,hdf->htf/dot_general | solution.py:30
  91.0 6.9 %copy.11 = f32[8,2048,64]{2,1,0:T(8,128)} copy(f32[8,2048,64]{1,2,0:T(8,128)} %get-tuple-element.26) | data formatting | bytes 8388608 | tf_op jit(solution)/shard_map/hdt,hdf->htf/dot_general | solution.py:30
  97.9 1.1 slice_bitcast_fusion.5
  99.0 7.4 %fusion.3 = f32[8,2048]{1,0:T(8,128)S(1)} fusion(f32[8,2048,64]{2,1,0:T(8,128)} %copy.11, f32[8,2048]{1,0:T(8,128)S(1)} %get-tuple-element.25), kind=kLoop, calls=%fused_computation.8 | loop fusion | flops 2080768 | bytes 4325376 | tf_op jit(solution)/shard_map/reduce_sum | solution.py:31
  106.4 5.5 %fusion.18 = (f32[8,2048]{1,0:T(8,128)S(1)}, f32[8,2048,64]{2,1,0:T(8,128)}) fusion(f32[8,2048,64]{2,1,0:T(8,128)S(1)} %copy-done.1), kind=kOutput, calls=%fused_computation.48 | output fusion | flops 4194367 | bytes 8454144 | tf_op jit(solution)/shard_map/sub | solution.py:31
  111.8 6.3 %divide_convert_fusion.1 = bf16[8,2048,64]{2,1,0:T(8,128)(2,1)} fusion(f32[8,2048,64]{2,1,0:T(8,128)S(1)} %copy-done.1, f32[8,2048]{1,0:T(8,128)S(1)} %fusion.3, f32[8,2048]{1,0:T(8,128)S(1)} %get-tuple-element.25), kind=kLoop, calls=%fused_computation.6 | loop fusion | flops 3145728 | bytes 6422528 | tf_op jit(solution)/shard_map/convert.2
  118.2 16.3 %all-to-all-done.2 = bf16[64,16,2048]{2,0,1:T(8,128)(2,1)} async-done(((bf16[64,16,2048]{2,0,1:T(8,128)(2,1)}), bf16[64,16,2048]{2,0,1:T(8,128)(2,1)}, u32[]{:S(2)}, u32[]{:S(2)}) %all-to-all-start.2) | async-done | bytes 4194336 | tf_op jit(solution)/shard_map/all_to_all | solution.py:25
  134.4 10.1 %all-to-all-start.3 = ((bf16[16,64,1024]{2,1,0:T(8,128)(2,1)}), bf16[16,64,1024]{2,1,0:T(8,128)(2,1)S(1)}, u32[]{:S(2)}, u32[]{:S(2)}) async-start(bf16[16,64,1024]{2,1,0:T(8,128)(2,1)} %get-tuple-element.19), calls=%async_computation.3 | async-start | bytes 4194304 | tf_op jit(solution)/shard_map/all_to_all | solution.py:247
  144.5 1.1 slice_bitcast_fusion.4
  145.6 5.5 %divide_convert_fusion = bf16[8,2048,64]{2,1,0:T(8,128)(2,1)S(1)} fusion(f32[8,2048,64]{2,1,0:T(8,128)} %get-tuple-element.24, f32[8,2048]{1,0:T(8,128)S(1)} %get-tuple-element.23), kind=kLoop, calls=%fused_computation.4 | loop fusion | flops 2097152 | bytes 6356992 | tf_op jit(solution)/shard_map/convert.3
  151.1 2.6 convert_reduce_fusion
  153.8 4.9 %fusion.22 = f32[8,128,128]{2,1,0:T(8,128)S(1)} fusion(bf16[8,128,2048]{2,1,0:T(8,128)(2,1)} %bitcast.9.refs_2_, bf16[8,2048,128]{2,1,0:T(8,128)(2,1)S(1)} %get-tuple-element.18.refs_3_), kind=kOutput, calls=%fused_computation.52 | convolution fusion | flops 536870912 | bytes 8912896 | tf_op jit(solution)/shard_map/htf,hdt->hdf/dot_general | solution.py:258
  158.7 0.9 pad_maximum_fusion.2
  159.6 3.1 %collective-permute-start = (bf16[2,8,128,64]{3,2,1,0:T(8,128)(2,1)}, bf16[2,8,128,64]{3,2,1,0:T(8,128)(2,1)S(1)}, u32[]{:S(2)}, u32[]{:S(2)}) collective-permute-start(bf16[2,8,128,64]{3,2,1,0:T(8,128)(2,1)} %pad_maximum_fusion.2), channel_id=1, source_target_pairs={{0,1},{1,2},{2,3},{3,4},{4,5},{5,6},{6,7},{7,8},{8,9},{9,10},{10,1... | collective-permute-start | bytes 786440 | tf_op jit(solution)/shard_map/ppermute | solution.py:21
  163.4 2.1 collective-permute-start.1
  166.2 6.5 %copy.17.refs_1_ = bf16[8,2048,128]{2,1,0:T(8,128)(2,1)} copy(bf16[8,2048,128]{1,2,0:T(8,128)(2,1)} %bitcast.6) | data formatting | bytes 8388608 | tf_op jit(solution)/shard_map/transpose | solution.py:226
  172.7 6.3 %collective-permute-done = bf16[2,8,128,64]{3,2,1,0:T(8,128)(2,1)S(1)} collective-permute-done((bf16[2,8,128,64]{3,2,1,0:T(8,128)(2,1)}, bf16[2,8,128,64]{3,2,1,0:T(8,128)(2,1)S(1)}, u32[]{:S(2)}, u32[]{:S(2)}) %collective-permute-start) | collective-permute-done | bytes 262176 | tf_op jit(solution)/shard_map/ppermute | solution.py:21
  178.9 1.6 fusion.20
  180.6 3.6 %collective-permute-done.1 = bf16[1032,128]{1,0:T(8,128)(2,1)S(1)} collective-permute-done((bf16[1032,128]{1,0:T(8,128)(2,1)}, bf16[1032,128]{1,0:T(8,128)(2,1)S(1)}, u32[]{:S(2)}, u32[]{:S(2)}) %collective-permute-start.1) | collective-permute-done | bytes 264224 | tf_op jit(solution)/shard_map/ppermute | solution.py:21
  185.0 1.3 collective-permute-start.2
  186.3 2.6 fusion.21
  188.8 1.9 slice_bitcast_fusion.2
  190.7 6.1 %collective-permute-done.2 = bf16[1032,128]{1,0:T(8,128)(2,1)S(1)} collective-permute-done((bf16[1032,128]{1,0:T(8,128)(2,1)}, bf16[1032,128]{1,0:T(8,128)(2,1)S(1)}, u32[]{:S(2)}, u32[]{:S(2)}) %collective-permute-start.2) | collective-permute-done | bytes 264224 | tf_op jit(solution)/shard_map/ppermute | solution.py:21
  196.8 0.8 fusion.17
  197.6 1.3 collective-permute-start.3
  198.9 9.0 %all-to-all-start = ((bf16[16,64,1024]{2,1,0:T(8,128)(2,1)}), bf16[16,64,1024]{2,1,0:T(8,128)(2,1)}, u32[]{:S(2)}, u32[]{:S(2)}) async-start(bf16[16,64,1024]{2,1,0:T(8,128)(2,1)} %get-tuple-element.20), calls=%async_computation | async-start | bytes 4194304 | tf_op jit(solution)/shard_map/all_to_all | solution.py:247
  207.9 1.8 pad_bitcast_fusion
  209.7 1.2 divide_convert_fusion.2
  211.0 0.8 fusion.12
  211.8 1.3 collective-permute-start.4
  213.3 1.8 copy.18.refs_4_
  215.8 1.8 concatenate.26.refs_5_
  217.6 1.2 fusion.16
  218.8 18.7 %collective-permute-done.4 = bf16[1032,128]{1,0:T(8,128)(2,1)} collective-permute-done((bf16[1032,128]{1,0:T(8,128)(2,1)}, bf16[1032,128]{1,0:T(8,128)(2,1)}, u32[]{:S(2)}, u32[]{:S(2)}) %collective-permute-start.4) | collective-permute-done | bytes 264224 | tf_op jit(solution)/shard_map/ppermute | solution.py:21
  237.5 1.2 add_subtract_fusion
  239.4 0.8 sub.58.refs_8_
  240.2 1.4 broadcast_in_dim.16.refs_11_
  241.6 1.3 broadcast_in_dim.13.refs_10_
  242.9 26.0 %shard_map.64 = (bf16[2048,1024]{1,0:T(8,128)(2,1)}, f32[8,128,128]{2,1,0:T(8,128)}, f32[8,8,128]{2,1,0:T(8,128)}) custom-call(bf16[8,128,1024]{2,1,0:T(8,128)(2,1)} %bitcast.67, bf16[8,2048,128]{2,1,0:T(8,128)(2,1)} %copy.17.refs_1_, bf16[8,128,2048]{2,1,0:T(8,128)(2,1)} %bitcast.9.refs_2_, bf16[8,2048,128]{2,1,0:T(8,128)(2,1)} %copy-done.2, ...), custom_call_target="tpu_custom_call" | custom-call | tf_op jit(solution)/shard_map/pallas_call | solution.py:194
  269.0 25.8 %shard_map.65 = bf16[2048,1024]{1,0:T(8,128)(2,1)} custom-call(bf16[8,128,1024]{2,1,0:T(8,128)(2,1)} %bitcast.2.refs_0_, bf16[8,2048,128]{2,1,0:T(8,128)(2,1)} %copy.17.refs_1_, bf16[8,128,2048]{2,1,0:T(8,128)(2,1)} %bitcast.9.refs_2_, bf16[8,2048,128]{2,1,0:T(8,128)(2,1)} %copy-done.2, ...), custom_call_target="tpu_custom_call", output_to_operand_aliasing={{}: (12, {})} | custom-call | tf_op jit(solution)/shard_map/pallas_call | solution.py:194
  (34 shorter events, 5.0 us)
Async XLA Ops:
  0.0 86.1 %copy-start = (bf16[8,128,64]{1,2,0:T(8,128)(2,1)S(1)}, bf16[8,128,64]{1,2,0:T(8,128)(2,1)}, u32[]{:S(2)}) copy-start(bf16[8,128,64]{1,2,0:T(8,128)(2,1)} %param.10) | copy-start | bytes 393220
  4.8 64.3 %all-to-all-start.1 = ((bf16[64,16,2048]{2,0,1:T(8,128)(2,1)}), bf16[64,16,2048]{2,0,1:T(8,128)(2,1)}, u32[]{:S(2)}, u32[]{:S(2)}) async-start(bf16[64,16,2048]{2,0,1:T(8,128)(2,1)} %bitcast.66), calls=%async_computation.1 | async-start | bytes 8388608 | tf_op jit(solution)/shard_map/all_to_all | solution.py:25
  19.5 6.6 %copy-start.5 = (bf16[64,32768]{1,0:T(8,128)(2,1)S(1)}, bf16[64,32768]{1,0:T(8,128)(2,1)}, u32[]{:S(2)}) copy-start(bf16[64,32768]{1,0:T(8,128)(2,1)} %param.8) | copy-start | bytes 12582916
  69.0 10.8 %copy-start.8 = (bf16[8,128,64]{1,2,0:T(8,128)(2,1)S(1)}, bf16[8,128,64]{1,2,0:T(8,128)(2,1)}, u32[]{:S(2)}) copy-start(bf16[8,128,64]{1,2,0:T(8,128)(2,1)} %param.9) | copy-start | bytes 393220
  69.1 11.6 %copy-start.9 = (f32[8]{0:T(128)S(1)}, f32[8]{0:T(128)}, u32[]{:S(2)}) copy-start(f32[8]{0:T(128)} %param.11) | copy-start | bytes 100
  69.1 65.4 %all-to-all-start.2 = ((bf16[64,16,2048]{2,0,1:T(8,128)(2,1)}), bf16[64,16,2048]{2,0,1:T(8,128)(2,1)}, u32[]{:S(2)}, u32[]{:S(2)}) async-start(bf16[64,16,2048]{2,0,1:T(8,128)(2,1)} %bitcast.64), calls=%async_computation.2 | async-start | bytes 8388608 | tf_op jit(solution)/shard_map/all_to_all | solution.py:25
  99.0 7.4 %copy-start.1 = (f32[8,2048,64]{2,1,0:T(8,128)S(1)}, f32[8,2048,64]{2,1,0:T(8,128)}, u32[]{:S(2)}) copy-start(f32[8,2048,64]{2,1,0:T(8,128)} %copy.11) | copy-start | bytes 12582916
  134.4 64.5 %all-to-all-start.3 = ((bf16[16,64,1024]{2,1,0:T(8,128)(2,1)}), bf16[16,64,1024]{2,1,0:T(8,128)(2,1)S(1)}, u32[]{:S(2)}, u32[]{:S(2)}) async-start(bf16[16,64,1024]{2,1,0:T(8,128)(2,1)} %get-tuple-element.19), calls=%async_computation.3 | async-start | bytes 4194304 | tf_op jit(solution)/shard_map/all_to_all | solution.py:247
  145.6 5.5 %copy-start.3 = (bf16[8,2048,64]{2,1,0:T(8,128)(2,1)S(1)}, bf16[8,2048,64]{2,1,0:T(8,128)(2,1)}, u32[]{:S(2)}) copy-start(bf16[8,2048,64]{2,1,0:T(8,128)(2,1)} %divide_convert_fusion.1) | copy-start | bytes 6291460
  153.8 5.0 %copy-start.2 = (bf16[8,2048,128]{2,1,0:T(8,128)(2,1)}, bf16[8,2048,128]{2,1,0:T(8,128)(2,1)S(1)}, u32[]{:S(2)}) copy-start(bf16[8,2048,128]{2,1,0:T(8,128)(2,1)S(1)} %get-tuple-element.18.refs_3_) | copy-start | bytes 12582916
  159.6 19.3 %collective-permute-start = (bf16[2,8,128,64]{3,2,1,0:T(8,128)(2,1)}, bf16[2,8,128,64]{3,2,1,0:T(8,128)(2,1)S(1)}, u32[]{:S(2)}, u32[]{:S(2)}) collective-permute-start(bf16[2,8,128,64]{3,2,1,0:T(8,128)(2,1)} %pad_maximum_fusion.2), channel_id=1, source_target_pairs={{0,1},{1,2},{2,3},{3,4},{4,5},{5,6},{6,7},{7,8},{8,9},{9,10},{10,1... | collective-permute-start | bytes 786440 | tf_op jit(solution)/shard_map/ppermute | solution.py:21
  163.4 20.8 %collective-permute-start.1 = (bf16[1032,128]{1,0:T(8,128)(2,1)}, bf16[1032,128]{1,0:T(8,128)(2,1)S(1)}, u32[]{:S(2)}, u32[]{:S(2)}) collective-permute-start(bf16[1032,128]{1,0:T(8,128)(2,1)} %fusion.13), channel_id=1, source_target_pairs={{0,1},{1,2},{2,3},{3,4},{4,5},{5,6},{6,7},{7,8},{8,9},{9,10},{10,1... | collective-permute-start | bytes 792584 | tf_op jit(solution)/shard_map/ppermute | solution.py:21
  178.9 5.3 %copy-start.6 = (bf16[2,8,128,64]{3,2,1,0:T(8,128)(2,1)}, bf16[2,8,128,64]{3,2,1,0:T(8,128)(2,1)S(1)}, u32[]{:S(2)}) copy-start(bf16[2,8,128,64]{3,2,1,0:T(8,128)(2,1)S(1)} %collective-permute-done) | copy-start | bytes 786436
  185.0 11.8 %collective-permute-start.2 = (bf16[1032,128]{1,0:T(8,128)(2,1)}, bf16[1032,128]{1,0:T(8,128)(2,1)S(1)}, u32[]{:S(2)}, u32[]{:S(2)}) collective-permute-start(bf16[1032,128]{1,0:T(8,128)(2,1)} %fusion.11), channel_id=1, source_target_pairs={{0,2},{1,3},{2,4},{3,5},{4,6},{5,7},{6,8},{7,9},{8,10},{9,11},{10,... | collective-permute-start | bytes 792584 | tf_op jit(solution)/shard_map/ppermute | solution.py:21
  197.6 13.4 %collective-permute-start.3 = (bf16[1032,128]{1,0:T(8,128)(2,1)}, bf16[1032,128]{1,0:T(8,128)(2,1)S(1)}, u32[]{:S(2)}, u32[]{:S(2)}) collective-permute-start(bf16[1032,128]{1,0:T(8,128)(2,1)} %fusion.17), channel_id=1, source_target_pairs={{0,4},{1,5},{2,6},{3,7},{4,8},{5,9},{6,10},{7,11},{8,12},{9,13},{1... | collective-permute-start | bytes 792584 | tf_op jit(solution)/shard_map/ppermute | solution.py:21
  198.9 16.9 %copy-start.4 = (bf16[16,64,1024]{2,1,0:T(8,128)(2,1)}, bf16[16,64,1024]{2,1,0:T(8,128)(2,1)S(1)}, u32[]{:S(2)}) copy-start(bf16[16,64,1024]{2,1,0:T(8,128)(2,1)S(1)} %all-to-all-done.3) | copy-start | bytes 6291460
  198.9 70.1 %all-to-all-start = ((bf16[16,64,1024]{2,1,0:T(8,128)(2,1)}), bf16[16,64,1024]{2,1,0:T(8,128)(2,1)}, u32[]{:S(2)}, u32[]{:S(2)}) async-start(bf16[16,64,1024]{2,1,0:T(8,128)(2,1)} %get-tuple-element.20), calls=%async_computation | async-start | bytes 4194304 | tf_op jit(solution)/shard_map/all_to_all | solution.py:247
  211.0 2.1 copy-start.7
  211.8 25.6 %collective-permute-start.4 = (bf16[1032,128]{1,0:T(8,128)(2,1)}, bf16[1032,128]{1,0:T(8,128)(2,1)}, u32[]{:S(2)}, u32[]{:S(2)}) collective-permute-start(bf16[1032,128]{1,0:T(8,128)(2,1)} %fusion.12), channel_id=1, source_target_pairs={{0,8},{1,9},{2,10},{3,11},{4,12},{5,13},{6,14},{7,15},{16,24},{17,... | collective-permute-start | bytes 792584 | tf_op jit(solution)/shard_map/ppermute | solution.py:21

commit v11 on v10

--- a/solution.py
+++ b/solution.py
@@ -12,6 +12,7 @@
 HEADS_PER_STEP = 2
 Q_PIECES = 2
 UNROLL = 8
+RADIX = 4
 INTERPRET = False
 
 
@@ -261,8 +262,13 @@
     prior = own
     distance = 1
     while distance < shards:
-        prior = prior + passed_along(prior.astype(jnp.bfloat16), "seq", distance).astype(jnp.float32)
-        distance *= 2
+        sent = prior.astype(jnp.bfloat16)
+        total = prior
+        for j in range(1, RADIX):
+            if distance * j < shards:
+                total = total + passed_along(sent, "seq", distance * j).astype(jnp.float32)
+        prior = total
+        distance *= RADIX
     prior = prior - own
     prior_state = prior[: group * head_dim].reshape(own_state.shape)
     prior_norm = prior[group * head_dim :]

time: 296 us -> 288 us (0.973); the launches traced: 295 us -> 283 us
  waiting for transfers between devices: 91.6 us -> 77.5 us
  starting transfers between devices: 45.9 us -> 53.4 us
  matrix products: 15.2 us -> 12.1 us
    ppermute x5 -> x7, waiting for transfers between devices: 34.7 us -> 21.3 us  [passed_along(): return lax.ppermute(block, axis, route)]
    all_to_all x2, starting transfers between devices: 19.1 us -> 24.1 us  [body(): lax.all_to_all(halves[c], 'seq', split_axis=0, concat_axis=0, tiled=True)]
    ppermute x5 -> x7, starting transfers between devices: 9.03 us -> 11.6 us  [passed_along(): return lax.ppermute(block, axis, route)]
  transfers between devices with their start and end apart: 9 -> 11, of which waited for: 6 -> 6; matrix products, arithmetic and copies ran while one was open for 34% -> 34% of each run, Pallas kernels for 9% -> 9%
where the time goes in v11:
time: 288 us; the launch traced here: 283 us
  waiting for transfers between devices  77.5 us (27%)
  starting transfers between devices  53.4 us (19%)
  Pallas kernels  51.8 us (18%)
  local copies, waits for them, and re-layouts  51.1 us (18%)
  other arithmetic  36.6 us (13%)
  matrix products  12.1 us (4%)
    all_to_all x2, waiting for transfers between devices, exchange(): moved = lax.all_to_all(rows, 'seq', split_axis=1, concat_axis=0, tiled=True)  56.2 us
    pallas_call x2, Pallas kernels, attend(): pl.pallas_call(make_kernel(t_begin, span // QB), grid=(group // hb,), in_...  51.8 us
    all_to_all x2, starting transfers between devices, body(): lax.all_to_all(halves[c], 'seq', split_axis=0, concat_axis=0, tiled=True)  24.1 us
    ppermute x7, waiting for transfers between devices, passed_along(): return lax.ppermute(block, axis, route)  21.3 us
    all_to_all x2, starting transfers between devices, exchange(): moved = lax.all_to_all(rows, 'seq', split_axis=1, concat_axis=0, tiled=True)  17.7 us
    reshape x2, local copies, waits for them, and re-layouts, body(): queries.reshape(feature_rows, shards, Q_PIECES, length // Q_PIECES)  14.4 us
    another operation x3, other arithmetic  13.1 us
    ppermute x7, starting transfers between devices, passed_along(): return lax.ppermute(block, axis, route)  11.6 us
  transfers between devices with their start and end apart: 11, of which 6 were waited for; matrix products, arithmetic and copies ran while one was open for 34% of the time, Pallas kernels for 9%

profile of v11, /device:TPU:116, one launch (start us, length us, event | category | flops | bytes accessed | tf_op | source)
XLA Modules:
  0.0 282.8 jit_solution(14637562165378789712)
XLA Ops:
  0.0 4.8 %copy.27 = bf16[8,16,8,2048]{3,2,0,1:T(8,128)(2,1)} copy(bf16[8,16,8,2048]{3,2,1,0:T(8,128)(2,1)} %bitcast.66) | data formatting | bytes 8388608 | tf_op jit(solution)/shard_map/reshape | solution.py:245
  4.8 6.9 %all-to-all-start.1 = ((bf16[64,16,2048]{2,0,1:T(8,128)(2,1)}), bf16[64,16,2048]{2,0,1:T(8,128)(2,1)}, u32[]{:S(2)}, u32[]{:S(2)}) async-start(bf16[64,16,2048]{2,0,1:T(8,128)(2,1)} %bitcast.61), calls=%async_computation.1 | async-start | bytes 8388608 | tf_op jit(solution)/shard_map/all_to_all | solution.py:26
  11.7 7.8 %reshape.51 = bf16[64,16,2,1024]{3,2,1,0:T(2,128)(2,1)} reshape(bf16[64,32768]{1,0:T(8,128)(2,1)} %param.6) | data formatting | bytes 8388608 | tf_op jit(solution)/shard_map/reshape | solution.py:243
  19.5 6.6 %copy.28 = bf16[64,16,2,1024]{3,0,1,2:T(8,128)(2,1)} copy(bf16[64,16,2,1024]{3,2,1,0:T(2,128)(2,1)} %reshape.51) | data formatting | bytes 8388608 | tf_op jit(solution)/shard_map/reshape | solution.py:243
  26.1 2.3 copy.26
  28.4 40.6 %all-to-all-done.1 = bf16[64,16,2048]{2,0,1:T(8,128)(2,1)} async-done(((bf16[64,16,2048]{2,0,1:T(8,128)(2,1)}), bf16[64,16,2048]{2,0,1:T(8,128)(2,1)}, u32[]{:S(2)}, u32[]{:S(2)}) %all-to-all-start.1) | async-done | bytes 4194336 | tf_op jit(solution)/shard_map/all_to_all | solution.py:26
  69.1 10.8 %all-to-all-start.2 = ((bf16[64,16,2048]{2,0,1:T(8,128)(2,1)}), bf16[64,16,2048]{2,0,1:T(8,128)(2,1)}, u32[]{:S(2)}, u32[]{:S(2)}) async-start(bf16[64,16,2048]{2,0,1:T(8,128)(2,1)} %bitcast.59), calls=%async_computation.2 | async-start | bytes 8388608 | tf_op jit(solution)/shard_map/all_to_all | solution.py:26
  80.5 0.7 maximum_bitcast_fusion.refs_7_
  81.8 4.9 %slice_bitcast_fusion = (bf16[16,64,1024]{2,1,0:T(8,128)(2,1)}, bf16[16,64,1024]{2,1,0:T(8,128)(2,1)}) fusion(bf16[2,16,64,1024]{3,2,1,0:T(8,128)(2,1)} %bitcast.60), kind=kLoop, calls=%fused_computation.15 | loop fusion | bytes 8388608 | tf_op jit(solution)/shard_map/squeeze | solution.py:248
  86.7 4.9 %fusion.17 = (f32[8,2048]{1,0:T(8,128)S(1)}, f32[8,2048,64]{1,2,0:T(8,128)}) fusion(bf16[8,128,64]{1,2,0:T(8,128)(2,1)S(1)} %copy-done, bf16[8,128,2048]{2,1,0:T(8,128)(2,1)} %bitcast.5), kind=kOutput, calls=%fused_computation.45 | convolution fusion | flops 269467648 | bytes 8585216 | tf_op jit(solution)/shard_map/hdt,hdf->htf/dot_general | solution.py:31
  91.6 6.9 %copy.11 = f32[8,2048,64]{2,1,0:T(8,128)} copy(f32[8,2048,64]{1,2,0:T(8,128)} %get-tuple-element.26) | data formatting | bytes 8388608 | tf_op jit(solution)/shard_map/hdt,hdf->htf/dot_general | solution.py:31
  98.5 1.1 slice_bitcast_fusion.5
  99.6 7.4 %fusion.3 = f32[8,2048]{1,0:T(8,128)S(1)} fusion(f32[8,2048,64]{2,1,0:T(8,128)} %copy.11, f32[8,2048]{1,0:T(8,128)S(1)} %get-tuple-element.25), kind=kLoop, calls=%fused_computation.8 | loop fusion | flops 2080768 | bytes 4325376 | tf_op jit(solution)/shard_map/reduce_sum | solution.py:32
  106.9 5.5 %fusion.16 = (f32[8,2048]{1,0:T(8,128)S(1)}, f32[8,2048,64]{2,1,0:T(8,128)}) fusion(f32[8,2048,64]{2,1,0:T(8,128)S(1)} %copy-done.1), kind=kOutput, calls=%fused_computation.44 | output fusion | flops 4194367 | bytes 8454144 | tf_op jit(solution)/shard_map/sub | solution.py:32
  112.4 6.4 %divide_convert_fusion.1 = bf16[8,2048,64]{2,1,0:T(8,128)(2,1)} fusion(f32[8,2048,64]{2,1,0:T(8,128)S(1)} %copy-done.1, f32[8,2048]{1,0:T(8,128)S(1)} %fusion.3, f32[8,2048]{1,0:T(8,128)S(1)} %get-tuple-element.25), kind=kLoop, calls=%fused_computation.6 | loop fusion | flops 3145728 | bytes 6422528 | tf_op jit(solution)/shard_map/convert.2
  118.8 15.6 %all-to-all-done.2 = bf16[64,16,2048]{2,0,1:T(8,128)(2,1)} async-done(((bf16[64,16,2048]{2,0,1:T(8,128)(2,1)}), bf16[64,16,2048]{2,0,1:T(8,128)(2,1)}, u32[]{:S(2)}, u32[]{:S(2)}) %all-to-all-start.2) | async-done | bytes 4194336 | tf_op jit(solution)/shard_map/all_to_all | solution.py:26
  134.4 10.1 %all-to-all-start.3 = ((bf16[16,64,1024]{2,1,0:T(8,128)(2,1)}), bf16[16,64,1024]{2,1,0:T(8,128)(2,1)S(1)}, u32[]{:S(2)}, u32[]{:S(2)}) async-start(bf16[16,64,1024]{2,1,0:T(8,128)(2,1)} %get-tuple-element.19), calls=%async_computation.3 | async-start | bytes 4194304 | tf_op jit(solution)/shard_map/all_to_all | solution.py:248
  144.5 1.1 slice_bitcast_fusion.4
  145.6 0.9 pad_maximum_fusion.2
  146.5 3.1 %collective-permute-start = (bf16[2,8,128,64]{3,2,1,0:T(8,128)(2,1)}, bf16[2,8,128,64]{3,2,1,0:T(8,128)(2,1)S(1)}, u32[]{:S(2)}, u32[]{:S(2)}) collective-permute-start(bf16[2,8,128,64]{3,2,1,0:T(8,128)(2,1)} %pad_maximum_fusion.2), channel_id=1, source_target_pairs={{0,1},{1,2},{2,3},{3,4},{4,5},{5,6},{6,7},{7,8},{8,9},{9,10},{10,1... | collective-permute-start | bytes 786440 | tf_op jit(solution)/shard_map/ppermute | solution.py:22
  149.6 5.5 %divide_convert_fusion = bf16[8,2048,64]{2,1,0:T(8,128)(2,1)S(1)} fusion(f32[8,2048,64]{2,1,0:T(8,128)} %get-tuple-element.24, f32[8,2048]{1,0:T(8,128)S(1)} %get-tuple-element.23), kind=kLoop, calls=%fused_computation.4 | loop fusion | flops 2097152 | bytes 6356992 | tf_op jit(solution)/shard_map/convert.3
  155.1 2.6 convert_reduce_fusion
  157.8 4.9 %fusion.20 = f32[8,128,128]{2,1,0:T(8,128)S(1)} fusion(bf16[8,128,2048]{2,1,0:T(8,128)(2,1)} %bitcast.9.refs_2_, bf16[8,2048,128]{2,1,0:T(8,128)(2,1)S(1)} %get-tuple-element.18.refs_3_), kind=kOutput, calls=%fused_computation.48 | convolution fusion | flops 536870912 | bytes 8912896 | tf_op jit(solution)/shard_map/htf,hdt->hdf/dot_general | solution.py:259
  163.4 1.9 collective-permute-start.1
  165.4 1.3 collective-permute-start.2
  166.7 1.3 collective-permute-start.3
  168.0 6.5 %copy.17.refs_1_ = bf16[8,2048,128]{2,1,0:T(8,128)(2,1)} copy(bf16[8,2048,128]{1,2,0:T(8,128)(2,1)} %bitcast.6) | data formatting | bytes 8388608 | tf_op jit(solution)/shard_map/transpose | solution.py:227
  174.5 4.4 %collective-permute-done = bf16[2,8,128,64]{3,2,1,0:T(8,128)(2,1)S(1)} collective-permute-done((bf16[2,8,128,64]{3,2,1,0:T(8,128)(2,1)}, bf16[2,8,128,64]{3,2,1,0:T(8,128)(2,1)S(1)}, u32[]{:S(2)}, u32[]{:S(2)}) %collective-permute-start) | collective-permute-done | bytes 262176 | tf_op jit(solution)/shard_map/ppermute | solution.py:22
  178.9 1.0 fusion.18
  180.0 1.0 fusion.19
  181.0 0.8 slice_bitcast_fusion.2
  181.8 14.0 %all-to-all-start = ((bf16[16,64,1024]{2,1,0:T(8,128)(2,1)}), bf16[16,64,1024]{2,1,0:T(8,128)(2,1)}, u32[]{:S(2)}, u32[]{:S(2)}) async-start(bf16[16,64,1024]{2,1,0:T(8,128)(2,1)} %get-tuple-element.20), calls=%async_computation | async-start | bytes 4194304 | tf_op jit(solution)/shard_map/all_to_all | solution.py:248
  195.9 1.8 pad_bitcast_fusion
  197.7 1.2 divide_convert_fusion.2
  199.0 1.9 fusion.13
  200.9 1.4 collective-permute-start.4
  202.3 1.3 collective-permute-start.5
  203.6 1.3 collective-permute-start.6
  205.1 1.8 copy.18.refs_4_
  207.6 1.8 concatenate.26.refs_5_
  209.6 10.5 %collective-permute-done.4 = bf16[1032,128]{1,0:T(8,128)(2,1)} collective-permute-done((bf16[1032,128]{1,0:T(8,128)(2,1)}, bf16[1032,128]{1,0:T(8,128)(2,1)}, u32[]{:S(2)}, u32[]{:S(2)}) %collective-permute-start.4) | collective-permute-done | bytes 264224 | tf_op jit(solution)/shard_map/ppermute | solution.py:22
  220.1 1.8 collective-permute-done.5
  221.9 4.5 %collective-permute-done.6 = bf16[1032,128]{1,0:T(8,128)(2,1)} collective-permute-done((bf16[1032,128]{1,0:T(8,128)(2,1)}, bf16[1032,128]{1,0:T(8,128)(2,1)}, u32[]{:S(2)}, u32[]{:S(2)}) %collective-permute-start.6) | collective-permute-done | bytes 264224 | tf_op jit(solution)/shard_map/ppermute | solution.py:22
  226.4 1.6 add_subtract_fusion
  228.7 0.8 sub.58.refs_8_
  229.5 0.8 broadcast_in_dim.16.refs_11_
  231.0 26.0 %shard_map.64 = (bf16[2048,1024]{1,0:T(8,128)(2,1)}, f32[8,128,128]{2,1,0:T(8,128)}, f32[8,8,128]{2,1,0:T(8,128)}) custom-call(bf16[8,128,1024]{2,1,0:T(8,128)(2,1)} %bitcast.65, bf16[8,2048,128]{2,1,0:T(8,128)(2,1)} %copy.17.refs_1_, bf16[8,128,2048]{2,1,0:T(8,128)(2,1)} %bitcast.9.refs_2_, bf16[8,2048,128]{2,1,0:T(8,128)(2,1)} %copy-done.2, ...), custom_call_target="tpu_custom_call" | custom-call | tf_op jit(solution)/shard_map/pallas_call | solution.py:195
  257.0 25.8 %shard_map.65 = bf16[2048,1024]{1,0:T(8,128)(2,1)} custom-call(bf16[8,128,1024]{2,1,0:T(8,128)(2,1)} %bitcast.2.refs_0_, bf16[8,2048,128]{2,1,0:T(8,128)(2,1)} %copy.17.refs_1_, bf16[8,128,2048]{2,1,0:T(8,128)(2,1)} %bitcast.9.refs_2_, bf16[8,2048,128]{2,1,0:T(8,128)(2,1)} %copy-done.2, ...), custom_call_target="tpu_custom_call", output_to_operand_aliasing={{}: (12, {})} | custom-call | tf_op jit(solution)/shard_map/pallas_call | solution.py:195
  (38 shorter events, 4.3 us)
Async XLA Ops:
  0.0 86.7 %copy-start = (bf16[8,128,64]{1,2,0:T(8,128)(2,1)S(1)}, bf16[8,128,64]{1,2,0:T(8,128)(2,1)}, u32[]{:S(2)}) copy-start(bf16[8,128,64]{1,2,0:T(8,128)(2,1)} %param.10) | copy-start | bytes 393220
  4.8 64.3 %all-to-all-start.1 = ((bf16[64,16,2048]{2,0,1:T(8,128)(2,1)}), bf16[64,16,2048]{2,0,1:T(8,128)(2,1)}, u32[]{:S(2)}, u32[]{:S(2)}) async-start(bf16[64,16,2048]{2,0,1:T(8,128)(2,1)} %bitcast.61), calls=%async_computation.1 | async-start | bytes 8388608 | tf_op jit(solution)/shard_map/all_to_all | solution.py:26
  19.5 6.6 %copy-start.5 = (bf16[64,32768]{1,0:T(8,128)(2,1)S(1)}, bf16[64,32768]{1,0:T(8,128)(2,1)}, u32[]{:S(2)}) copy-start(bf16[64,32768]{1,0:T(8,128)(2,1)} %param.8) | copy-start | bytes 12582916
  69.1 10.8 %copy-start.7 = (bf16[8,128,64]{1,2,0:T(8,128)(2,1)S(1)}, bf16[8,128,64]{1,2,0:T(8,128)(2,1)}, u32[]{:S(2)}) copy-start(bf16[8,128,64]{1,2,0:T(8,128)(2,1)} %param.9) | copy-start | bytes 393220
  69.1 12.2 %copy-start.10 = (f32[8]{0:T(128)S(1)}, f32[8]{0:T(128)}, u32[]{:S(2)}) copy-start(f32[8]{0:T(128)} %param.11) | copy-start | bytes 100
  69.1 65.4 %all-to-all-start.2 = ((bf16[64,16,2048]{2,0,1:T(8,128)(2,1)}), bf16[64,16,2048]{2,0,1:T(8,128)(2,1)}, u32[]{:S(2)}, u32[]{:S(2)}) async-start(bf16[64,16,2048]{2,0,1:T(8,128)(2,1)} %bitcast.59), calls=%async_computation.2 | async-start | bytes 8388608 | tf_op jit(solution)/shard_map/all_to_all | solution.py:26
  99.6 7.4 %copy-start.1 = (f32[8,2048,64]{2,1,0:T(8,128)S(1)}, f32[8,2048,64]{2,1,0:T(8,128)}, u32[]{:S(2)}) copy-start(f32[8,2048,64]{2,1,0:T(8,128)} %copy.11) | copy-start | bytes 12582916
  134.4 47.4 %all-to-all-start.3 = ((bf16[16,64,1024]{2,1,0:T(8,128)(2,1)}), bf16[16,64,1024]{2,1,0:T(8,128)(2,1)S(1)}, u32[]{:S(2)}, u32[]{:S(2)}) async-start(bf16[16,64,1024]{2,1,0:T(8,128)(2,1)} %get-tuple-element.19), calls=%async_computation.3 | async-start | bytes 4194304 | tf_op jit(solution)/shard_map/all_to_all | solution.py:248
  146.5 32.4 %collective-permute-start = (bf16[2,8,128,64]{3,2,1,0:T(8,128)(2,1)}, bf16[2,8,128,64]{3,2,1,0:T(8,128)(2,1)S(1)}, u32[]{:S(2)}, u32[]{:S(2)}) collective-permute-start(bf16[2,8,128,64]{3,2,1,0:T(8,128)(2,1)} %pad_maximum_fusion.2), channel_id=1, source_target_pairs={{0,1},{1,2},{2,3},{3,4},{4,5},{5,6},{6,7},{7,8},{8,9},{9,10},{10,1... | collective-permute-start | bytes 786440 | tf_op jit(solution)/shard_map/ppermute | solution.py:22
  149.6 5.5 %copy-start.3 = (bf16[8,2048,64]{2,1,0:T(8,128)(2,1)S(1)}, bf16[8,2048,64]{2,1,0:T(8,128)(2,1)}, u32[]{:S(2)}) copy-start(bf16[8,2048,64]{2,1,0:T(8,128)(2,1)} %divide_convert_fusion.1) | copy-start | bytes 6291460
  157.7 5.0 %copy-start.2 = (bf16[8,2048,128]{2,1,0:T(8,128)(2,1)}, bf16[8,2048,128]{2,1,0:T(8,128)(2,1)S(1)}, u32[]{:S(2)}) copy-start(bf16[8,2048,128]{2,1,0:T(8,128)(2,1)S(1)} %get-tuple-element.18.refs_3_) | copy-start | bytes 12582916
  163.4 35.5 %collective-permute-start.1 = (bf16[1032,128]{1,0:T(8,128)(2,1)}, bf16[1032,128]{1,0:T(8,128)(2,1)S(1)}, u32[]{:S(2)}, u32[]{:S(2)}) collective-permute-start(bf16[1032,128]{1,0:T(8,128)(2,1)} %fusion.11), channel_id=1, source_target_pairs={{0,1},{1,2},{2,3},{3,4},{4,5},{5,6},{6,7},{7,8},{8,9},{9,10},{10,1... | collective-permute-start | bytes 792584 | tf_op jit(solution)/shard_map/ppermute | solution.py:22
  165.4 33.6 %collective-permute-start.2 = (bf16[1032,128]{1,0:T(8,128)(2,1)}, bf16[1032,128]{1,0:T(8,128)(2,1)}, u32[]{:S(2)}, u32[]{:S(2)}) collective-permute-start(bf16[1032,128]{1,0:T(8,128)(2,1)} %fusion.11), channel_id=1, source_target_pairs={{0,2},{1,3},{2,4},{3,5},{4,6},{5,7},{6,8},{7,9},{8,10},{9,11},{10,... | collective-permute-start | bytes 792584 | tf_op jit(solution)/shard_map/ppermute | solution.py:22
  166.7 32.3 %collective-permute-start.3 = (bf16[1032,128]{1,0:T(8,128)(2,1)}, bf16[1032,128]{1,0:T(8,128)(2,1)}, u32[]{:S(2)}, u32[]{:S(2)}) collective-permute-start(bf16[1032,128]{1,0:T(8,128)(2,1)} %fusion.11), channel_id=1, source_target_pairs={{0,3},{1,4},{2,5},{3,6},{4,7},{5,8},{6,9},{7,10},{8,11},{9,12},{10... | collective-permute-start | bytes 792584 | tf_op jit(solution)/shard_map/ppermute | solution.py:22
  181.8 25.7 %copy-start.4 = (bf16[16,64,1024]{2,1,0:T(8,128)(2,1)}, bf16[16,64,1024]{2,1,0:T(8,128)(2,1)S(1)}, u32[]{:S(2)}) copy-start(bf16[16,64,1024]{2,1,0:T(8,128)(2,1)S(1)} %all-to-all-done.3) | copy-start | bytes 6291460
  181.8 75.2 %all-to-all-start = ((bf16[16,64,1024]{2,1,0:T(8,128)(2,1)}), bf16[16,64,1024]{2,1,0:T(8,128)(2,1)}, u32[]{:S(2)}, u32[]{:S(2)}) async-start(bf16[16,64,1024]{2,1,0:T(8,128)(2,1)} %get-tuple-element.20), calls=%async_computation | async-start | bytes 4194304 | tf_op jit(solution)/shard_map/all_to_all | solution.py:248
  198.9 6.0 %copy-start.6 = (bf16[1032,128]{1,0:T(8,128)(2,1)}, bf16[1032,128]{1,0:T(8,128)(2,1)S(1)}, u32[]{:S(2)}) copy-start(bf16[1032,128]{1,0:T(8,128)(2,1)S(1)} %collective-permute-done.1) | copy-start | bytes 792580
  200.9 28.6 %copy-start.8 = (f32[256]{0:T(256)S(1)}, f32[256]{0:T(256)}, u32[]{:S(2)}) copy-start(f32[256]{0:T(256)} %and_select_fusion) | copy-start | bytes 3076
  200.9 29.4 %copy-start.9 = (f32[8]{0:T(128)S(1)}, f32[8]{0:T(128)}, u32[]{:S(2)}) copy-start(f32[8]{0:T(128)} %add_divide_fusion) | copy-start | bytes 100
  200.9 19.2 %collective-permute-start.4 = (bf16[1032,128]{1,0:T(8,128)(2,1)}, bf16[1032,128]{1,0:T(8,128)(2,1)}, u32[]{:S(2)}, u32[]{:S(2)}) collective-permute-start(bf16[1032,128]{1,0:T(8,128)(2,1)} %fusion.13), channel_id=1, source_target_pairs={{0,4},{1,5},{2,6},{3,7},{4,8},{5,9},{6,10},{7,11},{8,12},{9,13},{1... | collective-permute-start | bytes 792584 | tf_op jit(solution)/shard_map/ppermute | solution.py:22
  202.3 19.6 %collective-permute-start.5 = (bf16[1032,128]{1,0:T(8,128)(2,1)}, bf16[1032,128]{1,0:T(8,128)(2,1)}, u32[]{:S(2)}, u32[]{:S(2)}) collective-permute-start(bf16[1032,128]{1,0:T(8,128)(2,1)} %fusion.13), channel_id=1, source_target_pairs={{0,8},{1,9},{2,10},{3,11},{4,12},{5,13},{6,14},{7,15},{16,24},{17,... | collective-permute-start | bytes 792584 | tf_op jit(solution)/shard_map/ppermute | solution.py:22
  203.6 22.8 %collective-permute-start.6 = (bf16[1032,128]{1,0:T(8,128)(2,1)}, bf16[1032,128]{1,0:T(8,128)(2,1)}, u32[]{:S(2)}, u32[]{:S(2)}) collective-permute-start(bf16[1032,128]{1,0:T(8,128)(2,1)} %fusion.13), channel_id=1, source_target_pairs={{0,12},{1,13},{2,14},{3,15},{16,28},{17,29},{18,30},{19,31},{32,44... | collective-permute-start | bytes 792584 | tf_op jit(solution)/shard_map/ppermute | solution.py:22

commit v12 on v11

--- a/solution.py
+++ b/solution.py
@@ -248,8 +248,9 @@
         lax.all_to_all(halves[c], "seq", split_axis=0, concat_axis=0, tiled=True).reshape(
             group, head_dim, -1
         )
-        for c in range(Q_PIECES)
+        for c in range(Q_PIECES - 1)
     ]
+    late_q = halves[Q_PIECES - 1]
 
     earlier = place > 0
     tails = jnp.stack([k[:, :, length - WIN :], v[:, :, length - WIN :]])
@@ -268,8 +269,15 @@
             if distance * j < shards:
                 total = total + passed_along(sent, "seq", distance * j).astype(jnp.float32)
         prior = total
+        if distance == 1:
+            late_q, prior = lax.optimization_barrier((late_q, prior))
         distance *= RADIX
     prior = prior - own
+    q_parts.append(
+        lax.all_to_all(late_q, "seq", split_axis=0, concat_axis=0, tiled=True).reshape(
+            group, head_dim, -1
+        )
+    )
     prior_state = prior[: group * head_dim].reshape(own_state.shape)
     prior_norm = prior[group * head_dim :]
     gate = jax.nn.sigmoid(mix)

time: 288 us -> 297 us (1.031)
  waiting for transfers between devices: 77.5 us -> 90.8 us
    all_to_all x2 -> x1, starting transfers between devices: 24.1 us -> 10.1 us  [body(): lax.all_to_all(halves[c], 'seq', split_axis=0, concat_axis=0, tiled=True)]
    ppermute x7, waiting for transfers between devices: 21.3 us -> 34 us  [passed_along(): return lax.ppermute(block, axis, route)]
    all_to_all x0 -> x1, starting transfers between devices: none -> 11.2 us  [body(): lax.all_to_all(late_q, 'seq', split_axis=0, concat_axis=0, tiled=True)]
  transfers between devices with their start and end apart: 11 -> 11, of which waited for: 6 -> 7; matrix products, arithmetic and copies ran while one was open for 34% -> 33% of each run, Pallas kernels for 9% -> 9%
where the time goes in v12:
time: 297 us; the launch traced here: 294 us
  waiting for transfers between devices  90.8 us (31%)
  Pallas kernels  51.8 us (17%)
  starting transfers between devices  50.7 us (17%)
  local copies, waits for them, and re-layouts  50.1 us (17%)
  other arithmetic  36.3 us (12%)
  matrix products  14.3 us (5%)
    all_to_all x2, waiting for transfers between devices, exchange(): moved = lax.all_to_all(rows, 'seq', split_axis=1, concat_axis=0, tiled=True)  56.7 us
    pallas_call x2, Pallas kernels, attend(): pl.pallas_call(make_kernel(t_begin, span // QB), grid=(group // hb,), in_...  51.8 us
    ppermute x7, waiting for transfers between devices, passed_along(): return lax.ppermute(block, axis, route)  34 us
    all_to_all x2, starting transfers between devices, exchange(): moved = lax.all_to_all(rows, 'seq', split_axis=1, concat_axis=0, tiled=True)  17.7 us
    reshape x2, local copies, waits for them, and re-layouts, body(): queries.reshape(feature_rows, shards, Q_PIECES, length // Q_PIECES)  14.4 us
    another operation x3, other arithmetic  13.1 us
    ppermute x7, starting transfers between devices, passed_along(): return lax.ppermute(block, axis, route)  11.6 us
    all_to_all x1, starting transfers between devices, body(): lax.all_to_all(late_q, 'seq', split_axis=0, concat_axis=0, tiled=True)  11.2 us
  transfers between devices with their start and end apart: 11, of which 7 were waited for; matrix products, arithmetic and copies ran while one was open for 33% of the time, Pallas kernels for 9%

profile of v12, /device:TPU:116, one launch (start us, length us, event | category | flops | bytes accessed | tf_op | source)
XLA Modules:
  0.0 294.3 jit_solution(15694432549331204093)
XLA Ops:
  0.0 4.8 %copy.26 = bf16[8,16,8,2048]{3,2,0,1:T(8,128)(2,1)} copy(bf16[8,16,8,2048]{3,2,1,0:T(8,128)(2,1)} %bitcast.66) | data formatting | bytes 8388608 | tf_op jit(solution)/shard_map/reshape | solution.py:245
  4.8 6.9 %all-to-all-start.1 = ((bf16[64,16,2048]{2,0,1:T(8,128)(2,1)}), bf16[64,16,2048]{2,0,1:T(8,128)(2,1)}, u32[]{:S(2)}, u32[]{:S(2)}) async-start(bf16[64,16,2048]{2,0,1:T(8,128)(2,1)} %bitcast.61), calls=%async_computation.1 | async-start | bytes 8388608 | tf_op jit(solution)/shard_map/all_to_all | solution.py:26
  11.7 7.8 %reshape.51 = bf16[64,16,2,1024]{3,2,1,0:T(2,128)(2,1)} reshape(bf16[64,32768]{1,0:T(8,128)(2,1)} %param.6) | data formatting | bytes 8388608 | tf_op jit(solution)/shard_map/reshape | solution.py:243
  19.5 6.6 %copy.28 = bf16[64,16,2,1024]{3,0,1,2:T(8,128)(2,1)} copy(bf16[64,16,2,1024]{3,2,1,0:T(2,128)(2,1)} %reshape.51) | data formatting | bytes 8388608 | tf_op jit(solution)/shard_map/reshape | solution.py:243
  26.1 2.3 copy.27
  28.4 40.6 %all-to-all-done.1 = bf16[64,16,2048]{2,0,1:T(8,128)(2,1)} async-done(((bf16[64,16,2048]{2,0,1:T(8,128)(2,1)}), bf16[64,16,2048]{2,0,1:T(8,128)(2,1)}, u32[]{:S(2)}, u32[]{:S(2)}) %all-to-all-start.1) | async-done | bytes 4194336 | tf_op jit(solution)/shard_map/all_to_all | solution.py:26
  69.1 10.8 %all-to-all-start = ((bf16[64,16,2048]{2,0,1:T(8,128)(2,1)}), bf16[64,16,2048]{2,0,1:T(8,128)(2,1)}, u32[]{:S(2)}, u32[]{:S(2)}) async-start(bf16[64,16,2048]{2,0,1:T(8,128)(2,1)} %bitcast.59), calls=%async_computation | async-start | bytes 8388608 | tf_op jit(solution)/shard_map/all_to_all | solution.py:26
  81.2 4.9 %slice_bitcast_fusion = (bf16[16,64,1024]{2,1,0:T(8,128)(2,1)}, bf16[16,64,1024]{2,1,0:T(8,128)(2,1)}) fusion(bf16[2,16,64,1024]{3,2,1,0:T(8,128)(2,1)} %bitcast.60), kind=kLoop, calls=%fused_computation.15 | loop fusion | bytes 8388608 | tf_op jit(solution)/shard_map/squeeze | solution.py:248
  86.2 4.9 %fusion.16 = (f32[8,2048]{1,0:T(8,128)S(1)}, f32[8,2048,64]{1,2,0:T(8,128)}) fusion(bf16[8,128,64]{1,2,0:T(8,128)(2,1)S(1)} %copy-done, bf16[8,128,2048]{2,1,0:T(8,128)(2,1)} %bitcast.7), kind=kOutput, calls=%fused_computation.44 | convolution fusion | flops 269467648 | bytes 8585216 | tf_op jit(solution)/shard_map/hdt,hdf->htf/dot_general | solution.py:31
  91.0 6.9 %copy.11 = f32[8,2048,64]{2,1,0:T(8,128)} copy(f32[8,2048,64]{1,2,0:T(8,128)} %get-tuple-element.30) | data formatting | bytes 8388608 | tf_op jit(solution)/shard_map/hdt,hdf->htf/dot_general | solution.py:31
  97.9 1.1 slice_bitcast_fusion.5
  99.0 7.4 %fusion.3 = f32[8,2048]{1,0:T(8,128)S(1)} fusion(f32[8,2048,64]{2,1,0:T(8,128)} %copy.11, f32[8,2048]{1,0:T(8,128)S(1)} %get-tuple-element.29), kind=kLoop, calls=%fused_computation.8 | loop fusion | flops 2080768 | bytes 4325376 | tf_op jit(solution)/shard_map/reduce_sum | solution.py:32
  106.4 5.5 %fusion.15 = (f32[8,2048]{1,0:T(8,128)S(1)}, f32[8,2048,64]{2,1,0:T(8,128)}) fusion(f32[8,2048,64]{2,1,0:T(8,128)S(1)} %copy-done.1), kind=kOutput, calls=%fused_computation.43 | output fusion | flops 4194367 | bytes 8454144 | tf_op jit(solution)/shard_map/sub | solution.py:32
  111.9 6.4 %divide_convert_fusion.1 = bf16[8,2048,64]{2,1,0:T(8,128)(2,1)} fusion(f32[8,2048,64]{2,1,0:T(8,128)S(1)} %copy-done.1, f32[8,2048]{1,0:T(8,128)S(1)} %fusion.3, f32[8,2048]{1,0:T(8,128)S(1)} %get-tuple-element.29), kind=kLoop, calls=%fused_computation.6 | loop fusion | flops 3145728 | bytes 6422528 | tf_op jit(solution)/shard_map/convert.2
  118.3 16.1 %all-to-all-done = bf16[64,16,2048]{2,0,1:T(8,128)(2,1)} async-done(((bf16[64,16,2048]{2,0,1:T(8,128)(2,1)}), bf16[64,16,2048]{2,0,1:T(8,128)(2,1)}, u32[]{:S(2)}, u32[]{:S(2)}) %all-to-all-start) | async-done | bytes 4194336 | tf_op jit(solution)/shard_map/all_to_all | solution.py:26
  134.4 10.1 %all-to-all-start.3 = ((bf16[16,64,1024]{2,1,0:T(8,128)(2,1)}), bf16[16,64,1024]{2,1,0:T(8,128)(2,1)S(1)}, u32[]{:S(2)}, u32[]{:S(2)}) async-start(bf16[16,64,1024]{2,1,0:T(8,128)(2,1)} %get-tuple-element.23), calls=%async_computation.3 | async-start | bytes 4194304 | tf_op jit(solution)/shard_map/all_to_all | solution.py:248
  144.5 1.1 slice_bitcast_fusion.4
  145.6 0.9 pad_maximum_fusion.2
  146.5 3.1 %collective-permute-start.3 = (bf16[2,8,128,64]{3,2,1,0:T(8,128)(2,1)}, bf16[2,8,128,64]{3,2,1,0:T(8,128)(2,1)S(1)}, u32[]{:S(2)}, u32[]{:S(2)}) collective-permute-start(bf16[2,8,128,64]{3,2,1,0:T(8,128)(2,1)} %pad_maximum_fusion.2), channel_id=1, source_target_pairs={{0,1},{1,2},{2,3},{3,4},{4,5},{5,6},{6,7},{7,8},{8,9},{9,10},{10,1... | collective-permute-start | bytes 786440 | tf_op jit(solution)/shard_map/ppermute | solution.py:22
  149.6 5.5 %divide_convert_fusion = bf16[8,2048,64]{2,1,0:T(8,128)(2,1)S(1)} fusion(f32[8,2048,64]{2,1,0:T(8,128)} %get-tuple-element.28, f32[8,2048]{1,0:T(8,128)S(1)} %get-tuple-element.27), kind=kLoop, calls=%fused_computation.4 | loop fusion | flops 2097152 | bytes 6356992 | tf_op jit(solution)/shard_map/convert.3
  155.1 2.6 convert_reduce_fusion
  157.8 4.9 %fusion.19 = f32[8,128,128]{2,1,0:T(8,128)S(1)} fusion(bf16[8,128,2048]{2,1,0:T(8,128)(2,1)} %bitcast.4.refs_2_, bf16[8,2048,128]{2,1,0:T(8,128)(2,1)S(1)} %get-tuple-element.22.refs_3_), kind=kOutput, calls=%fused_computation.47 | convolution fusion | flops 536870912 | bytes 8912896 | tf_op jit(solution)/shard_map/htf,hdt->hdf/dot_general | solution.py:260
  163.5 2.1 collective-permute-start
  165.6 1.3 collective-permute-start.1
  166.9 1.3 collective-permute-start.2
  168.8 6.5 %copy.17.refs_1_ = bf16[8,2048,128]{2,1,0:T(8,128)(2,1)} copy(bf16[8,2048,128]{1,2,0:T(8,128)(2,1)} %bitcast.12) | data formatting | bytes 8388608 | tf_op jit(solution)/shard_map/transpose | solution.py:227
  175.3 3.6 %collective-permute-done.3 = bf16[2,8,128,64]{3,2,1,0:T(8,128)(2,1)S(1)} collective-permute-done((bf16[2,8,128,64]{3,2,1,0:T(8,128)(2,1)}, bf16[2,8,128,64]{3,2,1,0:T(8,128)(2,1)S(1)}, u32[]{:S(2)}, u32[]{:S(2)}) %collective-permute-start.3) | collective-permute-done | bytes 262176 | tf_op jit(solution)/shard_map/ppermute | solution.py:22
  178.9 0.8 slice_bitcast_fusion.2
  179.7 10.2 %collective-permute-done = bf16[1032,128]{1,0:T(8,128)(2,1)} collective-permute-done((bf16[1032,128]{1,0:T(8,128)(2,1)}, bf16[1032,128]{1,0:T(8,128)(2,1)}, u32[]{:S(2)}, u32[]{:S(2)}) %collective-permute-start) | collective-permute-done | bytes 264224 | tf_op jit(solution)/shard_map/ppermute | solution.py:22
  190.0 1.2 convert_add_fusion
  191.2 11.2 %all-to-all-start.2 = ((bf16[16,64,1024]{2,1,0:T(8,128)(2,1)}), bf16[16,64,1024]{2,1,0:T(8,128)(2,1)}, u32[]{:S(2)}, u32[]{:S(2)}) async-start(bf16[16,64,1024]{2,1,0:T(8,128)(2,1)} %get-tuple-element.14), calls=%async_computation.2 | async-start | bytes 4194304 | tf_op jit(solution)/shard_map/all_to_all | solution.py:277
  202.5 0.9 pad_bitcast_fusion
  203.3 2.0 fusion.17
  205.3 1.4 fusion.18
  206.7 1.2 divide_convert_fusion.2
  208.6 1.3 collective-permute-start.4
  209.9 1.3 collective-permute-start.5
  211.2 1.3 collective-permute-start.6
  212.6 1.8 copy.18.refs_4_
  215.1 1.8 concatenate.27.refs_5_
  217.0 1.2 fusion.14
  218.1 13.6 %collective-permute-done.4 = bf16[1032,128]{1,0:T(8,128)(2,1)} collective-permute-done((bf16[1032,128]{1,0:T(8,128)(2,1)}, bf16[1032,128]{1,0:T(8,128)(2,1)}, u32[]{:S(2)}, u32[]{:S(2)}) %collective-permute-start.4) | collective-permute-done | bytes 264224 | tf_op jit(solution)/shard_map/ppermute | solution.py:22
  231.7 1.1 collective-permute-done.5
  232.8 5.5 %collective-permute-done.6 = bf16[1032,128]{1,0:T(8,128)(2,1)} collective-permute-done((bf16[1032,128]{1,0:T(8,128)(2,1)}, bf16[1032,128]{1,0:T(8,128)(2,1)}, u32[]{:S(2)}, u32[]{:S(2)}) %collective-permute-start.6) | collective-permute-done | bytes 264224 | tf_op jit(solution)/shard_map/ppermute | solution.py:22
  238.3 1.2 add_subtract_fusion
  240.2 0.8 sub.58.refs_8_
  242.5 26.0 %shard_map.64 = (bf16[2048,1024]{1,0:T(8,128)(2,1)}, f32[8,128,128]{2,1,0:T(8,128)}, f32[8,8,128]{2,1,0:T(8,128)}) custom-call(bf16[8,128,1024]{2,1,0:T(8,128)(2,1)} %bitcast.65, bf16[8,2048,128]{2,1,0:T(8,128)(2,1)} %copy.17.refs_1_, bf16[8,128,2048]{2,1,0:T(8,128)(2,1)} %bitcast.4.refs_2_, bf16[8,2048,128]{2,1,0:T(8,128)(2,1)} %copy-done.2, ...), custom_call_target="tpu_custom_call" | custom-call | tf_op jit(solution)/shard_map/pallas_call | solution.py:195
  268.5 25.8 %shard_map.65 = bf16[2048,1024]{1,0:T(8,128)(2,1)} custom-call(bf16[8,128,1024]{2,1,0:T(8,128)(2,1)} %bitcast.9.refs_0_, bf16[8,2048,128]{2,1,0:T(8,128)(2,1)} %copy.17.refs_1_, bf16[8,128,2048]{2,1,0:T(8,128)(2,1)} %bitcast.4.refs_2_, bf16[8,2048,128]{2,1,0:T(8,128)(2,1)} %copy-done.2, ...), custom_call_target="tpu_custom_call", output_to_operand_aliasing={{}: (12, {})} | custom-call | tf_op jit(solution)/shard_map/pallas_call | solution.py:195
  (39 shorter events, 6.4 us)
Async XLA Ops:
  0.0 86.2 %copy-start = (bf16[8,128,64]{1,2,0:T(8,128)(2,1)S(1)}, bf16[8,128,64]{1,2,0:T(8,128)(2,1)}, u32[]{:S(2)}) copy-start(bf16[8,128,64]{1,2,0:T(8,128)(2,1)} %param.10) | copy-start | bytes 393220
  4.8 64.3 %all-to-all-start.1 = ((bf16[64,16,2048]{2,0,1:T(8,128)(2,1)}), bf16[64,16,2048]{2,0,1:T(8,128)(2,1)}, u32[]{:S(2)}, u32[]{:S(2)}) async-start(bf16[64,16,2048]{2,0,1:T(8,128)(2,1)} %bitcast.61), calls=%async_computation.1 | async-start | bytes 8388608 | tf_op jit(solution)/shard_map/all_to_all | solution.py:26
  19.5 6.6 %copy-start.5 = (bf16[64,32768]{1,0:T(8,128)(2,1)S(1)}, bf16[64,32768]{1,0:T(8,128)(2,1)}, u32[]{:S(2)}) copy-start(bf16[64,32768]{1,0:T(8,128)(2,1)} %param.8) | copy-start | bytes 12582916
  69.1 10.8 %copy-start.7 = (bf16[8,128,64]{1,2,0:T(8,128)(2,1)S(1)}, bf16[8,128,64]{1,2,0:T(8,128)(2,1)}, u32[]{:S(2)}) copy-start(bf16[8,128,64]{1,2,0:T(8,128)(2,1)} %param.9) | copy-start | bytes 393220
  69.1 11.6 %copy-start.10 = (f32[8]{0:T(128)S(1)}, f32[8]{0:T(128)}, u32[]{:S(2)}) copy-start(f32[8]{0:T(128)} %param.11) | copy-start | bytes 100
  69.1 65.4 %all-to-all-start = ((bf16[64,16,2048]{2,0,1:T(8,128)(2,1)}), bf16[64,16,2048]{2,0,1:T(8,128)(2,1)}, u32[]{:S(2)}, u32[]{:S(2)}) async-start(bf16[64,16,2048]{2,0,1:T(8,128)(2,1)} %bitcast.59), calls=%async_computation | async-start | bytes 8388608 | tf_op jit(solution)/shard_map/all_to_all | solution.py:26
  99.0 7.4 %copy-start.1 = (f32[8,2048,64]{2,1,0:T(8,128)S(1)}, f32[8,2048,64]{2,1,0:T(8,128)}, u32[]{:S(2)}) copy-start(f32[8,2048,64]{2,1,0:T(8,128)} %copy.11) | copy-start | bytes 12582916
  134.4 56.8 %all-to-all-start.3 = ((bf16[16,64,1024]{2,1,0:T(8,128)(2,1)}), bf16[16,64,1024]{2,1,0:T(8,128)(2,1)S(1)}, u32[]{:S(2)}, u32[]{:S(2)}) async-start(bf16[16,64,1024]{2,1,0:T(8,128)(2,1)} %get-tuple-element.23), calls=%async_computation.3 | async-start | bytes 4194304 | tf_op jit(solution)/shard_map/all_to_all | solution.py:248
  146.5 32.4 %collective-permute-start.3 = (bf16[2,8,128,64]{3,2,1,0:T(8,128)(2,1)}, bf16[2,8,128,64]{3,2,1,0:T(8,128)(2,1)S(1)}, u32[]{:S(2)}, u32[]{:S(2)}) collective-permute-start(bf16[2,8,128,64]{3,2,1,0:T(8,128)(2,1)} %pad_maximum_fusion.2), channel_id=1, source_target_pairs={{0,1},{1,2},{2,3},{3,4},{4,5},{5,6},{6,7},{7,8},{8,9},{9,10},{10,1... | collective-permute-start | bytes 786440 | tf_op jit(solution)/shard_map/ppermute | solution.py:22
  149.6 5.5 %copy-start.3 = (bf16[8,2048,64]{2,1,0:T(8,128)(2,1)S(1)}, bf16[8,2048,64]{2,1,0:T(8,128)(2,1)}, u32[]{:S(2)}) copy-start(bf16[8,2048,64]{2,1,0:T(8,128)(2,1)} %divide_convert_fusion.1) | copy-start | bytes 6291460
  157.7 5.0 %copy-start.2 = (bf16[8,2048,128]{2,1,0:T(8,128)(2,1)}, bf16[8,2048,128]{2,1,0:T(8,128)(2,1)S(1)}, u32[]{:S(2)}) copy-start(bf16[8,2048,128]{2,1,0:T(8,128)(2,1)S(1)} %get-tuple-element.22.refs_3_) | copy-start | bytes 12582916
  163.5 26.5 %collective-permute-start = (bf16[1032,128]{1,0:T(8,128)(2,1)}, bf16[1032,128]{1,0:T(8,128)(2,1)}, u32[]{:S(2)}, u32[]{:S(2)}) collective-permute-start(bf16[1032,128]{1,0:T(8,128)(2,1)} %fusion.11), channel_id=1, source_target_pairs={{0,1},{1,2},{2,3},{3,4},{4,5},{5,6},{6,7},{7,8},{8,9},{9,10},{10,1... | collective-permute-start | bytes 792584 | tf_op jit(solution)/shard_map/ppermute | solution.py:22
  165.6 24.4 %collective-permute-start.1 = (bf16[1032,128]{1,0:T(8,128)(2,1)}, bf16[1032,128]{1,0:T(8,128)(2,1)}, u32[]{:S(2)}, u32[]{:S(2)}) collective-permute-start(bf16[1032,128]{1,0:T(8,128)(2,1)} %fusion.11), channel_id=1, source_target_pairs={{0,2},{1,3},{2,4},{3,5},{4,6},{5,7},{6,8},{7,9},{8,10},{9,11},{10,... | collective-permute-start | bytes 792584 | tf_op jit(solution)/shard_map/ppermute | solution.py:22
  166.9 23.1 %collective-permute-start.2 = (bf16[1032,128]{1,0:T(8,128)(2,1)}, bf16[1032,128]{1,0:T(8,128)(2,1)}, u32[]{:S(2)}, u32[]{:S(2)}) collective-permute-start(bf16[1032,128]{1,0:T(8,128)(2,1)} %fusion.11), channel_id=1, source_target_pairs={{0,3},{1,4},{2,5},{3,6},{4,7},{5,8},{6,9},{7,10},{8,11},{9,12},{10... | collective-permute-start | bytes 792584 | tf_op jit(solution)/shard_map/ppermute | solution.py:22
  178.9 11.1 %copy-start.6 = (bf16[2,8,128,64]{3,2,1,0:T(8,128)(2,1)}, bf16[2,8,128,64]{3,2,1,0:T(8,128)(2,1)S(1)}, u32[]{:S(2)}) copy-start(bf16[2,8,128,64]{3,2,1,0:T(8,128)(2,1)S(1)} %collective-permute-done.3) | copy-start | bytes 786436
  191.2 23.2 %copy-start.4 = (bf16[16,64,1024]{2,1,0:T(8,128)(2,1)}, bf16[16,64,1024]{2,1,0:T(8,128)(2,1)S(1)}, u32[]{:S(2)}) copy-start(bf16[16,64,1024]{2,1,0:T(8,128)(2,1)S(1)} %all-to-all-done.3) | copy-start | bytes 6291460
  191.2 77.3 %all-to-all-start.2 = ((bf16[16,64,1024]{2,1,0:T(8,128)(2,1)}), bf16[16,64,1024]{2,1,0:T(8,128)(2,1)}, u32[]{:S(2)}, u32[]{:S(2)}) async-start(bf16[16,64,1024]{2,1,0:T(8,128)(2,1)} %get-tuple-element.14), calls=%async_computation.2 | async-start | bytes 4194304 | tf_op jit(solution)/shard_map/all_to_all | solution.py:277
  207.8 33.2 %copy-start.8 = (f32[256]{0:T(256)S(1)}, f32[256]{0:T(256)}, u32[]{:S(2)}) copy-start(f32[256]{0:T(256)} %and_select_fusion) | copy-start | bytes 3076
  207.9 34.0 %copy-start.9 = (f32[8]{0:T(128)S(1)}, f32[8]{0:T(128)}, u32[]{:S(2)}) copy-start(f32[8]{0:T(128)} %add_divide_fusion) | copy-start | bytes 100
  208.6 23.1 %collective-permute-start.4 = (bf16[1032,128]{1,0:T(8,128)(2,1)}, bf16[1032,128]{1,0:T(8,128)(2,1)}, u32[]{:S(2)}, u32[]{:S(2)}) collective-permute-start(bf16[1032,128]{1,0:T(8,128)(2,1)} %convert_element_type.44), channel_id=1, source_target_pairs={{0,4},{1,5},{2,6},{3,7},{4,8},{5,9},{6,10},{7,11},{8,12},{9,13},{1... | collective-permute-start | bytes 792584 | tf_op jit(solution)/shard_map/ppermute | solution.py:22
  209.9 22.9 %collective-permute-start.5 = (bf16[1032,128]{1,0:T(8,128)(2,1)}, bf16[1032,128]{1,0:T(8,128)(2,1)}, u32[]{:S(2)}, u32[]{:S(2)}) collective-permute-start(bf16[1032,128]{1,0:T(8,128)(2,1)} %convert_element_type.44), channel_id=1, source_target_pairs={{0,8},{1,9},{2,10},{3,11},{4,12},{5,13},{6,14},{7,15},{16,24},{17,... | collective-permute-start | bytes 792584 | tf_op jit(solution)/shard_map/ppermute | solution.py:22
  211.2 27.1 %collective-permute-start.6 = (bf16[1032,128]{1,0:T(8,128)(2,1)}, bf16[1032,128]{1,0:T(8,128)(2,1)}, u32[]{:S(2)}, u32[]{:S(2)}) collective-permute-start(bf16[1032,128]{1,0:T(8,128)(2,1)} %convert_element_type.44), channel_id=1, source_target_pairs={{0,12},{1,13},{2,14},{3,15},{16,28},{17,29},{18,30},{19,31},{32,44... | collective-permute-start | bytes 792584 | tf_op jit(solution)/shard_map/ppermute | solution.py:22

commit v13 on v11

--- a/solution.py
+++ b/solution.py
@@ -203,7 +203,7 @@
     )(*args)
 
 
-def local_part(q_parts, k, v, before, earlier, feat_q, feat_k, prior_state, prior_norm, gate):
+def local_part(q_parts, k, k_tm, v, before, earlier, feat_q, feat_k, prior_state, prior_norm, gate):
     group, head_dim, length = k.shape
     keep = earlier.astype(jnp.bfloat16)
     phi_k = feature_map(k, feat_k)
@@ -224,7 +224,6 @@
     halo_rows = (jnp.arange(2 * QB) >= QB - WIN) & (jnp.arange(2 * QB) < QB)
     bias0 = jnp.where(halo_rows & jnp.logical_not(earlier), jnp.float32(-1e30), jnp.float32(0.0))
     bias0 = jnp.broadcast_to(bias0[:, None], (2 * QB, QB))
-    k_tm = k.transpose(0, 2, 1)
     span = q_parts[0].shape[2]
     out, st, z = attend(q_parts[0], 0, k_tm, v, phi_k, kh, vh, pkh, fq_t, st, z, gate_rows, bias0, None)
     for c in range(1, len(q_parts)):
@@ -256,6 +255,7 @@
     before = passed_along(tails, "seq", 1)
 
     phi_own = feature_map(k, feat_k)
+    k_tm, phi_own = lax.optimization_barrier((k.transpose(0, 2, 1), phi_own))
     own_state = jnp.einsum("htf,hdt->hdf", phi_own, v, preferred_element_type=jnp.float32)
     own_norm = jnp.sum(phi_own, axis=1, dtype=jnp.float32)
     own = jnp.concatenate([own_state.reshape(group * head_dim, -1), own_norm], axis=0)
@@ -273,7 +273,7 @@
     prior_state = prior[: group * head_dim].reshape(own_state.shape)
     prior_norm = prior[group * head_dim :]
     gate = jax.nn.sigmoid(mix)
-    return local_part(q_parts, k, v, before, earlier, feat_q, feat_k, prior_state, prior_norm, gate)
+    return local_part(q_parts, k, k_tm, v, before, earlier, feat_q, feat_k, prior_state, prior_norm, gate)
 
 
 def solution(mesh):

time: 288 us -> 290 us (level)
  other arithmetic: 36.6 us -> 41 us
  waiting for transfers between devices: 77.5 us -> 73.9 us
  starting transfers between devices: 53.4 us -> 56.8 us
    div x0 -> x1, other arithmetic: none -> 12.3 us  [feature_map(): halves = [jax.nn.softmax(logits, axis=-1), jax.nn.softmax(-logits, axis=-1)]]
    all_to_all x2, waiting for transfers between devices: 56.2 us -> 44.3 us  [exchange(): moved = lax.all_to_all(rows, 'seq', split_axis=1, concat_axis=0, tiled=True)]
    ppermute x7, waiting for transfers between devices: 21.3 us -> 29.7 us  [passed_along(): return lax.ppermute(block, axis, route)]
    transpose x1 -> x0, local copies, waits for them, and re-layouts: 6.52 us -> none  [local_part(): k_tm = k.transpose(0, 2, 1)]
    optimization_barrier x0 -> x1, local copies, waits for them, and re-layouts: none -> 6.51 us  [body(): k_tm, phi_own = lax.optimization_barrier((k.transpose(0, 2, 1), phi_own))]
    sub x1 -> x0, other arithmetic: 5.47 us -> none  [feature_map(): halves = [jax.nn.softmax(logits, axis=-1), jax.nn.softmax(-logits, axis=-1)]]
    concatenate x0 -> x1, other arithmetic: none -> 3.65 us  [feature_map(): return jnp.concatenate(halves, axis=-1).astype(jnp.bfloat16)]
    another operation x3 -> x2, other arithmetic: 13.1 us -> 9.66 us
  transfers between devices with their start and end apart: 11 -> 11, of which waited for: 6 -> 6; matrix products, arithmetic and copies ran while one was open for 34% -> 35% of each run, Pallas kernels for 9% -> 9%
where the time goes in v13:
time: 290 us; the launch traced here: 287 us
  waiting for transfers between devices  73.9 us (25%)
  starting transfers between devices  56.8 us (20%)
  Pallas kernels  51.8 us (18%)
  local copies, waits for them, and re-layouts  51 us (18%)
  other arithmetic  41 us (14%)
  matrix products  11.9 us (4%)
    pallas_call x2, Pallas kernels, attend(): pl.pallas_call(make_kernel(t_begin, span // QB), grid=(group // hb,), in_...  51.8 us
    all_to_all x2, waiting for transfers between devices, exchange(): moved = lax.all_to_all(rows, 'seq', split_axis=1, concat_axis=0, tiled=True)  44.3 us
    ppermute x7, waiting for transfers between devices, passed_along(): return lax.ppermute(block, axis, route)  29.7 us
    all_to_all x2, starting transfers between devices, body(): lax.all_to_all(halves[c], 'seq', split_axis=0, concat_axis=0, tiled=True)  27 us
    all_to_all x2, starting transfers between devices, exchange(): moved = lax.all_to_all(rows, 'seq', split_axis=1, concat_axis=0, tiled=True)  17.7 us
    reshape x2, local copies, waits for them, and re-layouts, body(): queries.reshape(feature_rows, shards, Q_PIECES, length // Q_PIECES)  14.4 us
    div x1, other arithmetic, feature_map(): halves = [jax.nn.softmax(logits, axis=-1), jax.nn.softmax(-logits, axis=-1)]  12.3 us
    ppermute x7, starting transfers between devices, passed_along(): return lax.ppermute(block, axis, route)  12 us
  transfers between devices with their start and end apart: 11, of which 6 were waited for; matrix products, arithmetic and copies ran while one was open for 35% of the time, Pallas kernels for 9%

profile of v13, /device:TPU:116, one launch (start us, length us, event | category | flops | bytes accessed | tf_op | source)
XLA Modules:
  0.0 286.6 jit_solution(6262582030903103299)
XLA Ops:
  0.0 4.8 %copy.27 = bf16[8,16,8,2048]{3,2,0,1:T(8,128)(2,1)} copy(bf16[8,16,8,2048]{3,2,1,0:T(8,128)(2,1)} %bitcast.66) | data formatting | bytes 8388608 | tf_op jit(solution)/shard_map/reshape | solution.py:244
  4.8 6.9 %all-to-all-start.1 = ((bf16[64,16,2048]{2,0,1:T(8,128)(2,1)}), bf16[64,16,2048]{2,0,1:T(8,128)(2,1)}, u32[]{:S(2)}, u32[]{:S(2)}) async-start(bf16[64,16,2048]{2,0,1:T(8,128)(2,1)} %bitcast.61), calls=%async_computation.1 | async-start | bytes 8388608 | tf_op jit(solution)/shard_map/all_to_all | solution.py:26
  11.7 7.8 %reshape.51 = bf16[64,16,2,1024]{3,2,1,0:T(2,128)(2,1)} reshape(bf16[64,32768]{1,0:T(8,128)(2,1)} %param.6) | data formatting | bytes 8388608 | tf_op jit(solution)/shard_map/reshape | solution.py:242
  19.5 6.6 %copy.28 = bf16[64,16,2,1024]{3,0,1,2:T(8,128)(2,1)} copy(bf16[64,16,2,1024]{3,2,1,0:T(2,128)(2,1)} %reshape.51) | data formatting | bytes 8388608 | tf_op jit(solution)/shard_map/reshape | solution.py:242
  26.1 2.3 copy.26
  29.0 40.1 %all-to-all-done.1 = bf16[64,16,2048]{2,0,1:T(8,128)(2,1)} async-done(((bf16[64,16,2048]{2,0,1:T(8,128)(2,1)}), bf16[64,16,2048]{2,0,1:T(8,128)(2,1)}, u32[]{:S(2)}, u32[]{:S(2)}) %all-to-all-start.1) | async-done | bytes 4194336 | tf_op jit(solution)/shard_map/all_to_all | solution.py:26
  69.1 10.8 %all-to-all-start.2 = ((bf16[64,16,2048]{2,0,1:T(8,128)(2,1)}), bf16[64,16,2048]{2,0,1:T(8,128)(2,1)}, u32[]{:S(2)}, u32[]{:S(2)}) async-start(bf16[64,16,2048]{2,0,1:T(8,128)(2,1)} %bitcast.59), calls=%async_computation.2 | async-start | bytes 8388608 | tf_op jit(solution)/shard_map/all_to_all | solution.py:26
  80.5 0.7 maximum_bitcast_fusion.refs_7_
  81.2 4.9 %slice_bitcast_fusion = (bf16[16,64,1024]{2,1,0:T(8,128)(2,1)}, bf16[16,64,1024]{2,1,0:T(8,128)(2,1)}) fusion(bf16[2,16,64,1024]{3,2,1,0:T(8,128)(2,1)} %bitcast.60), kind=kLoop, calls=%fused_computation.16 | loop fusion | bytes 8388608 | tf_op jit(solution)/shard_map/squeeze | solution.py:247
  86.1 4.9 %fusion.20 = (f32[8,2048]{1,0:T(8,128)S(1)}, f32[8,2048,64]{1,2,0:T(8,128)}) fusion(bf16[8,128,64]{1,2,0:T(8,128)(2,1)S(1)} %copy-done, bf16[8,128,2048]{2,1,0:T(8,128)(2,1)} %bitcast.5), kind=kOutput, calls=%fused_computation.46 | convolution fusion | flops 269467648 | bytes 8585216 | tf_op jit(solution)/shard_map/hdt,hdf->htf/dot_general | solution.py:31
  91.0 6.9 %copy.10 = f32[8,2048,64]{2,1,0:T(8,128)} copy(f32[8,2048,64]{1,2,0:T(8,128)} %get-tuple-element.26) | data formatting | bytes 8388608 | tf_op jit(solution)/shard_map/hdt,hdf->htf/dot_general | solution.py:31
  97.9 1.1 slice_bitcast_fusion.5
  99.0 6.8 %fusion.3 = f32[8,2048]{1,0:T(8,128)S(1)} fusion(f32[8,2048,64]{2,1,0:T(8,128)} %copy.10, f32[8,2048]{1,0:T(8,128)S(1)} %get-tuple-element.25), kind=kLoop, calls=%fused_computation.8 | loop fusion | flops 2080768 | bytes 4325376 | tf_op jit(solution)/shard_map/reduce_sum | solution.py:32
  105.8 12.3 %divide_convert_fusion = bf16[8,2048,64]{2,1,0:T(8,128)(2,1)} fusion(f32[8,2048,64]{2,1,0:T(8,128)} %copy.10), kind=kOutput, calls=%fused_computation.4 | output fusion | flops 5275774 | bytes 6291456 | tf_op jit(solution)/shard_map/div | solution.py:32
  118.1 8.4 %divide_convert_fusion.1 = bf16[8,2048,64]{2,1,0:T(8,128)(2,1)S(1)} fusion(f32[8,2048,64]{2,1,0:T(8,128)} %copy.10, f32[8,2048]{1,0:T(8,128)S(1)} %fusion.3, f32[8,2048]{1,0:T(8,128)S(1)} %get-tuple-element.25), kind=kLoop, calls=%fused_computation.6 | loop fusion | flops 3145728 | bytes 6422528 | tf_op jit(solution)/shard_map/convert.2
  126.6 3.6 %pad_maximum_fusion.refs_3_ = bf16[8,2048,128]{2,1,0:T(8,128)(2,1)} fusion(bf16[8,2048,64]{2,1,0:T(8,128)(2,1)S(1)} %copy-done.3, bf16[8,2048,64]{2,1,0:T(8,128)(2,1)S(1)} %divide_convert_fusion.1), kind=kLoop, calls=%fused_computation.13 | loop fusion | flops 8388608 | bytes 8388608 | tf_op jit(solution)/shard_map/concatenate | solution.py:33
  130.2 4.2 %all-to-all-done.2 = bf16[64,16,2048]{2,0,1:T(8,128)(2,1)} async-done(((bf16[64,16,2048]{2,0,1:T(8,128)(2,1)}), bf16[64,16,2048]{2,0,1:T(8,128)(2,1)}, u32[]{:S(2)}, u32[]{:S(2)}) %all-to-all-start.2) | async-done | bytes 4194336 | tf_op jit(solution)/shard_map/all_to_all | solution.py:26
  134.4 10.1 %all-to-all-start.3 = ((bf16[16,64,1024]{2,1,0:T(8,128)(2,1)}), bf16[16,64,1024]{2,1,0:T(8,128)(2,1)S(1)}, u32[]{:S(2)}, u32[]{:S(2)}) async-start(bf16[16,64,1024]{2,1,0:T(8,128)(2,1)} %get-tuple-element.21), calls=%async_computation.3 | async-start | bytes 4194304 | tf_op jit(solution)/shard_map/all_to_all | solution.py:247
  144.5 1.1 slice_bitcast_fusion.4
  145.6 0.9 pad_maximum_fusion.2
  146.5 3.5 %collective-permute-start = (bf16[2,8,128,64]{3,2,1,0:T(8,128)(2,1)}, bf16[2,8,128,64]{3,2,1,0:T(8,128)(2,1)S(1)}, u32[]{:S(2)}, u32[]{:S(2)}) collective-permute-start(bf16[2,8,128,64]{3,2,1,0:T(8,128)(2,1)} %pad_maximum_fusion.2), channel_id=1, source_target_pairs={{0,1},{1,2},{2,3},{3,4},{4,5},{5,6},{6,7},{7,8},{8,9},{9,10},{10,1... | collective-permute-start | bytes 786440 | tf_op jit(solution)/shard_map/ppermute | solution.py:22
  150.1 4.7 %fusion.23 = f32[8,128,128]{2,1,0:T(8,128)S(1)} fusion(bf16[8,128,2048]{2,1,0:T(8,128)(2,1)} %bitcast.11.refs_2_, bf16[8,2048,128]{2,1,0:T(8,128)(2,1)} %pad_maximum_fusion.refs_3_), kind=kOutput, calls=%fused_computation.49 | convolution fusion | flops 536870912 | bytes 8912896 | tf_op jit(solution)/shard_map/htf,hdt->hdf/dot_general | solution.py:259
  156.1 1.9 collective-permute-start.1
  158.0 1.3 collective-permute-start.2
  159.3 1.3 collective-permute-start.3
  160.6 6.5 %copy.17.refs_1_ = bf16[8,2048,128]{2,1,0:T(8,128)(2,1)} copy(bf16[8,2048,128]{1,2,0:T(8,128)(2,1)} %bitcast.6) | data formatting | bytes 8388608 | tf_op jit(solution)/shard_map/optimization_barrier | solution.py:258
  167.1 11.8 %collective-permute-done = bf16[2,8,128,64]{3,2,1,0:T(8,128)(2,1)S(1)} collective-permute-done((bf16[2,8,128,64]{3,2,1,0:T(8,128)(2,1)}, bf16[2,8,128,64]{3,2,1,0:T(8,128)(2,1)S(1)}, u32[]{:S(2)}, u32[]{:S(2)}) %collective-permute-start) | collective-permute-done | bytes 262176 | tf_op jit(solution)/shard_map/ppermute | solution.py:22
  178.9 1.0 fusion.21
  180.0 1.0 fusion.22
  181.0 0.8 slice_bitcast_fusion.2
  181.8 16.9 %all-to-all-start = ((bf16[16,64,1024]{2,1,0:T(8,128)(2,1)}), bf16[16,64,1024]{2,1,0:T(8,128)(2,1)}, u32[]{:S(2)}, u32[]{:S(2)}) async-start(bf16[16,64,1024]{2,1,0:T(8,128)(2,1)} %get-tuple-element.22), calls=%async_computation | async-start | bytes 4194304 | tf_op jit(solution)/shard_map/all_to_all | solution.py:247
  198.7 1.8 pad_bitcast_fusion
  200.5 1.2 divide_convert_fusion.2
  201.8 1.9 fusion.16
  203.8 1.4 collective-permute-start.4
  205.2 1.3 collective-permute-start.5
  206.5 1.3 collective-permute-start.6
  207.9 1.8 copy.18.refs_4_
  209.7 0.7 concatenate.28.refs_6_
  210.5 1.8 concatenate.26.refs_5_
  212.5 12.3 %collective-permute-done.4 = bf16[1032,128]{1,0:T(8,128)(2,1)} collective-permute-done((bf16[1032,128]{1,0:T(8,128)(2,1)}, bf16[1032,128]{1,0:T(8,128)(2,1)}, u32[]{:S(2)}, u32[]{:S(2)}) %collective-permute-start.4) | collective-permute-done | bytes 264224 | tf_op jit(solution)/shard_map/ppermute | solution.py:22
  224.8 0.8 collective-permute-done.5
  225.6 4.7 %collective-permute-done.6 = bf16[1032,128]{1,0:T(8,128)(2,1)} collective-permute-done((bf16[1032,128]{1,0:T(8,128)(2,1)}, bf16[1032,128]{1,0:T(8,128)(2,1)}, u32[]{:S(2)}, u32[]{:S(2)}) %collective-permute-start.6) | collective-permute-done | bytes 264224 | tf_op jit(solution)/shard_map/ppermute | solution.py:22
  230.3 1.6 add_subtract_fusion
  232.6 0.8 sub.58.refs_8_
  233.4 0.8 broadcast_in_dim.16.refs_11_
  234.8 26.0 %shard_map.64 = (bf16[2048,1024]{1,0:T(8,128)(2,1)}, f32[8,128,128]{2,1,0:T(8,128)}, f32[8,8,128]{2,1,0:T(8,128)}) custom-call(bf16[8,128,1024]{2,1,0:T(8,128)(2,1)} %bitcast.65, bf16[8,2048,128]{2,1,0:T(8,128)(2,1)} %copy.17.refs_1_, bf16[8,128,2048]{2,1,0:T(8,128)(2,1)} %bitcast.11.refs_2_, bf16[8,2048,128]{2,1,0:T(8,128)(2,1)} %pad_maximum_fusion.refs_3_, ...), custom_call_target="tpu_custom_call" | custom-call | tf_op jit(solution)/shard_map/pallas_call | solution.py:195
  260.8 25.8 %shard_map.65 = bf16[2048,1024]{1,0:T(8,128)(2,1)} custom-call(bf16[8,128,1024]{2,1,0:T(8,128)(2,1)} %bitcast.2.refs_0_, bf16[8,2048,128]{2,1,0:T(8,128)(2,1)} %copy.17.refs_1_, bf16[8,128,2048]{2,1,0:T(8,128)(2,1)} %bitcast.11.refs_2_, bf16[8,2048,128]{2,1,0:T(8,128)(2,1)} %pad_maximum_fusion.refs_3_, ...), custom_call_target="tpu_custom_call", output_to_operand_aliasing={{}: (12, {})} | custom-call | tf_op jit(solution)/shard_map/pallas_call | solution.py:195
  (36 shorter events, 4.1 us)
Async XLA Ops:
  0.0 86.1 %copy-start = (bf16[8,128,64]{1,2,0:T(8,128)(2,1)S(1)}, bf16[8,128,64]{1,2,0:T(8,128)(2,1)}, u32[]{:S(2)}) copy-start(bf16[8,128,64]{1,2,0:T(8,128)(2,1)} %param.10) | copy-start | bytes 393220
  4.8 64.3 %all-to-all-start.1 = ((bf16[64,16,2048]{2,0,1:T(8,128)(2,1)}), bf16[64,16,2048]{2,0,1:T(8,128)(2,1)}, u32[]{:S(2)}, u32[]{:S(2)}) async-start(bf16[64,16,2048]{2,0,1:T(8,128)(2,1)} %bitcast.61), calls=%async_computation.1 | async-start | bytes 8388608 | tf_op jit(solution)/shard_map/all_to_all | solution.py:26
  19.5 6.6 %copy-start.4 = (bf16[64,32768]{1,0:T(8,128)(2,1)S(1)}, bf16[64,32768]{1,0:T(8,128)(2,1)}, u32[]{:S(2)}) copy-start(bf16[64,32768]{1,0:T(8,128)(2,1)} %param.8) | copy-start | bytes 12582916
  26.1 2.3 copy-start.9
  69.0 11.4 %copy-start.6 = (bf16[8,128,64]{1,2,0:T(8,128)(2,1)S(1)}, bf16[8,128,64]{1,2,0:T(8,128)(2,1)}, u32[]{:S(2)}) copy-start(bf16[8,128,64]{1,2,0:T(8,128)(2,1)} %param.9) | copy-start | bytes 393220
  69.1 65.4 %all-to-all-start.2 = ((bf16[64,16,2048]{2,0,1:T(8,128)(2,1)}), bf16[64,16,2048]{2,0,1:T(8,128)(2,1)}, u32[]{:S(2)}, u32[]{:S(2)}) async-start(bf16[64,16,2048]{2,0,1:T(8,128)(2,1)} %bitcast.59), calls=%async_computation.2 | async-start | bytes 8388608 | tf_op jit(solution)/shard_map/all_to_all | solution.py:26
  118.1 8.4 %copy-start.3 = (bf16[8,2048,64]{2,1,0:T(8,128)(2,1)S(1)}, bf16[8,2048,64]{2,1,0:T(8,128)(2,1)}, u32[]{:S(2)}) copy-start(bf16[8,2048,64]{2,1,0:T(8,128)(2,1)} %divide_convert_fusion) | copy-start | bytes 6291460
  134.4 47.4 %all-to-all-start.3 = ((bf16[16,64,1024]{2,1,0:T(8,128)(2,1)}), bf16[16,64,1024]{2,1,0:T(8,128)(2,1)S(1)}, u32[]{:S(2)}, u32[]{:S(2)}) async-start(bf16[16,64,1024]{2,1,0:T(8,128)(2,1)} %get-tuple-element.21), calls=%async_computation.3 | async-start | bytes 4194304 | tf_op jit(solution)/shard_map/all_to_all | solution.py:247
  146.5 8.3 %copy-start.1 = (bf16[8,2048,128]{2,1,0:T(8,128)(2,1)S(1)}, bf16[8,2048,128]{2,1,0:T(8,128)(2,1)}, u32[]{:S(2)}) copy-start(bf16[8,2048,128]{2,1,0:T(8,128)(2,1)} %pad_maximum_fusion.refs_3_) | copy-start | bytes 12582916
  146.5 32.4 %collective-permute-start = (bf16[2,8,128,64]{3,2,1,0:T(8,128)(2,1)}, bf16[2,8,128,64]{3,2,1,0:T(8,128)(2,1)S(1)}, u32[]{:S(2)}, u32[]{:S(2)}) collective-permute-start(bf16[2,8,128,64]{3,2,1,0:T(8,128)(2,1)} %pad_maximum_fusion.2), channel_id=1, source_target_pairs={{0,1},{1,2},{2,3},{3,4},{4,5},{5,6},{6,7},{7,8},{8,9},{9,10},{10,1... | collective-permute-start | bytes 786440 | tf_op jit(solution)/shard_map/ppermute | solution.py:22
  156.1 45.7 %collective-permute-start.1 = (bf16[1032,128]{1,0:T(8,128)(2,1)}, bf16[1032,128]{1,0:T(8,128)(2,1)S(1)}, u32[]{:S(2)}, u32[]{:S(2)}) collective-permute-start(bf16[1032,128]{1,0:T(8,128)(2,1)} %fusion.12), channel_id=1, source_target_pairs={{0,1},{1,2},{2,3},{3,4},{4,5},{5,6},{6,7},{7,8},{8,9},{9,10},{10,1... | collective-permute-start | bytes 792584 | tf_op jit(solution)/shard_map/ppermute | solution.py:22
  158.0 43.8 %collective-permute-start.2 = (bf16[1032,128]{1,0:T(8,128)(2,1)}, bf16[1032,128]{1,0:T(8,128)(2,1)}, u32[]{:S(2)}, u32[]{:S(2)}) collective-permute-start(bf16[1032,128]{1,0:T(8,128)(2,1)} %fusion.12), channel_id=1, source_target_pairs={{0,2},{1,3},{2,4},{3,5},{4,6},{5,7},{6,8},{7,9},{8,10},{9,11},{10,... | collective-permute-start | bytes 792584 | tf_op jit(solution)/shard_map/ppermute | solution.py:22
  159.3 42.5 %collective-permute-start.3 = (bf16[1032,128]{1,0:T(8,128)(2,1)}, bf16[1032,128]{1,0:T(8,128)(2,1)}, u32[]{:S(2)}, u32[]{:S(2)}) collective-permute-start(bf16[1032,128]{1,0:T(8,128)(2,1)} %fusion.12), channel_id=1, source_target_pairs={{0,3},{1,4},{2,5},{3,6},{4,7},{5,8},{6,9},{7,10},{8,11},{9,12},{10... | collective-permute-start | bytes 792584 | tf_op jit(solution)/shard_map/ppermute | solution.py:22
  181.8 28.6 %copy-start.2 = (bf16[16,64,1024]{2,1,0:T(8,128)(2,1)}, bf16[16,64,1024]{2,1,0:T(8,128)(2,1)S(1)}, u32[]{:S(2)}) copy-start(bf16[16,64,1024]{2,1,0:T(8,128)(2,1)S(1)} %all-to-all-done.3) | copy-start | bytes 6291460
  181.8 79.0 %all-to-all-start = ((bf16[16,64,1024]{2,1,0:T(8,128)(2,1)}), bf16[16,64,1024]{2,1,0:T(8,128)(2,1)}, u32[]{:S(2)}, u32[]{:S(2)}) async-start(bf16[16,64,1024]{2,1,0:T(8,128)(2,1)} %get-tuple-element.22), calls=%async_computation | async-start | bytes 4194304 | tf_op jit(solution)/shard_map/all_to_all | solution.py:247
  201.8 6.0 %copy-start.5 = (bf16[1032,128]{1,0:T(8,128)(2,1)}, bf16[1032,128]{1,0:T(8,128)(2,1)S(1)}, u32[]{:S(2)}) copy-start(bf16[1032,128]{1,0:T(8,128)(2,1)S(1)} %collective-permute-done.1) | copy-start | bytes 792580
  203.8 29.6 %copy-start.7 = (f32[256]{0:T(256)S(1)}, f32[256]{0:T(256)}, u32[]{:S(2)}) copy-start(f32[256]{0:T(256)} %and_select_fusion) | copy-start | bytes 3076
  203.8 30.4 %copy-start.8 = (f32[8]{0:T(128)S(1)}, f32[8]{0:T(128)}, u32[]{:S(2)}) copy-start(f32[8]{0:T(128)} %add_divide_fusion) | copy-start | bytes 100
  203.8 21.0 %collective-permute-start.4 = (bf16[1032,128]{1,0:T(8,128)(2,1)}, bf16[1032,128]{1,0:T(8,128)(2,1)}, u32[]{:S(2)}, u32[]{:S(2)}) collective-permute-start(bf16[1032,128]{1,0:T(8,128)(2,1)} %fusion.16), channel_id=1, source_target_pairs={{0,4},{1,5},{2,6},{3,7},{4,8},{5,9},{6,10},{7,11},{8,12},{9,13},{1... | collective-permute-start | bytes 792584 | tf_op jit(solution)/shard_map/ppermute | solution.py:22
  205.2 20.4 %collective-permute-start.5 = (bf16[1032,128]{1,0:T(8,128)(2,1)}, bf16[1032,128]{1,0:T(8,128)(2,1)}, u32[]{:S(2)}, u32[]{:S(2)}) collective-permute-start(bf16[1032,128]{1,0:T(8,128)(2,1)} %fusion.16), channel_id=1, source_target_pairs={{0,8},{1,9},{2,10},{3,11},{4,12},{5,13},{6,14},{7,15},{16,24},{17,... | collective-permute-start | bytes 792584 | tf_op jit(solution)/shard_map/ppermute | solution.py:22
  206.5 23.8 %collective-permute-start.6 = (bf16[1032,128]{1,0:T(8,128)(2,1)}, bf16[1032,128]{1,0:T(8,128)(2,1)}, u32[]{:S(2)}, u32[]{:S(2)}) collective-permute-start(bf16[1032,128]{1,0:T(8,128)(2,1)} %fusion.16), channel_id=1, source_target_pairs={{0,12},{1,13},{2,14},{3,15},{16,28},{17,29},{18,30},{19,31},{32,44... | collective-permute-start | bytes 792584 | tf_op jit(solution)/shard_map/ppermute | solution.py:22
